TPU v7x, 128 devices: a whole 4x4x4 slice. The times are simulated.
128 devices in a mesh: mass: 4 (over y), shard: 32 (over x, z, core).
Axes of the slice: x: 4, y: 4, z: 4, core: 2. Of those that a mesh axis runs over, the one named last changes fastest.
Arguments:
- queries: bfloat16 [2048, 8192], P(('mass', 'shard')), may hold values from -6 to 6
- library: bfloat16 [131072, 8192], P(('mass', 'shard')), may hold values from -0.0625 to 0.0625
- routes: int32 [2048, 1], P(('mass', 'shard')), may hold values from 0 to 3; in each aligned block of 16 rows (0 to 15, 16 to 31, ...) at most 8 rows name the same one
- offsets: int32 [2048], P(('mass', 'shard')), may hold values from -2048 to 2048
Outputs:
- best_scores: float32 [2048, 16], P(('mass', 'shard'))
Inputs may be any that keep to these rules, and one draw needn't show every extreme that they name: `routes`: in each device's aligned block of 16 queries at most 8 go to one mass group, and some group gets exactly 8 from some device.
All inputs are finite; a program needn't handle non-finite values.
Results may differ from a plain program's by a relative error of at most 0.00087.
Values may be sent and summed in bfloat16 or wider, within the bound.
No kernel may reach another device: no remote copies, remote signals or barrier semaphores. Data moves between devices by JAX's collectives and lax.ppermute only.
A program may use at most 128 MiB of HBM per device.

v0:
```python
import jax
import jax.numpy as jnp
from jax import lax
from jax.sharding import PartitionSpec as P

MAX_SHIFT = 2048
TOP_K = 16


def combined_all(value, axis, join):
    pieces = lax.all_gather(value, axis)
    head = pieces[0]
    tail = pieces[1:]
    subtotal, _ = lax.scan(lambda subtotal, piece: (join(subtotal, piece), None), head, tail)
    return subtotal


def shifted_spectra(queries, offsets):
    row_count = queries.shape[0]
    bin_count = queries.shape[1]
    margin = jnp.zeros((row_count, MAX_SHIFT), queries.dtype)
    current = jnp.concatenate([margin, queries, margin], axis=1)
    window_start = MAX_SHIFT - offsets
    bit_total = (2 * MAX_SHIFT).bit_length()
    for bit_number in range(bit_total):
        step_size = 1 << bit_number
        moved = jnp.concatenate(
            [current[:, step_size:], jnp.zeros((row_count, step_size), current.dtype)], axis=1
        )
        taken = window_start >> bit_number & 1 == 1
        current = jnp.where(taken[:, None], moved, current)
    shifted = current[:, :bin_count]
    combined = queries.astype(jnp.float32) + shifted.astype(jnp.float32)
    scale_factor = lax.rsqrt(jnp.mean(combined * combined, axis=1, keepdims=True) + 1e-06)
    return (combined * scale_factor).astype(jnp.bfloat16)


def block_ranks(dest_group):
    length = dest_group.shape[0]
    position_ids = jnp.arange(length, dtype=jnp.int32)
    earlier = (dest_group[:, None] == dest_group[None, :]) & (
        position_ids[:, None] > position_ids[None, :]
    )
    return jnp.sum(earlier.astype(jnp.int32), axis=1)


def keep_best(values):
    return lax.top_k(values, TOP_K)[0]


def combine_best(first_list, second_list):
    return keep_best(jnp.concatenate([first_list, second_list], axis=1))


def per_device(queries, library, routes, offsets):
    mass_count = lax.axis_size("mass")
    query_count = queries.shape[0]
    capacity = query_count // 2
    spectra = shifted_spectra(queries, offsets)
    dest_group = routes[:, 0]
    slot_index = dest_group * capacity + block_ranks(dest_group)
    selector = (
        jnp.arange(mass_count * capacity, dtype=jnp.int32)[:, None] == slot_index[None, :]
    ).astype(jnp.bfloat16)
    packed = jnp.dot(selector, spectra, preferred_element_type=jnp.float32).astype(jnp.bfloat16)
    arrived = lax.all_to_all(packed, "mass", split_axis=0, concat_axis=0, tiled=True)
    scores = lax.dot_general(
        lax.all_gather(arrived, "shard", axis=0, tiled=True),
        library,
        (((1,), (1,)), ((), ())),
        preferred_element_type=jnp.float32,
    )
    local_best = keep_best(scores)
    merged = combined_all(local_best, "shard", combine_best)
    own_best = lax.dynamic_slice_in_dim(
        merged, lax.axis_index("shard") * (mass_count * capacity), mass_count * capacity, 0
    )
    returned_best = lax.all_to_all(own_best, "mass", split_axis=0, concat_axis=0, tiled=True)
    slot_match = slot_index[:, None] == jnp.arange(mass_count * capacity, dtype=jnp.int32)[None, :]
    return jnp.sum(
        jnp.where(slot_match[:, :, None], returned_best[None, :, :], jnp.float32(0.0)), axis=1
    )


def solution(mesh):
    placed = (
        P(("mass", "shard"), None),
        P(("mass", "shard"), None),
        P(("mass", "shard"), None),
        P(("mass", "shard")),
    )
    return jax.shard_map(
        per_device,
        mesh=mesh,
        in_specs=placed,
        out_specs=P(("mass", "shard"), None),
        check_vma=False,
    )
```

profile of v0, /device:TPU:1, one launch (start us, length us, event | category | flops | bytes accessed | tf_op | source)
XLA Modules:
  0.0 458.3 jit_solution(13185339797025698650)
XLA Ops:
  6.6 1.0 pad_maximum_fusion.1
  8.4 1.1 pad_select_fusion.11
  13.6 13.5 %all_to_all.21 = bf16[4,8,8192]{2,1,0:T(8,128)(2,1)} all-to-all(bf16[4,8,8192]{2,1,0:T(8,128)(2,1)S(1)} %fusion), channel_id=1, replica_groups=mesh['mass'=4,'shard'=32] {'mass'}, dimensions={0} | all-to-all | bytes 1048576 | tf_op jit(solution)/shard_map/all_to_all | solution.py:66
  27.4 74.5 %all-gather.4.cloned.1.call-done = bf16[1024,8192]{1,0:T(8,128)(2,1)} async-done(((bf16[32,8192]{1,0:T(8,128)(2,1)}), bf16[1024,8192]{1,0:T(8,128)(2,1)}) %all-gather.4.cloned.1.call-update) | async-done | bytes 16777232 | tf_op jit(solution)/shard_map/all_gather | solution.py:68
  101.9 23.6 %fusion.5 = f32[1024,1024]{0,1:T(8,128)} fusion(bf16[1024,8192]{1,0:T(8,128)(2,1)} %all-gather.4.cloned.1.call-done, bf16[1024,8192]{1,0:T(8,128)(2,1)} %param.7), kind=kOutput, calls=%fused_computation.48 | convolution fusion | flops 17179869184 | bytes 37748736
  125.5 2.2 iota.24.clone
  127.7 145.0 %top_k.14 = (f32[1024,1024]{0,1:T(8,128)}, s32[1024,1024]{0,1:T(8,128)}) sort(f32[1024,1024]{0,1:T(8,128)} %fusion.5, s32[1024,1024]{0,1:T(8,128)} %iota.24.clone), dimensions={1}, to_apply=%region_2.3 | sort | flops 20971520 | bytes 16777216 | tf_op jit(solution)/shard_map/top_k | solution.py:48
  272.7 5.3 %copy.17 = f32[1024,1024]{1,0:T(8,128)} copy(f32[1024,1024]{0,1:T(8,128)} %get-tuple-element.37) | data formatting | bytes 8388608 | tf_op jit(solution)/shard_map/top_k | solution.py:48
  278.1 1.9 top_k.20
  280.0 72.2 %all-gather.6.cloned.1.call-done = f32[32768,16]{1,0:T(8,128)} async-done(((f32[1024,16]{1,0:T(8,128)}), f32[32768,16]{1,0:T(8,128)}) %all-gather.6.cloned.1.call-update) | async-done | bytes 2097168 | tf_op jit(solution)/shard_map/all_gather | solution.py:11
  352.2 1.1 slice.82
  353.4 11.1 %slice.83 = f32[31744,16]{1,0:T(8,128)} slice(f32[32768,16]{1,0:T(8,128)} %all-gather.6.cloned.1.call-done), slice={[1024:32768], [0:16]} | slice | bytes 4063232 | tf_op jit(solution)/shard_map/slice | solution.py:13
  364.6 9.4 %copy.12 = f32[31,1024,16]{1,2,0:T(8,128)S(1)} copy(f32[31,1024,16]{2,1,0:T(8,128)} %bitcast.21) | data formatting | bytes 4063232 | tf_op jit(solution)/shard_map/while | solution.py:14
  373.9 66.5 %while.10 = (s32[]{:T(128)}, f32[1024,16]{0,1:T(8,128)S(1)}, f32[31,1024,16]{1,2,0:T(8,128)S(1)}, s32[]{:T(128)}) while((s32[]{:T(128)}, f32[1024,16]{0,1:T(8,128)S(1)}, f32[31,1024,16]{1,2,0:T(8,128)S(1)}, s32[]{:T(128)}) %tuple.34), condition=%wide.region_5.6_spmd, body=%wide.region_3.5_spmd.sunk | while | flops 524290 | bytes 1179713 | solution.py:14
  374.0 2.1 top_k.23
  376.2 2.1 top_k.23
  378.3 2.1 top_k.23
  380.4 2.1 top_k.23
  382.6 2.1 top_k.23
  384.7 2.1 top_k.23
  386.9 2.1 top_k.23
  389.0 2.1 top_k.23
  391.2 2.1 top_k.23
  393.3 2.1 top_k.23
  395.5 2.1 top_k.23
  397.6 2.1 top_k.23
  399.8 2.1 top_k.23
  401.9 2.1 top_k.23
  404.1 2.1 top_k.23
  406.2 2.1 top_k.23
  408.3 2.1 top_k.23
  410.5 2.1 top_k.23
  412.6 2.1 top_k.23
  414.8 2.1 top_k.23
  416.9 2.1 top_k.23
  419.1 2.1 top_k.23
  421.2 2.1 top_k.23
  423.4 2.1 top_k.23
  425.5 2.1 top_k.23
  427.7 2.1 top_k.23
  429.8 2.1 top_k.23
  431.9 2.1 top_k.23
  434.1 2.1 top_k.23
  436.2 2.1 top_k.23
  438.4 2.1 top_k.23
  441.4 4.0 all-to-all-start.1
  445.4 4.0 all-to-all-done.1
  450.8 0.7 select_reduce_fusion
  (173 shorter events, 8.5 us)
Async XLA Ops:
  6.5 6.1 %copy-start = (bf16[16,8192]{1,0:T(8,128)(2,1)S(1)}, bf16[16,8192]{1,0:T(8,128)(2,1)}, u32[]{:S(2)}) copy-start(bf16[16,8192]{1,0:T(8,128)(2,1)} %param.6) | copy-start | bytes 786436
  6.5 6.5 %copy-start.1 = (s32[16,1]{0,1:T(1,128)S(1)}, s32[16,1]{0,1:T(1,128)}, u32[]{:S(2)}) copy-start(s32[16,1]{0,1:T(1,128)} %param.8) | copy-start | bytes 196
  6.5 95.3 %all-gather.4.cloned.1.call-start = ((), (), s32[]{:S(2)}) async-start(), calls=%async_computation.2 | async-start | bytes 17301504 | tf_op jit(solution)/shard_map/all_gather | solution.py:68
  27.1 325.0 %all-gather.6.cloned.1.call-start = ((), (), s32[]{:S(2)}) async-start(), calls=%async_computation.3 | async-start | bytes 17301504 | tf_op jit(solution)/shard_map/all_gather | solution.py:11
  441.4 8.1 %all-to-all-start.1 = ((f32[4,1,128]{2,1,0:T(1,128)}), f32[4,1,128]{2,1,0:T(1,128)S(1)}, u32[]{:S(2)}, u32[]{:S(2)}) async-start(f32[4,1,128]{2,1,0:T(1,128)} %reshape.63), calls=%async_computation.1 | async-start | bytes 4096 | tf_op jit(solution)/shard_map/all_to_all | solution.py:78
Sparse Core Ops, SparseCore 0:
  27.2 74.5 all-gather.3
  280.1 72.0 all-gather.5
where the time goes:
time: 460 us; the launch traced here: 458 us
  other arithmetic  217 us (47%)
  waiting for transfers between devices  151 us (33%)
  local copies, waits for them, and re-layouts  34.7 us (8%)
  matrix products  24 us (5%)
  between operations  13.6 us (3%)
  blocking collectives  13.5 us (3%)
    top_k x32, other arithmetic, keep_best(): return lax.top_k(values, TOP_K)[0]  210 us
    all_gather x1, waiting for transfers between devices, per_device(): lax.all_gather(arrived, 'shard', axis=0, tiled=True)  74.5 us
    all_gather x1, waiting for transfers between devices, combined_all(): pieces = lax.all_gather(value, axis)  72.2 us
    unnamed x1, matrix products  23.6 us
    all_to_all x1, blocking collectives, per_device(): lax.all_to_all(packed, 'mass', split_axis=0, concat_axis=0, tiled=True)  13.5 us
    slice x1, local copies, waits for them, and re-layouts, combined_all(): tail = pieces[1:]  11.1 us
    while x3, local copies, waits for them, and re-layouts, combined_all(): lax.scan(lambda subtotal, piece: (join(subtotal, piece), None), head, tail)  9.73 us
  transfers between devices with their start and end apart: 3, of which 3 were waited for; matrix products, arithmetic and copies ran while one was open for 0% of the time, Pallas kernels for 0%

commit v1 on v0

--- a/solution.py
+++ b/solution.py
@@ -1,18 +1,17 @@
+import functools
+
 import jax
 import jax.numpy as jnp
 from jax import lax
+from jax.experimental import pallas as pl
+from jax.experimental.pallas import tpu as pltpu
+from jax.sharding import Mesh
 from jax.sharding import PartitionSpec as P
 
 MAX_SHIFT = 2048
 TOP_K = 16
-
-
-def combined_all(value, axis, join):
-    pieces = lax.all_gather(value, axis)
-    head = pieces[0]
-    tail = pieces[1:]
-    subtotal, _ = lax.scan(lambda subtotal, piece: (join(subtotal, piece), None), head, tail)
-    return subtotal
+LANES = 128
+SUBLANES = 8
 
 
 def shifted_spectra(queries, offsets):
@@ -44,16 +43,60 @@
     return jnp.sum(earlier.astype(jnp.int32), axis=1)
 
 
-def keep_best(values):
-    return lax.top_k(values, TOP_K)[0]
+def merge_sorted(first, second):
+    merged = [jnp.maximum(first[k], second[TOP_K - 1 - k]) for k in range(TOP_K)]
+    span = TOP_K // 2
+    while span >= 1:
+        for k in range(TOP_K):
+            if (k // span) % 2 == 0:
+                upper, lower = merged[k], merged[k + span]
+                merged[k] = jnp.maximum(upper, lower)
+                merged[k + span] = jnp.minimum(upper, lower)
+        span //= 2
+    return merged
 
 
-def combine_best(first_list, second_list):
-    return keep_best(jnp.concatenate([first_list, second_list], axis=1))
+def column_topk_kernel(scores_ref, out_ref):
+    steps = scores_ref.shape[0] // SUBLANES
+    lowest = jnp.full((SUBLANES, LANES), -jnp.inf, jnp.float32)
+
+    def insert(step, kept):
+        start = pl.multiple_of(step * SUBLANES, SUBLANES)
+        value = scores_ref[pl.ds(start, SUBLANES), :]
+        updated = []
+        for k in range(TOP_K):
+            updated.append(jnp.maximum(kept[k], value))
+            value = jnp.minimum(kept[k], value)
+        return tuple(updated)
+
+    kept = lax.fori_loop(0, steps, insert, (lowest,) * TOP_K, unroll=8)
+    kept = list(kept)
+    shift = SUBLANES // 2
+    while shift >= 1:
+        rolled = [pltpu.roll(kept[k], shift, 0) for k in range(TOP_K)]
+        kept = merge_sorted(kept, rolled)
+        shift //= 2
+    for k in range(TOP_K):
+        out_ref[pl.ds(k, 1), :] = kept[k][0:1, :]
+
+
+def column_topk(scores):
+    rows, columns = scores.shape
+    return pl.pallas_call(
+        column_topk_kernel,
+        out_shape=jax.ShapeDtypeStruct((TOP_K, columns), jnp.float32),
+        grid=(columns // LANES,),
+        in_specs=[pl.BlockSpec((rows, LANES), lambda j: (0, j))],
+        out_specs=pl.BlockSpec((TOP_K, LANES), lambda j: (0, j)),
+        cost_estimate=pl.CostEstimate(
+            flops=2 * TOP_K * rows * columns, transcendentals=0, bytes_accessed=4 * rows * columns
+        ),
+    )(scores)
 
 
 def per_device(queries, library, routes, offsets):
     mass_count = lax.axis_size("mass")
+    shard_count = lax.axis_size("shard")
     query_count = queries.shape[0]
     capacity = query_count // 2
     spectra = shifted_spectra(queries, offsets)
@@ -64,17 +107,16 @@
     ).astype(jnp.bfloat16)
     packed = jnp.dot(selector, spectra, preferred_element_type=jnp.float32).astype(jnp.bfloat16)
     arrived = lax.all_to_all(packed, "mass", split_axis=0, concat_axis=0, tiled=True)
-    scores = lax.dot_general(
-        lax.all_gather(arrived, "shard", axis=0, tiled=True),
-        library,
-        (((1,), (1,)), ((), ())),
-        preferred_element_type=jnp.float32,
+    gathered = lax.all_gather(arrived, "shard", axis=0, tiled=True)
+    scores_t = lax.dot_general(
+        library, gathered, (((1,), (1,)), ((), ())), preferred_element_type=jnp.float32
     )
-    local_best = keep_best(scores)
-    merged = combined_all(local_best, "shard", combine_best)
-    own_best = lax.dynamic_slice_in_dim(
-        merged, lax.axis_index("shard") * (mass_count * capacity), mass_count * capacity, 0
-    )
+    local_best = column_topk(scores_t)
+    slots_per_shard = mass_count * capacity
+    outgoing = local_best.T.reshape(shard_count, slots_per_shard, TOP_K)
+    incoming = lax.all_to_all(outgoing, "shard", split_axis=0, concat_axis=0, tiled=True)
+    candidates = incoming.transpose(1, 0, 2).reshape(slots_per_shard, shard_count * TOP_K)
+    own_best = lax.top_k(candidates, TOP_K)[0]
     returned_best = lax.all_to_all(own_best, "mass", split_axis=0, concat_axis=0, tiled=True)
     slot_match = slot_index[:, None] == jnp.arange(mass_count * capacity, dtype=jnp.int32)[None, :]
     return jnp.sum(

time: 460 us -> 173 us (0.38)
  other arithmetic: 217 us -> 11.9 us
  waiting for transfers between devices: 151 us -> 86.1 us
  local copies, waits for them, and re-layouts: 34.7 us -> 4.87 us
  Pallas kernels: 0 us -> 8.41 us
  starting transfers between devices: 4.23 us -> 9.4 us
    top_k x32 -> x1, other arithmetic: 210 us -> 4.37 us  [per_device(): own_best = lax.top_k(candidates, TOP_K)[0]]
    all_gather x2 -> x1, waiting for transfers between devices: 147 us -> 74.7 us  [per_device(): gathered = lax.all_gather(arrived, 'shard', axis=0, tiled=True)]
    unnamed x1 -> x0, matrix products: 23.6 us -> none
    dot_general x0 -> x1, matrix products: none -> 23.6 us  [per_device(): lax.dot_general(library, gathered, (((1,), (1,)), ((), ())), preferred_el...]
    slice x2 -> x0, local copies, waits for them, and re-layouts: 12.2 us -> none  [the longest x1 11.1 us: combined_all(): tail = pieces[1:]]
    while x3 -> x0, local copies, waits for them, and re-layouts: 9.73 us -> none  [combined_all(): lax.scan(lambda subtotal, piece: (join(subtotal, piece), None), head, tail)]
    pallas_call x0 -> x1, Pallas kernels: none -> 8.41 us  [column_topk(): pl.pallas_call(column_topk_kernel, out_shape=jax.ShapeDtypeStruct((TOP_K,...]
    top_k x33 -> x0, local copies, waits for them, and re-layouts: 7.38 us -> none  [keep_best(): return lax.top_k(values, TOP_K)[0]]
where the time goes in v1:
time: 173 us; the launch traced here: 172 us
  waiting for transfers between devices  86.1 us (50%)
  matrix products  24 us (14%)
  between operations  13.6 us (8%)
  blocking collectives  13.5 us (8%)
  other arithmetic  11.9 us (7%)
  starting transfers between devices  9.4 us (5%)
  Pallas kernels  8.41 us (5%)
  local copies, waits for them, and re-layouts  4.87 us (3%)
    all_gather x1, waiting for transfers between devices, per_device(): gathered = lax.all_gather(arrived, 'shard', axis=0, tiled=True)  74.7 us
    dot_general x1, matrix products, per_device(): lax.dot_general(library, gathered, (((1,), (1,)), ((), ())), preferred_el...  23.6 us
    all_to_all x1, blocking collectives, per_device(): lax.all_to_all(packed, 'mass', split_axis=0, concat_axis=0, tiled=True)  13.5 us
    pallas_call x1, Pallas kernels, column_topk(): pl.pallas_call(column_topk_kernel, out_shape=jax.ShapeDtypeStruct((TOP_K,...  8.41 us
    all_to_all x1, waiting for transfers between devices, per_device(): lax.all_to_all(outgoing, 'shard', split_axis=0, concat_axis=0, tiled=True)  7.35 us
    all_to_all x1, starting transfers between devices, per_device(): lax.all_to_all(outgoing, 'shard', split_axis=0, concat_axis=0, tiled=True)  5.4 us
    top_k x1, other arithmetic, per_device(): own_best = lax.top_k(candidates, TOP_K)[0]  4.37 us
    all_to_all x1, starting transfers between devices, per_device(): lax.all_to_all(own_best, 'mass', split_axis=0, concat_axis=0, tiled=True)  4 us
  transfers between devices with their start and end apart: 3, of which 3 were waited for; matrix products, arithmetic and copies ran while one was open for 0% of the time, Pallas kernels for 0%

profile of v1, /device:TPU:1, one launch (start us, length us, event | category | flops | bytes accessed | tf_op | source)
XLA Modules:
  0.0 171.8 jit_solution(18050672207637124518)
XLA Ops:
  6.5 0.0 all-gather.2.cloned.1.call-start
  6.5 0.7 and_compare_fusion.12
  7.3 1.0 pad_maximum_fusion
  8.3 0.2 slice.57
  8.4 1.1 pad_select_fusion.11
  9.5 0.2 slice.58
  9.7 0.2 pad_select_fusion.10
  9.9 0.2 slice.59
  10.1 0.2 pad_select_fusion.9
  10.2 0.2 slice.60
  10.4 0.2 pad_select_fusion.8
  10.6 0.2 slice.61
  10.7 0.2 pad_select_fusion.7
  10.9 0.2 slice.62
  11.1 0.2 pad_select_fusion.6
  11.3 0.2 slice.63
  11.4 0.2 pad_select_fusion.5
  11.6 0.2 pad_select_fusion.4
  11.8 0.2 pad_select_fusion.3
  12.0 0.2 pad_select_fusion.2
  12.2 0.2 pad_select_fusion.1
  12.4 0.2 pad_select_fusion
  12.6 0.4 multiply_reduce_fusion
  13.0 0.2 convert_reduce_fusion
  13.2 0.4 fusion
  13.6 13.5 %all_to_all.26 = bf16[4,8,8192]{2,1,0:T(8,128)(2,1)} all-to-all(bf16[4,8,8192]{2,1,0:T(8,128)(2,1)S(1)} %fusion), channel_id=1, replica_groups=mesh['mass'=4,'shard'=32] {'mass'}, dimensions={0} | all-to-all | bytes 1048576 | tf_op jit(solution)/shard_map/all_to_all | solution.py:109
  27.1 0.0 all-gather.2.cloned.1.call-update
  27.1 74.7 %all-gather.2.cloned.1.call-done = bf16[1024,8192]{1,0:T(8,128)(2,1)} async-done(((bf16[32,8192]{1,0:T(8,128)(2,1)}), bf16[1024,8192]{1,0:T(8,128)(2,1)}) %all-gather.2.cloned.1.call-update) | async-done | bytes 16777232 | tf_op jit(solution)/shard_map/all_gather | solution.py:110
  101.8 23.6 %convolution_bitcast_fusion.scores_ref = f32[1024,1024]{1,0:T(8,128)} fusion(bf16[1024,8192]{1,0:T(8,128)(2,1)} %all-gather.2.cloned.1.call-done, bf16[1024,8192]{1,0:T(8,128)(2,1)} %param.5), kind=kOutput, calls=%fused_computation.2 | convolution fusion | flops 17179869184 | bytes 37748736 | tf_op jit(solution)/shard_map/dot_general | solution.py:111
  125.5 8.4 %shard_map.46 = f32[16,1024]{1,0:T(8,128)} custom-call(f32[1024,1024]{1,0:T(8,128)} %convolution_bitcast_fusion.scores_ref), custom_call_target="tpu_custom_call" | custom-call | flops 33554432 | bytes 4194304 | tf_op jit(solution)/shard_map/pallas_call | solution.py:85
  133.9 1.0 reshape.65
  134.9 0.2 copy.17
  135.0 0.8 reshape.67
  135.8 5.4 %all-to-all-start.1 = ((f32[32,1,512]{2,1,0:T(1,128)}), f32[32,1,512]{2,1,0:T(1,128)S(1)}, u32[]{:S(2)}, u32[]{:S(2)}) async-start(f32[32,1,512]{2,1,0:T(1,128)} %reshape.67), calls=%async_computation.1 | async-start | bytes 131072 | tf_op jit(solution)/shard_map/all_to_all | solution.py:117
  141.2 7.3 %all-to-all-done.1 = f32[32,1,512]{2,1,0:T(1,128)S(1)} async-done(((f32[32,1,512]{2,1,0:T(1,128)}), f32[32,1,512]{2,1,0:T(1,128)S(1)}, u32[]{:S(2)}, u32[]{:S(2)}) %all-to-all-start.1) | async-done | bytes 65568 | tf_op jit(solution)/shard_map/all_to_all | solution.py:117
  148.6 0.6 broadcast.200
  149.2 0.8 reduce
  150.0 0.1 reshape.68
  150.1 0.1 copy.13
  150.2 4.4 %sort_prefixfusion = f32[32,16]{1,0:T(8,128)S(1)} fusion(f32[32,512]{1,0:T(8,128)S(1)} %copy.13), kind=kCustom, calls=%top_k.9.sort_prefix | custom fusion | flops 229376 | bytes 67584 | tf_op jit(solution)/shard_map/top_k | solution.py:119
  154.6 0.7 reshape.69
  155.3 4.0 %all-to-all-start.2 = ((f32[4,1,128]{2,1,0:T(1,128)}), f32[4,1,128]{2,1,0:T(1,128)S(1)}, u32[]{:S(2)}, u32[]{:S(2)}) async-start(f32[4,1,128]{2,1,0:T(1,128)} %reshape.69), calls=%async_computation.2 | async-start | bytes 4096 | tf_op jit(solution)/shard_map/all_to_all | solution.py:120
  159.3 0.1 iota_compare_fusion.2
  159.3 4.0 %all-to-all-done.2 = f32[4,1,128]{2,1,0:T(1,128)S(1)} async-done(((f32[4,1,128]{2,1,0:T(1,128)}), f32[4,1,128]{2,1,0:T(1,128)S(1)}, u32[]{:S(2)}, u32[]{:S(2)}) %all-to-all-start.2) | async-done | bytes 2080 | tf_op jit(solution)/shard_map/all_to_all | solution.py:120
  163.3 0.7 reduce.1
  164.0 0.1 reshape.70
  164.1 0.1 copy.14
  164.2 0.7 select_reduce_fusion
  (14 shorter events, 0.2 us)
Async XLA Ops:
  6.5 6.1 %copy-start = (bf16[16,8192]{1,0:T(8,128)(2,1)S(1)}, bf16[16,8192]{1,0:T(8,128)(2,1)}, u32[]{:S(2)}) copy-start(bf16[16,8192]{1,0:T(8,128)(2,1)} %param.4) | copy-start | bytes 786436
  6.5 6.5 %copy-start.1 = (s32[16,1]{0,1:T(1,128)S(1)}, s32[16,1]{0,1:T(1,128)}, u32[]{:S(2)}) copy-start(s32[16,1]{0,1:T(1,128)} %param.6) | copy-start | bytes 196
  6.5 95.3 %all-gather.2.cloned.1.call-start = ((), (), s32[]{:S(2)}) async-start(), calls=%async_computation.3 | async-start | bytes 17301504 | tf_op jit(solution)/shard_map/all_gather | solution.py:110
  135.8 12.8 %all-to-all-start.1 = ((f32[32,1,512]{2,1,0:T(1,128)}), f32[32,1,512]{2,1,0:T(1,128)S(1)}, u32[]{:S(2)}, u32[]{:S(2)}) async-start(f32[32,1,512]{2,1,0:T(1,128)} %reshape.67), calls=%async_computation.1 | async-start | bytes 131072 | tf_op jit(solution)/shard_map/all_to_all | solution.py:117
  155.3 8.1 %all-to-all-start.2 = ((f32[4,1,128]{2,1,0:T(1,128)}), f32[4,1,128]{2,1,0:T(1,128)S(1)}, u32[]{:S(2)}, u32[]{:S(2)}) async-start(f32[4,1,128]{2,1,0:T(1,128)} %reshape.69), calls=%async_computation.2 | async-start | bytes 4096 | tf_op jit(solution)/shard_map/all_to_all | solution.py:120
Sparse Core Ops, SparseCore 0:
  27.2 74.5 all-gather.1

commit v2 on v1

--- a/solution.py
+++ b/solution.py
@@ -94,47 +94,76 @@
     )(scores)
 
 
+def take_group(packed, group):
+    chooser = (jnp.arange(packed.shape[0], dtype=jnp.int32) == group).astype(packed.dtype)
+    return jnp.einsum("g,gsb->sb", chooser, packed)
+
+
 def per_device(queries, library, routes, offsets):
     mass_count = lax.axis_size("mass")
-    shard_count = lax.axis_size("shard")
+    core_count = lax.axis_size("core")
     query_count = queries.shape[0]
     capacity = query_count // 2
+    own_mass = lax.axis_index("mass")
+    own_core = lax.axis_index("core")
     spectra = shifted_spectra(queries, offsets)
     dest_group = routes[:, 0]
-    slot_index = dest_group * capacity + block_ranks(dest_group)
+    ranks = block_ranks(dest_group)
+    slot_index = dest_group * capacity + ranks
     selector = (
         jnp.arange(mass_count * capacity, dtype=jnp.int32)[:, None] == slot_index[None, :]
     ).astype(jnp.bfloat16)
     packed = jnp.dot(selector, spectra, preferred_element_type=jnp.float32).astype(jnp.bfloat16)
-    arrived = lax.all_to_all(packed, "mass", split_axis=0, concat_axis=0, tiled=True)
-    gathered = lax.all_gather(arrived, "shard", axis=0, tiled=True)
-    scores_t = lax.dot_general(
-        library, gathered, (((1,), (1,)), ((), ())), preferred_element_type=jnp.float32
+    packed = packed.reshape(mass_count, capacity, packed.shape[-1])
+    partner = [(core, core_count - 1 - core) for core in range(core_count)]
+    chunk_best = []
+    for distance in range(mass_count):
+        outgoing = take_group(packed, (own_mass + distance) % mass_count)
+        if distance == 0:
+            incoming = outgoing
+        else:
+            incoming = lax.ppermute(
+                outgoing,
+                "mass",
+                [(source, (source + distance) % mass_count) for source in range(mass_count)],
+            )
+        own_side = lax.all_gather(incoming, "xz", axis=0, tiled=True)
+        other_side = lax.ppermute(own_side, "core", partner)
+        both = jnp.concatenate([own_side, other_side], axis=0)
+        scores_t = lax.dot_general(
+            library, both, (((1,), (1,)), ((), ())), preferred_element_type=jnp.float32
+        )
+        chunk_best.append(column_topk(scores_t))
+    xz_count = lax.axis_size("xz")
+    stacked = jnp.stack(chunk_best).reshape(mass_count, TOP_K, core_count, xz_count, capacity)
+    stacked = stacked.transpose(0, 2, 3, 4, 1)
+    source_mass = jnp.arange(mass_count, dtype=jnp.int32)
+    by_mass = jnp.take(stacked, (own_mass - source_mass) % mass_count, axis=0)
+    side_of_core = jnp.where(jnp.arange(core_count, dtype=jnp.int32) == own_core, 0, 1)
+    by_core = jnp.take(by_mass, side_of_core, axis=1)
+    outgoing = by_core.transpose(0, 2, 1, 3, 4).reshape(-1, capacity, TOP_K)
+    received = lax.all_to_all(
+        outgoing, ("mass", "xz", "core"), split_axis=0, concat_axis=0, tiled=True
     )
-    local_best = column_topk(scores_t)
-    slots_per_shard = mass_count * capacity
-    outgoing = local_best.T.reshape(shard_count, slots_per_shard, TOP_K)
-    incoming = lax.all_to_all(outgoing, "shard", split_axis=0, concat_axis=0, tiled=True)
-    candidates = incoming.transpose(1, 0, 2).reshape(slots_per_shard, shard_count * TOP_K)
-    own_best = lax.top_k(candidates, TOP_K)[0]
-    returned_best = lax.all_to_all(own_best, "mass", split_axis=0, concat_axis=0, tiled=True)
-    slot_match = slot_index[:, None] == jnp.arange(mass_count * capacity, dtype=jnp.int32)[None, :]
-    return jnp.sum(
-        jnp.where(slot_match[:, :, None], returned_best[None, :, :], jnp.float32(0.0)), axis=1
-    )
+    received = received.reshape(mass_count, xz_count * core_count, capacity, TOP_K)
+    received = received.transpose(0, 2, 1, 3).reshape(mass_count * capacity, -1)
+    candidates = jnp.take(received, slot_index, axis=0)
+    return lax.top_k(candidates, TOP_K)[0]
 
 
 def solution(mesh):
-    placed = (
-        P(("mass", "shard"), None),
-        P(("mass", "shard"), None),
-        P(("mass", "shard"), None),
-        P(("mass", "shard")),
+    mass_count, shard_count = mesh.devices.shape
+    core_count = 2
+    split_mesh = Mesh(
+        mesh.devices.reshape(mass_count, shard_count // core_count, core_count),
+        ("mass", "xz", "core"),
     )
+    spread = ("mass", "xz", "core")
+    placed = (P(spread, None), P(spread, None), P(spread, None), P(spread))
     return jax.shard_map(
         per_device,
-        mesh=mesh,
+        mesh=split_mesh,
         in_specs=placed,
-        out_specs=P(("mass", "shard"), None),
+        out_specs=P(spread, None),
         check_vma=False,
     )

time: 173 us -> 299 us (1.73)
  waiting for transfers between devices: 86.1 us -> 179 us
  matrix products: 24 us -> 52.4 us
  blocking collectives: 13.5 us -> 0 us
  starting transfers between devices: 9.4 us -> 21 us
  local copies, waits for them, and re-layouts: 4.87 us -> 12 us
  Pallas kernels: 8.41 us -> 12.2 us
  other arithmetic: 11.9 us -> 8.82 us
    all_gather x1 -> x4, waiting for transfers between devices: 74.7 us -> 158 us  [per_device(): own_side = lax.all_gather(incoming, 'xz', axis=0, tiled=True)]
    dot_general x1 -> x8, matrix products: 23.6 us -> 52.1 us  [the longest x4 49.1 us: per_device(): lax.dot_general(library, both, (((1,), (1,)), ((), ())), preferred_elemen...]
    ppermute x0 -> x7, starting transfers between devices: none -> 13.9 us  [the longest x4 8.87 us: per_device(): other_side = lax.ppermute(own_side, 'core', partner)]
    all_to_all x1 -> x0, blocking collectives: 13.5 us -> none  [per_device(): lax.all_to_all(packed, 'mass', split_axis=0, concat_axis=0, tiled=True)]
    ppermute x0 -> x7, waiting for transfers between devices: none -> 11.3 us  [the longest x3 11.3 us: per_device(): lax.ppermute(outgoing, 'mass', [(source, (source + distance) % mass_count...]
    pallas_call x1 -> x4, Pallas kernels: 8.41 us -> 12.2 us  [column_topk(): pl.pallas_call(column_topk_kernel, out_shape=jax.ShapeDtypeStruct((TOP_K,...]
    pallas_call x0 -> x4, local copies, waits for them, and re-layouts: none -> 3.26 us  [column_topk(): pl.pallas_call(column_topk_kernel, out_shape=jax.ShapeDtypeStruct((TOP_K,...]
    all_to_all x2 -> x1, starting transfers between devices: 9.4 us -> 6.97 us  [per_device(): lax.all_to_all(outgoing, ('mass', 'xz', 'core'), split_axis=0, concat_axi...]
  transfers between devices with their start and end apart: 3 -> 12, of which waited for: 3 -> 8; matrix products, arithmetic and copies ran while one was open for 0% -> 14% of each run, Pallas kernels for 0% -> 3%
where the time goes in v2:
time: 299 us
  waiting for transfers between devices  179 us (60%)
  matrix products  52.4 us (18%)
  starting transfers between devices  21 us (7%)
  between operations  13.5 us (5%)
  Pallas kernels  12.2 us (4%)
  local copies, waits for them, and re-layouts  12 us (4%)
  other arithmetic  8.82 us (3%)
    all_gather x4, waiting for transfers between devices, per_device(): own_side = lax.all_gather(incoming, 'xz', axis=0, tiled=True)  158 us
    dot_general x4, matrix products, per_device(): lax.dot_general(library, both, (((1,), (1,)), ((), ())), preferred_elemen...  49.1 us
    pallas_call x4, Pallas kernels, column_topk(): pl.pallas_call(column_topk_kernel, out_shape=jax.ShapeDtypeStruct((TOP_K,...  12.2 us
    ppermute x3, waiting for transfers between devices, per_device(): lax.ppermute(outgoing, 'mass', [(source, (source + distance) % mass_count...  11.3 us
    all_to_all x1, waiting for transfers between devices, per_device(): lax.all_to_all(outgoing, ('mass', 'xz', 'core'), split_axis=0, concat_axi...  9.42 us
    ppermute x4, starting transfers between devices, per_device(): other_side = lax.ppermute(own_side, 'core', partner)  8.87 us
    all_to_all x1, starting transfers between devices, per_device(): lax.all_to_all(outgoing, ('mass', 'xz', 'core'), split_axis=0, concat_axi...  6.97 us
  transfers between devices with their start and end apart: 12, of which 8 were waited for; matrix products, arithmetic and copies ran while one was open for 14% of the time, Pallas kernels for 3%

profile of v2, /device:TPU:1, one launch (start us, length us, event | category | flops | bytes accessed | tf_op | source)
XLA Modules:
  0.0 298.8 jit_solution(17997369790238030211)
XLA Ops:
  6.5 0.7 and_compare_fusion.12
  7.2 1.0 pad_maximum_fusion
  8.4 1.1 pad_select_fusion.11
  12.7 0.4 multiply_reduce_fusion
  13.3 0.4 fusion
  13.6 0.7 fusion.36
  14.4 0.8 copy.56
  15.3 0.7 fusion.34
  16.2 2.2 collective-permute-start.1
  18.4 4.5 %collective-permute-done.1 = bf16[8,8192]{1,0:T(8,128)(2,1)S(1)} collective-permute-done((bf16[8,8192]{1,0:T(8,128)(2,1)S(1)}, bf16[8,8192]{1,0:T(8,128)(2,1)S(1)}, u32[]{:S(2)}, u32[]{:S(2)}) %collective-permute-start.1) | collective-permute-done | bytes 131104 | tf_op jit(solution)/shard_map/ppermute | solution.py:125
  22.9 0.7 copy-done.1
  23.6 0.7 fusion.32
  24.5 1.5 collective-permute-start.3
  26.1 3.9 %collective-permute-done.3 = bf16[8,8192]{1,0:T(8,128)(2,1)S(1)} collective-permute-done((bf16[8,8192]{1,0:T(8,128)(2,1)S(1)}, bf16[8,8192]{1,0:T(8,128)(2,1)S(1)}, u32[]{:S(2)}, u32[]{:S(2)}) %collective-permute-start.3) | collective-permute-done | bytes 131104 | tf_op jit(solution)/shard_map/ppermute | solution.py:125
  29.9 0.6 copy-done.2
  30.7 0.7 fusion.30
  31.6 1.4 collective-permute-start.5
  32.9 2.9 collective-permute-done.5
  35.8 0.6 copy-done.3
  36.5 25.5 %all-gather.5.cloned.1.call-done = bf16[128,8192]{1,0:T(8,128)(2,1)} async-done(((bf16[8,8192]{1,0:T(8,128)(2,1)}), bf16[128,8192]{1,0:T(8,128)(2,1)}) %all-gather.5.cloned.1.call-update) | async-done | bytes 2097168 | tf_op jit(solution)/shard_map/all_gather | solution.py:130
  62.0 2.2 collective-permute-start
  64.3 44.2 %all-gather.7.cloned.1.call-done = bf16[128,8192]{1,0:T(8,128)(2,1)} async-done(((bf16[8,8192]{1,0:T(8,128)(2,1)}), bf16[128,8192]{1,0:T(8,128)(2,1)}) %all-gather.7.cloned.1.call-update) | async-done | bytes 2097168 | tf_op jit(solution)/shard_map/all_gather | solution.py:130
  108.5 2.2 collective-permute-start.2
  110.8 44.1 %all-gather.9.cloned.1.call-done = bf16[128,8192]{1,0:T(8,128)(2,1)} async-done(((bf16[8,8192]{1,0:T(8,128)(2,1)}), bf16[128,8192]{1,0:T(8,128)(2,1)}) %all-gather.9.cloned.1.call-update) | async-done | bytes 2097168 | tf_op jit(solution)/shard_map/all_gather | solution.py:130
  155.0 2.2 collective-permute-start.4
  157.2 44.1 %all-gather.11.cloned.1.call-done = bf16[128,8192]{1,0:T(8,128)(2,1)} async-done(((bf16[8,8192]{1,0:T(8,128)(2,1)}), bf16[128,8192]{1,0:T(8,128)(2,1)}) %all-gather.11.cloned.1.call-update) | async-done | bytes 2097168 | tf_op jit(solution)/shard_map/all_gather | solution.py:130
  201.3 2.2 collective-permute-start.6
  203.5 12.5 %fusion.26.scores_ref = f32[1024,256]{1,0:T(8,128)} fusion(bf16[1024,8192]{1,0:T(8,128)(2,1)} %param.5, bf16[128,8192]{1,0:T(8,128)(2,1)} %collective-permute-done, bf16[128,8192]{1,0:T(8,128)(2,1)} %all-gather.5.cloned.1.call-done), kind=kOutput, calls=%fused_computation.24 | convolution fusion | flops 4303355904 | bytes 22020096 | tf_op jit(solution)/shard_map/dot_general | solution.py:133
  216.0 3.0 %shard_map.46 = f32[16,256]{1,0:T(8,128)} custom-call(f32[1024,256]{1,0:T(8,128)} %fusion.26.scores_ref), custom_call_target="tpu_custom_call" | custom-call | flops 8388608 | bytes 1048576 | tf_op jit(solution)/shard_map/pallas_call | solution.py:85
  219.1 0.8 copy.21
  219.9 11.9 %fusion.23.scores_ref = f32[1024,256]{1,0:T(8,128)} fusion(bf16[1024,8192]{1,0:T(8,128)(2,1)} %param.5, bf16[128,8192]{1,0:T(8,128)(2,1)} %collective-permute-done.2, bf16[128,8192]{1,0:T(8,128)(2,1)S(1)} %copy-done.5), kind=kOutput, calls=%fused_computation.23 | convolution fusion | flops 4303355904 | bytes 22020096 | tf_op jit(solution)/shard_map/dot_general | solution.py:133
  231.9 3.0 %shard_map.47 = f32[16,256]{1,0:T(8,128)} custom-call(f32[1024,256]{1,0:T(8,128)} %fusion.23.scores_ref), custom_call_target="tpu_custom_call" | custom-call | flops 8388608 | bytes 1048576 | tf_op jit(solution)/shard_map/pallas_call | solution.py:85
  234.9 0.8 copy.23
  235.7 12.7 %fusion.20.scores_ref = f32[1024,256]{1,0:T(8,128)} fusion(bf16[1024,8192]{1,0:T(8,128)(2,1)} %param.5, bf16[128,8192]{1,0:T(8,128)(2,1)} %collective-permute-done.4, bf16[128,8192]{1,0:T(8,128)(2,1)} %all-gather.9.cloned.1.call-done), kind=kOutput, calls=%fused_computation.22 | convolution fusion | flops 4303355904 | bytes 22020096 | tf_op jit(solution)/shard_map/dot_general | solution.py:133
  248.4 3.0 %shard_map.48 = f32[16,256]{1,0:T(8,128)} custom-call(f32[1024,256]{1,0:T(8,128)} %fusion.20.scores_ref), custom_call_target="tpu_custom_call" | custom-call | flops 8388608 | bytes 1048576 | tf_op jit(solution)/shard_map/pallas_call | solution.py:85
  251.5 0.8 copy.25
  252.3 11.9 %fusion.17.scores_ref = f32[1024,256]{1,0:T(8,128)} fusion(bf16[1024,8192]{1,0:T(8,128)(2,1)} %param.5, bf16[128,8192]{1,0:T(8,128)(2,1)} %collective-permute-done.6, bf16[128,8192]{1,0:T(8,128)(2,1)S(1)} %copy-done.6), kind=kOutput, calls=%fused_computation.21 | convolution fusion | flops 4303355904 | bytes 22020096 | tf_op jit(solution)/shard_map/dot_general | solution.py:133
  264.2 3.0 %shard_map.49 = f32[16,256]{1,0:T(8,128)} custom-call(f32[1024,256]{1,0:T(8,128)} %fusion.17.scores_ref), custom_call_target="tpu_custom_call" | custom-call | flops 8388608 | bytes 1048576 | tf_op jit(solution)/shard_map/pallas_call | solution.py:85
  267.3 0.8 copy.27
  268.2 0.6 gather_fusion
  268.9 0.6 gather_fusion.1
  269.6 0.8 reshape.162
  270.4 7.0 %all-to-all-start = ((f32[128,1,128]{2,1,0:T(1,128)}), f32[128,1,128]{2,1,0:T(1,128)S(1)}, u32[]{:S(2)}, u32[]{:S(2)}) async-start(f32[128,1,128]{2,1,0:T(1,128)} %reshape.162), calls=%async_computation | async-start | bytes 131072 | tf_op jit(solution)/shard_map/all_to_all | solution.py:145
  277.4 9.4 %all-to-all-done = f32[128,1,128]{2,1,0:T(1,128)S(1)} async-done(((f32[128,1,128]{2,1,0:T(1,128)}), f32[128,1,128]{2,1,0:T(1,128)S(1)}, u32[]{:S(2)}, u32[]{:S(2)}) %all-to-all-start) | async-done | bytes 65568 | tf_op jit(solution)/shard_map/all_to_all | solution.py:145
  286.9 0.5 broadcast.366
  287.4 0.8 reduce
  289.1 0.6 gather_fusion.2
  289.8 2.5 sort_prefixfusion
  (71 shorter events, 5.5 us)
Async XLA Ops:
  6.5 55.5 %all-gather.5.cloned.1.call-start = ((), (), s32[]{:S(2)}) async-start(), calls=%async_computation.1 | async-start | bytes 2228224 | tf_op jit(solution)/shard_map/all_gather | solution.py:130
  11.7 1.0 copy-start
  11.8 1.3 copy-start.4
  15.2 93.3 %all-gather.7.cloned.1.call-start = ((), (), s32[]{:S(2)}) async-start(), calls=%async_computation.2 | async-start | bytes 2228224 | tf_op jit(solution)/shard_map/all_gather | solution.py:130
  16.2 6.7 %collective-permute-start.1 = (bf16[8,8192]{1,0:T(8,128)(2,1)S(1)}, bf16[8,8192]{1,0:T(8,128)(2,1)S(1)}, u32[]{:S(2)}, u32[]{:S(2)}) collective-permute-start(bf16[8,8192]{1,0:T(8,128)(2,1)S(1)} %bitcast.73), channel_id=1, source_target_pairs={{0,32},{32,64},{64,96},{96,0},{1,33},{33,65},{65,97},{97,1},{2,34}... | collective-permute-start | bytes 393224 | tf_op jit(solution)/shard_map/ppermute | solution.py:125
  22.9 0.7 copy-start.1
  23.6 131.4 %all-gather.9.cloned.1.call-start = ((), (), s32[]{:S(2)}) async-start(), calls=%async_computation.3 | async-start | bytes 2228224 | tf_op jit(solution)/shard_map/all_gather | solution.py:130
  24.5 5.4 %collective-permute-start.3 = (bf16[8,8192]{1,0:T(8,128)(2,1)S(1)}, bf16[8,8192]{1,0:T(8,128)(2,1)S(1)}, u32[]{:S(2)}, u32[]{:S(2)}) collective-permute-start(bf16[8,8192]{1,0:T(8,128)(2,1)S(1)} %bitcast.74), channel_id=1, source_target_pairs={{0,64},{32,96},{64,0},{96,32},{1,65},{33,97},{65,1},{97,33},{2,66}... | collective-permute-start | bytes 393224 | tf_op jit(solution)/shard_map/ppermute | solution.py:125
  29.9 0.6 copy-start.2
  30.6 170.7 %all-gather.11.cloned.1.call-start = ((), (), s32[]{:S(2)}) async-start(), calls=%async_computation.4 | async-start | bytes 2228224 | tf_op jit(solution)/shard_map/all_gather | solution.py:130
  31.6 4.3 %collective-permute-start.5 = (bf16[8,8192]{1,0:T(8,128)(2,1)S(1)}, bf16[8,8192]{1,0:T(8,128)(2,1)S(1)}, u32[]{:S(2)}, u32[]{:S(2)}) collective-permute-start(bf16[8,8192]{1,0:T(8,128)(2,1)S(1)} %bitcast.75), channel_id=1, source_target_pairs={{0,96},{32,0},{64,32},{96,64},{1,97},{33,1},{65,33},{97,65},{2,98}... | collective-permute-start | bytes 393224 | tf_op jit(solution)/shard_map/ppermute | solution.py:125
  35.8 0.6 copy-start.3
  62.0 141.4 %collective-permute-start = (bf16[128,8192]{1,0:T(8,128)(2,1)}, bf16[128,8192]{1,0:T(8,128)(2,1)}, u32[]{:S(2)}, u32[]{:S(2)}) collective-permute-start(bf16[128,8192]{1,0:T(8,128)(2,1)} %all-gather.5.cloned.1.call-done), channel_id=1, source_target_pairs={{0,1},{1,0},{2,3},{3,2},{4,5},{5,4},{6,7},{7,6},{8,9},{9,8},{10,11... | collective-permute-start | bytes 6291464 | tf_op jit(solution)/shard_map/ppermute | solution.py:131
  108.5 111.4 %collective-permute-start.2 = (bf16[128,8192]{1,0:T(8,128)(2,1)}, bf16[128,8192]{1,0:T(8,128)(2,1)}, u32[]{:S(2)}, u32[]{:S(2)}) collective-permute-start(bf16[128,8192]{1,0:T(8,128)(2,1)} %all-gather.7.cloned.1.call-done), channel_id=1, source_target_pairs={{0,1},{1,0},{2,3},{3,2},{4,5},{5,4},{6,7},{7,6},{8,9},{9,8},{10,11... | collective-permute-start | bytes 6291464 | tf_op jit(solution)/shard_map/ppermute | solution.py:131
  110.8 109.1 %copy-start.5 = (bf16[128,8192]{1,0:T(8,128)(2,1)S(1)}, bf16[128,8192]{1,0:T(8,128)(2,1)}, u32[]{:S(2)}) copy-start(bf16[128,8192]{1,0:T(8,128)(2,1)} %all-gather.7.cloned.1.call-done) | copy-start | bytes 6291460
  155.0 80.8 %collective-permute-start.4 = (bf16[128,8192]{1,0:T(8,128)(2,1)}, bf16[128,8192]{1,0:T(8,128)(2,1)}, u32[]{:S(2)}, u32[]{:S(2)}) collective-permute-start(bf16[128,8192]{1,0:T(8,128)(2,1)} %all-gather.9.cloned.1.call-done), channel_id=1, source_target_pairs={{0,1},{1,0},{2,3},{3,2},{4,5},{5,4},{6,7},{7,6},{8,9},{9,8},{10,11... | collective-permute-start | bytes 6291464 | tf_op jit(solution)/shard_map/ppermute | solution.py:131
  201.3 51.1 %collective-permute-start.6 = (bf16[128,8192]{1,0:T(8,128)(2,1)}, bf16[128,8192]{1,0:T(8,128)(2,1)}, u32[]{:S(2)}, u32[]{:S(2)}) collective-permute-start(bf16[128,8192]{1,0:T(8,128)(2,1)} %all-gather.11.cloned.1.call-done), channel_id=1, source_target_pairs={{0,1},{1,0},{2,3},{3,2},{4,5},{5,4},{6,7},{7,6},{8,9},{9,8},{10,11... | collective-permute-start | bytes 6291464 | tf_op jit(solution)/shard_map/ppermute | solution.py:131
  235.7 16.6 %copy-start.6 = (bf16[128,8192]{1,0:T(8,128)(2,1)S(1)}, bf16[128,8192]{1,0:T(8,128)(2,1)}, u32[]{:S(2)}) copy-start(bf16[128,8192]{1,0:T(8,128)(2,1)} %all-gather.11.cloned.1.call-done) | copy-start | bytes 6291460
  270.4 16.4 %all-to-all-start = ((f32[128,1,128]{2,1,0:T(1,128)}), f32[128,1,128]{2,1,0:T(1,128)S(1)}, u32[]{:S(2)}, u32[]{:S(2)}) async-start(f32[128,1,128]{2,1,0:T(1,128)} %reshape.162), calls=%async_computation | async-start | bytes 131072 | tf_op jit(solution)/shard_map/all_to_all | solution.py:145
Sparse Core Ops, SparseCore 0:
  15.3 46.6 all-gather.4
  64.2 44.2 all-gather.6
  110.6 44.2 all-gather.8
  156.9 44.2 all-gather.10

commit v3 on v1

--- a/solution.py
+++ b/solution.py
@@ -96,7 +96,7 @@
 
 def per_device(queries, library, routes, offsets):
     mass_count = lax.axis_size("mass")
-    shard_count = lax.axis_size("shard")
+    shard_count = lax.axis_size("xz") * lax.axis_size("core")
     query_count = queries.shape[0]
     capacity = query_count // 2
     spectra = shifted_spectra(queries, offsets)
@@ -107,34 +107,35 @@
     ).astype(jnp.bfloat16)
     packed = jnp.dot(selector, spectra, preferred_element_type=jnp.float32).astype(jnp.bfloat16)
     arrived = lax.all_to_all(packed, "mass", split_axis=0, concat_axis=0, tiled=True)
-    gathered = lax.all_gather(arrived, "shard", axis=0, tiled=True)
+    gathered = lax.all_gather(arrived, ("xz", "core"), axis=0, tiled=True)
     scores_t = lax.dot_general(
         library, gathered, (((1,), (1,)), ((), ())), preferred_element_type=jnp.float32
     )
     local_best = column_topk(scores_t)
-    slots_per_shard = mass_count * capacity
-    outgoing = local_best.T.reshape(shard_count, slots_per_shard, TOP_K)
-    incoming = lax.all_to_all(outgoing, "shard", split_axis=0, concat_axis=0, tiled=True)
-    candidates = incoming.transpose(1, 0, 2).reshape(slots_per_shard, shard_count * TOP_K)
-    own_best = lax.top_k(candidates, TOP_K)[0]
-    returned_best = lax.all_to_all(own_best, "mass", split_axis=0, concat_axis=0, tiled=True)
-    slot_match = slot_index[:, None] == jnp.arange(mass_count * capacity, dtype=jnp.int32)[None, :]
-    return jnp.sum(
-        jnp.where(slot_match[:, :, None], returned_best[None, :, :], jnp.float32(0.0)), axis=1
+    outgoing = local_best.T.reshape(shard_count, mass_count, capacity, TOP_K)
+    outgoing = outgoing.transpose(1, 0, 2, 3).reshape(-1, capacity, TOP_K)
+    received = lax.all_to_all(
+        outgoing, ("mass", "xz", "core"), split_axis=0, concat_axis=0, tiled=True
     )
+    received = received.reshape(mass_count, shard_count, capacity, TOP_K)
+    received = received.transpose(0, 2, 1, 3).reshape(mass_count * capacity, -1)
+    candidates = jnp.take(received, slot_index, axis=0)
+    return lax.top_k(candidates, TOP_K)[0]
 
 
 def solution(mesh):
-    placed = (
-        P(("mass", "shard"), None),
-        P(("mass", "shard"), None),
-        P(("mass", "shard"), None),
-        P(("mass", "shard")),
+    mass_count, shard_count = mesh.devices.shape
+    core_count = 2
+    split_mesh = Mesh(
+        mesh.devices.reshape(mass_count, shard_count // core_count, core_count),
+        ("mass", "xz", "core"),
     )
+    spread = ("mass", "xz", "core")
+    placed = (P(spread, None), P(spread, None), P(spread, None), P(spread))
     return jax.shard_map(
         per_device,
-        mesh=mesh,
+        mesh=split_mesh,
         in_specs=placed,
-        out_specs=P(("mass", "shard"), None),
+        out_specs=P(spread, None),
         check_vma=False,
     )

time: 173 us -> 165 us (0.954)
  other arithmetic: 11.9 us -> 8.57 us
  starting transfers between devices: 9.4 us -> 7.29 us
  waiting for transfers between devices: 86.1 us -> 84.2 us
    all_to_all x2 -> x1, starting transfers between devices: 9.4 us -> 7.29 us  [per_device(): lax.all_to_all(outgoing, ('mass', 'xz', 'core'), split_axis=0, concat_axi...]
    all_to_all x2 -> x1, waiting for transfers between devices: 11.3 us -> 9.42 us  [per_device(): lax.all_to_all(outgoing, ('mass', 'xz', 'core'), split_axis=0, concat_axi...]
    top_k x1, other arithmetic: 4.37 us -> 2.52 us  [per_device(): return lax.top_k(candidates, TOP_K)[0]]
  transfers between devices with their start and end apart: 3 -> 2, of which waited for: 3 -> 2; matrix products, arithmetic and copies ran while one was open for 0% -> 0% of each run, Pallas kernels for 0% -> 0%
where the time goes in v3:
time: 165 us
  waiting for transfers between devices  84.2 us (51%)
  matrix products  24 us (15%)
  between operations  13.6 us (8%)
  blocking collectives  13.5 us (8%)
  other arithmetic  8.57 us (5%)
  Pallas kernels  8.41 us (5%)
  starting transfers between devices  7.29 us (4%)
  local copies, waits for them, and re-layouts  5.29 us (3%)
    all_gather x1, waiting for transfers between devices, per_device(): gathered = lax.all_gather(arrived, ('xz', 'core'), axis=0, tiled=True)  74.7 us
    dot_general x1, matrix products, per_device(): lax.dot_general(library, gathered, (((1,), (1,)), ((), ())), preferred_el...  23.6 us
    all_to_all x1, blocking collectives, per_device(): lax.all_to_all(packed, 'mass', split_axis=0, concat_axis=0, tiled=True)  13.5 us
    all_to_all x1, waiting for transfers between devices, per_device(): lax.all_to_all(outgoing, ('mass', 'xz', 'core'), split_axis=0, concat_axi...  9.42 us
    pallas_call x1, Pallas kernels, column_topk(): pl.pallas_call(column_topk_kernel, out_shape=jax.ShapeDtypeStruct((TOP_K,...  8.41 us
    all_to_all x1, starting transfers between devices, per_device(): lax.all_to_all(outgoing, ('mass', 'xz', 'core'), split_axis=0, concat_axi...  7.29 us
  transfers between devices with their start and end apart: 2, of which 2 were waited for; matrix products, arithmetic and copies ran while one was open for 0% of the time, Pallas kernels for 0%

profile of v3, /device:TPU:1, one launch (start us, length us, event | category | flops | bytes accessed | tf_op | source)
XLA Modules:
  0.0 164.8 jit_solution(11745647158660980569)
XLA Ops:
  6.5 0.0 copy-start
  6.5 0.0 copy-start.1
  6.5 0.0 all-gather.2.cloned.1.call-start
  6.5 0.7 and_compare_fusion.12
  7.3 1.0 pad_maximum_fusion
  8.3 0.2 slice.59
  8.4 1.1 pad_select_fusion.11
  9.5 0.2 slice.60
  9.7 0.2 pad_select_fusion.10
  9.9 0.2 slice.61
  10.1 0.2 pad_select_fusion.9
  10.2 0.2 slice.62
  10.4 0.2 pad_select_fusion.8
  10.6 0.2 slice.63
  10.7 0.2 pad_select_fusion.7
  10.9 0.2 slice.64
  11.1 0.2 pad_select_fusion.6
  11.3 0.2 slice.65
  11.4 0.2 pad_select_fusion.5
  11.6 0.2 pad_select_fusion.4
  11.8 0.2 pad_select_fusion.3
  12.0 0.2 pad_select_fusion.2
  12.2 0.2 pad_select_fusion.1
  12.4 0.2 pad_select_fusion
  12.6 0.0 copy-done
  12.6 0.4 multiply_reduce_fusion
  13.0 0.0 copy-done.1
  13.0 0.2 convert_reduce_fusion
  13.2 0.4 fusion
  13.6 13.5 %all_to_all.17 = bf16[4,8,8192]{2,1,0:T(8,128)(2,1)} all-to-all(bf16[4,8,8192]{2,1,0:T(8,128)(2,1)S(1)} %fusion), channel_id=1, replica_groups=mesh['mass'=4,'xz'=16,'core'=2] {'mass'}, dimensions={0} | all-to-all | bytes 1048576 | tf_op jit(solution)/shard_map/all_to_all | solution.py:109
  27.1 0.0 all-gather.2.cloned.1.call-update
  27.1 74.7 %all-gather.2.cloned.1.call-done = bf16[1024,8192]{1,0:T(8,128)(2,1)} async-done(((bf16[32,8192]{1,0:T(8,128)(2,1)}), bf16[1024,8192]{1,0:T(8,128)(2,1)}) %all-gather.2.cloned.1.call-update) | async-done | bytes 16777232 | tf_op jit(solution)/shard_map/all_gather | solution.py:110
  101.8 23.6 %convolution_bitcast_fusion.scores_ref = f32[1024,1024]{1,0:T(8,128)} fusion(bf16[1024,8192]{1,0:T(8,128)(2,1)} %all-gather.2.cloned.1.call-done, bf16[1024,8192]{1,0:T(8,128)(2,1)} %param.5), kind=kOutput, calls=%fused_computation.3 | convolution fusion | flops 17179869184 | bytes 37748736 | tf_op jit(solution)/shard_map/dot_general | solution.py:111
  125.5 8.4 %shard_map.46 = f32[16,1024]{1,0:T(8,128)} custom-call(f32[1024,1024]{1,0:T(8,128)} %convolution_bitcast_fusion.scores_ref), custom_call_target="tpu_custom_call" | custom-call | flops 33554432 | bytes 4194304 | tf_op jit(solution)/shard_map/pallas_call | solution.py:85
  133.9 1.0 copy.17
  135.0 0.8 reshape.62
  135.8 7.3 %all-to-all-start.1 = ((f32[128,1,128]{2,1,0:T(1,128)}), f32[128,1,128]{2,1,0:T(1,128)S(1)}, u32[]{:S(2)}, u32[]{:S(2)}) async-start(f32[128,1,128]{2,1,0:T(1,128)} %reshape.62), calls=%async_computation.1 | async-start | bytes 131072 | tf_op jit(solution)/shard_map/all_to_all | solution.py:117
  143.1 9.4 %all-to-all-done.1 = f32[128,1,128]{2,1,0:T(1,128)S(1)} async-done(((f32[128,1,128]{2,1,0:T(1,128)}), f32[128,1,128]{2,1,0:T(1,128)S(1)}, u32[]{:S(2)}, u32[]{:S(2)}) %all-to-all-start.1) | async-done | bytes 65568 | tf_op jit(solution)/shard_map/all_to_all | solution.py:117
  152.6 0.5 broadcast.204
  153.1 0.8 reduce
  153.9 0.2 reshape.63
  154.1 0.2 copy.24
  154.3 0.2 copy.21
  154.5 0.3 reshape.53
  154.8 0.6 gather_fusion
  155.4 0.1 broadcast_select_fusion
  155.5 2.5 %sort_prefixfusion = f32[16,16]{1,0:T(8,128)} fusion(f32[16,512]{1,0:T(8,128)S(1)} %broadcast_select_fusion), kind=kCustom, calls=%top_k.9.sort_prefix | custom fusion | flops 106496 | bytes 33792 | tf_op jit(solution)/shard_map/top_k | solution.py:123
  (12 shorter events, 0.2 us)
Async XLA Ops:
  6.5 6.1 %copy-start = (bf16[16,8192]{1,0:T(8,128)(2,1)S(1)}, bf16[16,8192]{1,0:T(8,128)(2,1)}, u32[]{:S(2)}) copy-start(bf16[16,8192]{1,0:T(8,128)(2,1)} %param.4) | copy-start | bytes 786436
  6.5 6.5 %copy-start.1 = (s32[16,1]{0,1:T(1,128)S(1)}, s32[16,1]{0,1:T(1,128)}, u32[]{:S(2)}) copy-start(s32[16,1]{0,1:T(1,128)} %param.6) | copy-start | bytes 196
  6.5 95.3 %all-gather.2.cloned.1.call-start = ((), (), s32[]{:S(2)}) async-start(), calls=%async_computation.2 | async-start | bytes 17301504 | tf_op jit(solution)/shard_map/all_gather | solution.py:110
  135.8 16.7 %all-to-all-start.1 = ((f32[128,1,128]{2,1,0:T(1,128)}), f32[128,1,128]{2,1,0:T(1,128)S(1)}, u32[]{:S(2)}, u32[]{:S(2)}) async-start(f32[128,1,128]{2,1,0:T(1,128)} %reshape.62), calls=%async_computation.1 | async-start | bytes 131072 | tf_op jit(solution)/shard_map/all_to_all | solution.py:117
Sparse Core Ops, SparseCore 0:
  27.2 74.5 all-gather.1

commit v4 on v3

--- a/solution.py
+++ b/solution.py
@@ -94,9 +94,27 @@
     )(scores)
 
 
+def ring_gather(block, axis):
+    size = 4
+    flat = block.reshape(-1, block.shape[-1])
+    half = flat.shape[0] // 2
+    forward = [(i, (i + 1) % size) for i in range(size)]
+    backward = [(i, (i - 1) % size) for i in range(size)]
+    from_minus = lax.ppermute(flat, axis, forward)
+    from_plus = lax.ppermute(flat, axis, backward)
+    far_first = lax.ppermute(from_minus[:half], axis, forward)
+    far_second = lax.ppermute(from_plus[half:], axis, backward)
+    far = jnp.concatenate([far_first, far_second], axis=0)
+    stacked = jnp.stack([flat, from_plus, far, from_minus])
+    return stacked.reshape((size,) + block.shape)
+
+
 def per_device(queries, library, routes, offsets):
     mass_count = lax.axis_size("mass")
-    shard_count = lax.axis_size("xz") * lax.axis_size("core")
+    x_count = lax.axis_size("x")
+    z_count = lax.axis_size("z")
+    core_count = lax.axis_size("core")
+    shard_count = x_count * z_count * core_count
     query_count = queries.shape[0]
     capacity = query_count // 2
     spectra = shifted_spectra(queries, offsets)
@@ -107,15 +125,42 @@
     ).astype(jnp.bfloat16)
     packed = jnp.dot(selector, spectra, preferred_element_type=jnp.float32).astype(jnp.bfloat16)
     arrived = lax.all_to_all(packed, "mass", split_axis=0, concat_axis=0, tiled=True)
-    gathered = lax.all_gather(arrived, ("xz", "core"), axis=0, tiled=True)
-    scores_t = lax.dot_general(
-        library, gathered, (((1,), (1,)), ((), ())), preferred_element_type=jnp.float32
+    part = arrived.shape[0] // 2
+    part_a = ring_gather(ring_gather(arrived[:part], "x"), "z")
+    part_b = ring_gather(ring_gather(arrived[part:], "z"), "x")
+    own_side = jnp.concatenate(
+        [part_a.reshape(-1, arrived.shape[1]), part_b.reshape(-1, arrived.shape[1])], axis=0
     )
-    local_best = column_topk(scores_t)
-    outgoing = local_best.T.reshape(shard_count, mass_count, capacity, TOP_K)
-    outgoing = outgoing.transpose(1, 0, 2, 3).reshape(-1, capacity, TOP_K)
+    partner = [(core, core_count - 1 - core) for core in range(core_count)]
+    other_side = lax.ppermute(own_side, "core", partner)
+    own_best = column_topk(
+        lax.dot_general(
+            library, own_side, (((1,), (1,)), ((), ())), preferred_element_type=jnp.float32
+        )
+    )
+    other_best = column_topk(
+        lax.dot_general(
+            library, other_side, (((1,), (1,)), ((), ())), preferred_element_type=jnp.float32
+        )
+    )
+    local_best = jnp.concatenate([own_best, other_best], axis=1).T
+    row = jnp.arange(local_best.shape[0], dtype=jnp.int32)
+    slot = row % capacity
+    source = row // capacity
+    source_core = source % core_count
+    source_z = source // core_count % z_count
+    source_x = source // (core_count * z_count) % x_count
+    source_mass = source // shard_count
+    step_x = (source_x - lax.axis_index("x")) % x_count
+    step_z = (source_z - lax.axis_index("z")) % z_count
+    side = jnp.where(source_core == lax.axis_index("core"), 0, 1)
+    in_part = source_mass * capacity + slot
+    column_a = (step_z * x_count + step_x) * part + in_part
+    column_b = (x_count * z_count + step_x * z_count + step_z) * part + in_part - part
+    column = side * (shard_count // core_count) * 2 * part + jnp.where(in_part < part, column_a, column_b)
+    outgoing = jnp.take(local_best, column, axis=0).reshape(-1, capacity, TOP_K)
     received = lax.all_to_all(
-        outgoing, ("mass", "xz", "core"), split_axis=0, concat_axis=0, tiled=True
+        outgoing, ("mass", "x", "z", "core"), split_axis=0, concat_axis=0, tiled=True
     )
     received = received.reshape(mass_count, shard_count, capacity, TOP_K)
     received = received.transpose(0, 2, 1, 3).reshape(mass_count * capacity, -1)
@@ -126,11 +171,12 @@
 def solution(mesh):
     mass_count, shard_count = mesh.devices.shape
     core_count = 2
+    side = 4
     split_mesh = Mesh(
-        mesh.devices.reshape(mass_count, shard_count // core_count, core_count),
-        ("mass", "xz", "core"),
+        mesh.devices.reshape(mass_count, side, shard_count // (side * core_count), core_count),
+        ("mass", "x", "z", "core"),
     )
-    spread = ("mass", "xz", "core")
+    spread = ("mass", "x", "z", "core")
     placed = (P(spread, None), P(spread, None), P(spread, None), P(spread))
     return jax.shard_map(
         per_device,

time: 165 us -> 155 us (0.939)
  waiting for transfers between devices: 84.2 us -> 36.4 us
  starting transfers between devices: 7.29 us -> 33.1 us
  other arithmetic: 8.57 us -> 22.2 us
  between operations: 13.6 us -> 0.42 us
  matrix products: 24 us -> 32 us
  local copies, waits for them, and re-layouts: 5.29 us -> 7.72 us
    all_gather x1 -> x0, waiting for transfers between devices: 74.7 us -> none  [per_device(): gathered = lax.all_gather(arrived, ('xz', 'core'), axis=0, tiled=True)]
    ppermute x0 -> x17, starting transfers between devices: none -> 28.2 us  [the longest x4 10.5 us: ring_gather(): far_second = lax.ppermute(from_plus[half:], axis, backward)]
    ppermute x0 -> x17, waiting for transfers between devices: none -> 27 us  [the longest x4 21.1 us: ring_gather(): from_minus = lax.ppermute(flat, axis, forward)]
    dot_general x1 -> x2, matrix products: 23.6 us -> 31.6 us  [the longest x1 15.8 us: per_device(): lax.dot_general(library, own_side, (((1,), (1,)), ((), ())), preferred_el...]
    concatenate x0 -> x1, other arithmetic: none -> 7.67 us  [per_device(): jnp.concatenate([part_a.reshape(-1, arrived.shape[1]), part_b.reshape(-1,...]
    another operation x0 -> x8, other arithmetic: none -> 4.93 us  [ring_gather(): stacked = jnp.stack([flat, from_plus, far, from_minus])]
    gather x0 -> x1, local copies, waits for them, and re-layouts: none -> 2.81 us  [per_device(): outgoing = jnp.take(local_best, column, axis=0).reshape(-1, capacity, TOP_K)]
    all_to_all x1, starting transfers between devices: 7.29 us -> 4.86 us  [per_device(): lax.all_to_all(outgoing, ('mass', 'x', 'z', 'core'), split_axis=0, concat...]
  transfers between devices with their start and end apart: 2 -> 18, of which waited for: 2 -> 5; matrix products, arithmetic and copies ran while one was open for 0% -> 12% of each run, Pallas kernels for 0% -> 3%
where the time goes in v4:
time: 155 us
  waiting for transfers between devices  36.4 us (23%)
  starting transfers between devices  33.1 us (21%)
  matrix products  32 us (21%)
  other arithmetic  22.2 us (14%)
  blocking collectives  13.4 us (9%)
  Pallas kernels  9.67 us (6%)
  local copies, waits for them, and re-layouts  7.72 us (5%)
    ppermute x4, waiting for transfers between devices, ring_gather(): from_minus = lax.ppermute(flat, axis, forward)  21.1 us
    dot_general x1, matrix products, per_device(): lax.dot_general(library, own_side, (((1,), (1,)), ((), ())), preferred_el...  15.8 us
    dot_general x1, matrix products, per_device(): lax.dot_general(library, other_side, (((1,), (1,)), ((), ())), preferred_...  15.8 us
    all_to_all x1, blocking collectives, per_device(): lax.all_to_all(packed, 'mass', split_axis=0, concat_axis=0, tiled=True)  13.4 us
    ppermute x4, starting transfers between devices, ring_gather(): far_second = lax.ppermute(from_plus[half:], axis, backward)  10.5 us
    pallas_call x2, Pallas kernels, column_topk(): pl.pallas_call(column_topk_kernel, out_shape=jax.ShapeDtypeStruct((TOP_K,...  9.67 us
    all_to_all x1, waiting for transfers between devices, per_device(): lax.all_to_all(outgoing, ('mass', 'x', 'z', 'core'), split_axis=0, concat...  9.42 us
    ppermute x4, starting transfers between devices, ring_gather(): from_plus = lax.ppermute(flat, axis, backward)  8.91 us
  transfers between devices with their start and end apart: 18, of which 5 were waited for; matrix products, arithmetic and copies ran while one was open for 12% of the time, Pallas kernels for 3%

profile of v4, /device:TPU:1, one launch (start us, length us, event | category | flops | bytes accessed | tf_op | source)
XLA Modules:
  0.0 154.9 jit_solution(8757362861455230892)
XLA Ops:
  0.0 0.7 and_compare_fusion.12
  0.7 1.0 pad_maximum_fusion.5
  1.7 0.2 slice.109
  1.8 1.1 pad_select_fusion.11
  3.3 0.2 slice.111
  3.6 0.2 slice.112
  6.2 0.4 multiply_reduce_fusion
  6.5 0.2 convert_reduce_fusion
  6.7 0.4 fusion
  7.1 13.4 %all_to_all.14 = bf16[4,8,8192]{2,1,0:T(8,128)(2,1)S(1)} all-to-all(bf16[4,8,8192]{2,1,0:T(8,128)(2,1)S(1)} %fusion), channel_id=1, replica_groups=mesh['mass'=4,'x'=4,'z'=4,'core'=2] {'mass'}, dimensions={0} | all-to-all | bytes 1048576 | tf_op jit(solution)/shard_map/all_to_all | solution.py:127
  20.6 1.3 collective-permute-start.1
  21.9 1.5 collective-permute-start
  23.3 1.6 %collective-permute-start.9 = (bf16[16,8192]{1,0:T(8,128)(2,1)S(1)}, bf16[16,8192]{1,0:T(8,128)(2,1)S(1)}, u32[]{:S(2)}, u32[]{:S(2)}) collective-permute-start(bf16[16,8192]{1,0:T(8,128)(2,1)S(1)} %get-tuple-element.13), channel_id=1, source_target_pairs={{0,2},{2,4},{4,6},{6,0},{1,3},{3,5},{5,7},{7,1},{8,10},{10,12},{12... | collective-permute-start | bytes 786440 | tf_op jit(solution)/shard_map/ppermute | solution.py:103
  25.0 2.1 %collective-permute-start.8 = (bf16[16,8192]{1,0:T(8,128)(2,1)S(1)}, bf16[16,8192]{1,0:T(8,128)(2,1)S(1)}, u32[]{:S(2)}, u32[]{:S(2)}) collective-permute-start(bf16[16,8192]{1,0:T(8,128)(2,1)S(1)} %get-tuple-element.13), channel_id=1, source_target_pairs={{0,6},{2,0},{4,2},{6,4},{1,7},{3,1},{5,3},{7,5},{8,14},{10,8},{12,... | collective-permute-start | bytes 786440 | tf_op jit(solution)/shard_map/ppermute | solution.py:104
  27.1 0.8 collective-permute-done.1
  28.1 2.7 %collective-permute-start.3 = (bf16[8,8192]{1,0:T(8,128)(2,1)S(1)}, bf16[8,8192]{1,0:T(8,128)(2,1)S(1)}, u32[]{:S(2)}, u32[]{:S(2)}) collective-permute-start(bf16[8,8192]{1,0:T(8,128)(2,1)S(1)} %slice.125), channel_id=1, source_target_pairs={{0,24},{8,0},{16,8},{24,16},{1,25},{9,1},{17,9},{25,17},{2,26},{10... | collective-permute-start | bytes 393224 | tf_op jit(solution)/shard_map/ppermute | solution.py:106
  30.8 0.6 collective-permute-done.9
  31.4 1.1 collective-permute-start.10
  32.5 2.2 %collective-permute-start.11 = (bf16[8,8192]{1,0:T(8,128)(2,1)S(1)}, bf16[8,8192]{1,0:T(8,128)(2,1)S(1)}, u32[]{:S(2)}, u32[]{:S(2)}) collective-permute-start(bf16[8,8192]{1,0:T(8,128)(2,1)S(1)} %slice.130), channel_id=1, source_target_pairs={{0,6},{2,0},{4,2},{6,4},{1,7},{3,1},{5,3},{7,5},{8,14},{10,8},{12,... | collective-permute-start | bytes 393224 | tf_op jit(solution)/shard_map/ppermute | solution.py:106
  35.0 2.7 %collective-permute-start.4 = (bf16[64,8192]{1,0:T(8,128)(2,1)S(1)}, bf16[64,8192]{1,0:T(8,128)(2,1)S(1)}, u32[]{:S(2)}, u32[]{:S(2)}) collective-permute-start(bf16[64,8192]{1,0:T(8,128)(2,1)S(1)} %bitcast.63), channel_id=1, source_target_pairs={{0,6},{2,0},{4,2},{6,4},{1,7},{3,1},{5,3},{7,5},{8,14},{10,8},{12,... | collective-permute-start | bytes 3145736 | tf_op jit(solution)/shard_map/ppermute | solution.py:104
  37.9 2.7 %collective-permute-start.12 = (bf16[64,8192]{1,0:T(8,128)(2,1)S(1)}, bf16[64,8192]{1,0:T(8,128)(2,1)S(1)}, u32[]{:S(2)}, u32[]{:S(2)}) collective-permute-start(bf16[64,8192]{1,0:T(8,128)(2,1)S(1)} %bitcast.66), channel_id=1, source_target_pairs={{0,24},{8,0},{16,8},{24,16},{1,25},{9,1},{17,9},{25,17},{2,26},{10... | collective-permute-start | bytes 3145736 | tf_op jit(solution)/shard_map/ppermute | solution.py:104
  40.6 19.6 %collective-permute-done.5 = bf16[64,8192]{1,0:T(8,128)(2,1)S(1)} collective-permute-done((bf16[64,8192]{1,0:T(8,128)(2,1)S(1)}, bf16[64,8192]{1,0:T(8,128)(2,1)S(1)}, u32[]{:S(2)}, u32[]{:S(2)}) %collective-permute-start.5) | collective-permute-done | bytes 1048608 | tf_op jit(solution)/shard_map/ppermute | solution.py:103
  60.4 2.7 %collective-permute-start.7 = (bf16[32,8192]{1,0:T(8,128)(2,1)S(1)}, bf16[32,8192]{1,0:T(8,128)(2,1)S(1)}, u32[]{:S(2)}, u32[]{:S(2)}) collective-permute-start(bf16[32,8192]{1,0:T(8,128)(2,1)S(1)} %slice.127), channel_id=1, source_target_pairs={{0,6},{2,0},{4,2},{6,4},{1,7},{3,1},{5,3},{7,5},{8,14},{10,8},{12,... | collective-permute-start | bytes 1572872 | tf_op jit(solution)/shard_map/ppermute | solution.py:106
  63.3 2.9 %collective-permute-start.15 = (bf16[32,8192]{1,0:T(8,128)(2,1)S(1)}, bf16[32,8192]{1,0:T(8,128)(2,1)S(1)}, u32[]{:S(2)}, u32[]{:S(2)}) collective-permute-start(bf16[32,8192]{1,0:T(8,128)(2,1)S(1)} %slice.132), channel_id=1, source_target_pairs={{0,24},{8,0},{16,8},{24,16},{1,25},{9,1},{17,9},{25,17},{2,26},{10... | collective-permute-start | bytes 1572872 | tf_op jit(solution)/shard_map/ppermute | solution.py:106
  66.2 5.9 %collective-permute-done.6 = bf16[32,8192]{1,0:T(8,128)(2,1)S(1)} collective-permute-done((bf16[32,8192]{1,0:T(8,128)(2,1)S(1)}, bf16[32,8192]{1,0:T(8,128)(2,1)S(1)}, u32[]{:S(2)}, u32[]{:S(2)}) %collective-permute-start.6) | collective-permute-done | bytes 524320 | tf_op jit(solution)/shard_map/ppermute | solution.py:105
  72.1 2.2 %pad_maximum_fusion.1 = bf16[4,64,8192]{2,1,0:T(8,128)(2,1)} fusion(bf16[1,64,8192]{2,1,0:T(8,128)(2,1)S(1)} %bitcast.68, bf16[1,64,8192]{2,1,0:T(8,128)(2,1)S(1)} %maximum_bitcast_fusion, bf16[1,64,8192]{2,1,0:T(8,128)(2,1)S(1)} %bitcast.69, bf16[1,64,8192]{2,1,0:T(8,128)(2,1)S(1)} %bitcast.64), kind=kLoop, calls=%fused_computation.5 | loop fusion | flops 6291456 | bytes 8388608 | tf_op jit(solution)/shard_map/stack | solution.py:108
  74.4 2.2 %pad_maximum_fusion.2 = bf16[4,64,8192]{2,1,0:T(8,128)(2,1)} fusion(bf16[1,64,8192]{2,1,0:T(8,128)(2,1)S(1)} %bitcast.70, bf16[1,64,8192]{2,1,0:T(8,128)(2,1)S(1)} %maximum_bitcast_fusion.1, bf16[1,64,8192]{2,1,0:T(8,128)(2,1)S(1)} %bitcast.71, bf16[1,64,8192]{2,1,0:T(8,128)(2,1)S(1)} %bitcast.67), kind=kLoop, calls=%fused_computation.6 | loop fusion | flops 6291456 | bytes 8388608 | tf_op jit(solution)/shard_map/stack | solution.py:108
  76.7 7.7 %pad_maximum_fusion = bf16[512,8192]{1,0:T(8,128)(2,1)} fusion(bf16[256,8192]{1,0:T(8,128)(2,1)} %bitcast.60, bf16[256,8192]{1,0:T(8,128)(2,1)} %bitcast.58), kind=kLoop, calls=%fused_computation.4 | loop fusion | flops 16777216 | bytes 16777216 | tf_op jit(solution)/shard_map/concatenate | solution.py:131
  84.4 4.4 %collective-permute-start.16 = (bf16[512,8192]{1,0:T(8,128)(2,1)}, bf16[512,8192]{1,0:T(8,128)(2,1)}, u32[]{:S(2)}, u32[]{:S(2)}) collective-permute-start(bf16[512,8192]{1,0:T(8,128)(2,1)} %pad_maximum_fusion), channel_id=1, source_target_pairs={{0,1},{1,0},{2,3},{3,2},{4,5},{5,4},{6,7},{7,6},{8,9},{9,8},{10,11... | collective-permute-start | bytes 25165832 | tf_op jit(solution)/shard_map/ppermute | solution.py:135
  89.0 15.8 %convolution_bitcast_fusion.1.scores_ref = f32[1024,512]{1,0:T(8,128)} fusion(bf16[1024,8192]{1,0:T(8,128)(2,1)} %param.5, bf16[256,8192]{1,0:T(8,128)(2,1)} %bitcast.61, bf16[256,8192]{1,0:T(8,128)(2,1)} %bitcast.59), kind=kOutput, calls=%fused_computation.8 | convolution fusion | flops 8606711808 | bytes 27262976 | tf_op jit(solution)/shard_map/dot_general | solution.py:137
  104.9 4.8 %shard_map.46 = f32[16,512]{1,0:T(8,128)} custom-call(f32[1024,512]{1,0:T(8,128)} %convolution_bitcast_fusion.1.scores_ref), custom_call_target="tpu_custom_call" | custom-call | flops 16777216 | bytes 2097152 | tf_op jit(solution)/shard_map/pallas_call | solution.py:85
  109.7 15.8 %convolution_bitcast_fusion.scores_ref = f32[1024,512]{1,0:T(8,128)} fusion(bf16[512,8192]{1,0:T(8,128)(2,1)} %collective-permute-done.16, bf16[1024,8192]{1,0:T(8,128)(2,1)} %param.5), kind=kOutput, calls=%fused_computation.7 | convolution fusion | flops 8589934592 | bytes 27262976 | tf_op jit(solution)/shard_map/dot_general | solution.py:142
  125.5 4.8 %shard_map.47 = f32[16,512]{1,0:T(8,128)} custom-call(f32[1024,512]{1,0:T(8,128)} %convolution_bitcast_fusion.scores_ref), custom_call_target="tpu_custom_call" | custom-call | flops 16777216 | bytes 2097152 | tf_op jit(solution)/shard_map/pallas_call | solution.py:85
  130.3 0.8 maximum_bitcast_fusion.4
  131.1 0.2 copy.30
  131.3 2.8 %gather_fusion = f32[1024,16]{1,0:T(8,128)S(1)} fusion(f32[1024,16]{1,0:T(8,128)S(1)} %copy.30, s32[1024]{0:T(1024)S(1)} %broadcast_clamp_fusion), kind=kCustom, calls=%fused_computation | custom fusion | bytes 135168 | tf_op jit(solution)/shard_map/jit(_take)/gather | solution.py:161
  134.1 0.2 bitcast_select_fusion
  134.3 0.8 reshape.463
  135.2 4.9 %all-to-all-start.1 = ((f32[128,1,128]{2,1,0:T(1,128)}), f32[128,1,128]{2,1,0:T(1,128)S(1)}, u32[]{:S(2)}, u32[]{:S(2)}) async-start(f32[128,1,128]{2,1,0:T(1,128)} %reshape.463), calls=%async_computation.1 | async-start | bytes 131072 | tf_op jit(solution)/shard_map/all_to_all | solution.py:162
  140.1 9.4 %all-to-all-done.1 = f32[128,1,128]{2,1,0:T(1,128)S(1)} async-done(((f32[128,1,128]{2,1,0:T(1,128)}), f32[128,1,128]{2,1,0:T(1,128)S(1)}, u32[]{:S(2)}, u32[]{:S(2)}) %all-to-all-start.1) | async-done | bytes 65568 | tf_op jit(solution)/shard_map/all_to_all | solution.py:162
  149.5 0.5 broadcast.949
  150.0 0.8 reduce
  150.8 0.2 reshape.464
  151.0 0.2 copy.35
  151.2 0.2 copy.32
  151.5 0.3 reshape.446
  151.7 0.6 gather_fusion.1
  152.4 2.5 %sort_prefixfusion = f32[16,16]{1,0:T(8,128)} fusion(f32[16,512]{1,0:T(8,128)S(1)} %broadcast_select_fusion), kind=kCustom, calls=%top_k.9.sort_prefix | custom fusion | flops 106496 | bytes 33792 | tf_op jit(solution)/shard_map/top_k | solution.py:168
  (70 shorter events, 4.2 us)
Async XLA Ops:
  5.2 1.0 copy-start
  5.3 1.3 copy-start.2
  20.6 7.3 %collective-permute-start.1 = (bf16[16,8192]{1,0:T(8,128)(2,1)S(1)}, bf16[16,8192]{1,0:T(8,128)(2,1)S(1)}, u32[]{:S(2)}, u32[]{:S(2)}) collective-permute-start(bf16[16,8192]{1,0:T(8,128)(2,1)S(1)} %get-tuple-element.12), channel_id=1, source_target_pairs={{0,8},{8,16},{16,24},{24,0},{1,9},{9,17},{17,25},{25,1},{2,10},{10... | collective-permute-start | bytes 786440 | tf_op jit(solution)/shard_map/ppermute | solution.py:103
  21.9 6.2 %collective-permute-start = (bf16[16,8192]{1,0:T(8,128)(2,1)S(1)}, bf16[16,8192]{1,0:T(8,128)(2,1)S(1)}, u32[]{:S(2)}, u32[]{:S(2)}) collective-permute-start(bf16[16,8192]{1,0:T(8,128)(2,1)S(1)} %get-tuple-element.12), channel_id=1, source_target_pairs={{0,24},{8,0},{16,8},{24,16},{1,25},{9,1},{17,9},{25,17},{2,26},{10... | collective-permute-start | bytes 786440 | tf_op jit(solution)/shard_map/ppermute | solution.py:104
  23.3 8.1 %collective-permute-start.9 = (bf16[16,8192]{1,0:T(8,128)(2,1)S(1)}, bf16[16,8192]{1,0:T(8,128)(2,1)S(1)}, u32[]{:S(2)}, u32[]{:S(2)}) collective-permute-start(bf16[16,8192]{1,0:T(8,128)(2,1)S(1)} %get-tuple-element.13), channel_id=1, source_target_pairs={{0,2},{2,4},{4,6},{6,0},{1,3},{3,5},{5,7},{7,1},{8,10},{10,12},{12... | collective-permute-start | bytes 786440 | tf_op jit(solution)/shard_map/ppermute | solution.py:103
  25.0 7.5 %collective-permute-start.8 = (bf16[16,8192]{1,0:T(8,128)(2,1)S(1)}, bf16[16,8192]{1,0:T(8,128)(2,1)S(1)}, u32[]{:S(2)}, u32[]{:S(2)}) collective-permute-start(bf16[16,8192]{1,0:T(8,128)(2,1)S(1)} %get-tuple-element.13), channel_id=1, source_target_pairs={{0,6},{2,0},{4,2},{6,4},{1,7},{3,1},{5,3},{7,5},{8,14},{10,8},{12,... | collective-permute-start | bytes 786440 | tf_op jit(solution)/shard_map/ppermute | solution.py:104
  27.9 6.8 %collective-permute-start.2 = (bf16[8,8192]{1,0:T(8,128)(2,1)S(1)}, bf16[8,8192]{1,0:T(8,128)(2,1)S(1)}, u32[]{:S(2)}, u32[]{:S(2)}) collective-permute-start(bf16[8,8192]{1,0:T(8,128)(2,1)S(1)} %slice.124), channel_id=1, source_target_pairs={{0,8},{8,16},{16,24},{24,0},{1,9},{9,17},{17,25},{25,1},{2,10},{10... | collective-permute-start | bytes 393224 | tf_op jit(solution)/shard_map/ppermute | solution.py:105
  28.1 6.7 %collective-permute-start.3 = (bf16[8,8192]{1,0:T(8,128)(2,1)S(1)}, bf16[8,8192]{1,0:T(8,128)(2,1)S(1)}, u32[]{:S(2)}, u32[]{:S(2)}) collective-permute-start(bf16[8,8192]{1,0:T(8,128)(2,1)S(1)} %slice.125), channel_id=1, source_target_pairs={{0,24},{8,0},{16,8},{24,16},{1,25},{9,1},{17,9},{25,17},{2,26},{10... | collective-permute-start | bytes 393224 | tf_op jit(solution)/shard_map/ppermute | solution.py:106
  31.4 6.2 %collective-permute-start.10 = (bf16[8,8192]{1,0:T(8,128)(2,1)S(1)}, bf16[8,8192]{1,0:T(8,128)(2,1)S(1)}, u32[]{:S(2)}, u32[]{:S(2)}) collective-permute-start(bf16[8,8192]{1,0:T(8,128)(2,1)S(1)} %slice.129), channel_id=1, source_target_pairs={{0,2},{2,4},{4,6},{6,0},{1,3},{3,5},{5,7},{7,1},{8,10},{10,12},{12... | collective-permute-start | bytes 393224 | tf_op jit(solution)/shard_map/ppermute | solution.py:105
  32.5 5.1 %collective-permute-start.11 = (bf16[8,8192]{1,0:T(8,128)(2,1)S(1)}, bf16[8,8192]{1,0:T(8,128)(2,1)S(1)}, u32[]{:S(2)}, u32[]{:S(2)}) collective-permute-start(bf16[8,8192]{1,0:T(8,128)(2,1)S(1)} %slice.130), channel_id=1, source_target_pairs={{0,6},{2,0},{4,2},{6,4},{1,7},{3,1},{5,3},{7,5},{8,14},{10,8},{12,... | collective-permute-start | bytes 393224 | tf_op jit(solution)/shard_map/ppermute | solution.py:106
  34.9 25.3 %collective-permute-start.5 = (bf16[64,8192]{1,0:T(8,128)(2,1)S(1)}, bf16[64,8192]{1,0:T(8,128)(2,1)S(1)}, u32[]{:S(2)}, u32[]{:S(2)}) collective-permute-start(bf16[64,8192]{1,0:T(8,128)(2,1)S(1)} %bitcast.62), channel_id=1, source_target_pairs={{0,2},{2,4},{4,6},{6,0},{1,3},{3,5},{5,7},{7,1},{8,10},{10,12},{12... | collective-permute-start | bytes 3145736 | tf_op jit(solution)/shard_map/ppermute | solution.py:103
  35.0 25.3 %collective-permute-start.4 = (bf16[64,8192]{1,0:T(8,128)(2,1)S(1)}, bf16[64,8192]{1,0:T(8,128)(2,1)S(1)}, u32[]{:S(2)}, u32[]{:S(2)}) collective-permute-start(bf16[64,8192]{1,0:T(8,128)(2,1)S(1)} %bitcast.63), channel_id=1, source_target_pairs={{0,6},{2,0},{4,2},{6,4},{1,7},{3,1},{5,3},{7,5},{8,14},{10,8},{12,... | collective-permute-start | bytes 3145736 | tf_op jit(solution)/shard_map/ppermute | solution.py:104
  37.8 25.3 %collective-permute-start.13 = (bf16[64,8192]{1,0:T(8,128)(2,1)S(1)}, bf16[64,8192]{1,0:T(8,128)(2,1)S(1)}, u32[]{:S(2)}, u32[]{:S(2)}) collective-permute-start(bf16[64,8192]{1,0:T(8,128)(2,1)S(1)} %bitcast.65), channel_id=1, source_target_pairs={{0,8},{8,16},{16,24},{24,0},{1,9},{9,17},{17,25},{25,1},{2,10},{10... | collective-permute-start | bytes 3145736 | tf_op jit(solution)/shard_map/ppermute | solution.py:103
  37.9 25.3 %collective-permute-start.12 = (bf16[64,8192]{1,0:T(8,128)(2,1)S(1)}, bf16[64,8192]{1,0:T(8,128)(2,1)S(1)}, u32[]{:S(2)}, u32[]{:S(2)}) collective-permute-start(bf16[64,8192]{1,0:T(8,128)(2,1)S(1)} %bitcast.66), channel_id=1, source_target_pairs={{0,24},{8,0},{16,8},{24,16},{1,25},{9,1},{17,9},{25,17},{2,26},{10... | collective-permute-start | bytes 3145736 | tf_op jit(solution)/shard_map/ppermute | solution.py:104
  60.2 11.8 %collective-permute-start.6 = (bf16[32,8192]{1,0:T(8,128)(2,1)S(1)}, bf16[32,8192]{1,0:T(8,128)(2,1)S(1)}, u32[]{:S(2)}, u32[]{:S(2)}) collective-permute-start(bf16[32,8192]{1,0:T(8,128)(2,1)S(1)} %slice.126), channel_id=1, source_target_pairs={{0,2},{2,4},{4,6},{6,0},{1,3},{3,5},{5,7},{7,1},{8,10},{10,12},{12... | collective-permute-start | bytes 1572872 | tf_op jit(solution)/shard_map/ppermute | solution.py:105
  60.4 11.7 %collective-permute-start.7 = (bf16[32,8192]{1,0:T(8,128)(2,1)S(1)}, bf16[32,8192]{1,0:T(8,128)(2,1)S(1)}, u32[]{:S(2)}, u32[]{:S(2)}) collective-permute-start(bf16[32,8192]{1,0:T(8,128)(2,1)S(1)} %slice.127), channel_id=1, source_target_pairs={{0,6},{2,0},{4,2},{6,4},{1,7},{3,1},{5,3},{7,5},{8,14},{10,8},{12,... | collective-permute-start | bytes 1572872 | tf_op jit(solution)/shard_map/ppermute | solution.py:106
  63.1 11.2 %collective-permute-start.14 = (bf16[32,8192]{1,0:T(8,128)(2,1)S(1)}, bf16[32,8192]{1,0:T(8,128)(2,1)S(1)}, u32[]{:S(2)}, u32[]{:S(2)}) collective-permute-start(bf16[32,8192]{1,0:T(8,128)(2,1)S(1)} %slice.131), channel_id=1, source_target_pairs={{0,8},{8,16},{16,24},{24,0},{1,9},{9,17},{17,25},{25,1},{2,10},{10... | collective-permute-start | bytes 1572872 | tf_op jit(solution)/shard_map/ppermute | solution.py:105
  63.3 11.1 %collective-permute-start.15 = (bf16[32,8192]{1,0:T(8,128)(2,1)S(1)}, bf16[32,8192]{1,0:T(8,128)(2,1)S(1)}, u32[]{:S(2)}, u32[]{:S(2)}) collective-permute-start(bf16[32,8192]{1,0:T(8,128)(2,1)S(1)} %slice.132), channel_id=1, source_target_pairs={{0,24},{8,0},{16,8},{24,16},{1,25},{9,1},{17,9},{25,17},{2,26},{10... | collective-permute-start | bytes 1572872 | tf_op jit(solution)/shard_map/ppermute | solution.py:106
  84.4 25.3 %collective-permute-start.16 = (bf16[512,8192]{1,0:T(8,128)(2,1)}, bf16[512,8192]{1,0:T(8,128)(2,1)}, u32[]{:S(2)}, u32[]{:S(2)}) collective-permute-start(bf16[512,8192]{1,0:T(8,128)(2,1)} %pad_maximum_fusion), channel_id=1, source_target_pairs={{0,1},{1,0},{2,3},{3,2},{4,5},{5,4},{6,7},{7,6},{8,9},{9,8},{10,11... | collective-permute-start | bytes 25165832 | tf_op jit(solution)/shard_map/ppermute | solution.py:135
  109.7 20.6 %copy-start.1 = (f32[16,512]{1,0:T(8,128)S(1)}, f32[16,512]{1,0:T(8,128)}, u32[]{:S(2)}) copy-start(f32[16,512]{1,0:T(8,128)} %shard_map.46) | copy-start | bytes 98308
  135.2 14.3 %all-to-all-start.1 = ((f32[128,1,128]{2,1,0:T(1,128)}), f32[128,1,128]{2,1,0:T(1,128)S(1)}, u32[]{:S(2)}, u32[]{:S(2)}) async-start(f32[128,1,128]{2,1,0:T(1,128)} %reshape.463), calls=%async_computation.1 | async-start | bytes 131072 | tf_op jit(solution)/shard_map/all_to_all | solution.py:162

commit v5 on v4

--- a/solution.py
+++ b/solution.py
@@ -92,6 +92,98 @@
             flops=2 * TOP_K * rows * columns, transcendentals=0, bytes_accessed=4 * rows * columns
         ),
     )(scores)
+
+
+LIB_BLOCK = 256
+BIN_BLOCK = 1024
+
+
+def score_topk_kernel(library_ref, first_ref, second_ref, out_ref, scores_ref, kept_ref):
+    block = pl.program_id(0)
+    slots = first_ref.shape[0]
+    bins = first_ref.shape[1]
+
+    @pl.when(block == 0)
+    def _():
+        kept_ref[...] = jnp.full(kept_ref.shape, -jnp.inf, jnp.float32)
+
+    for piece, query_ref in enumerate((first_ref, second_ref)):
+        scores_ref[...] = jnp.zeros(scores_ref.shape, jnp.float32)
+
+        def accumulate(chunk, carry):
+            lo = pl.multiple_of(chunk * BIN_BLOCK, BIN_BLOCK)
+            scores_ref[...] += lax.dot_general(
+                library_ref[:, pl.ds(lo, BIN_BLOCK)],
+                query_ref[:, pl.ds(lo, BIN_BLOCK)],
+                (((1,), (1,)), ((), ())),
+                preferred_element_type=jnp.float32,
+            )
+            return carry
+
+        lax.fori_loop(0, bins // BIN_BLOCK, accumulate, 0)
+        for lane_block in range(slots // LANES):
+            insert_rows_at(scores_ref, kept_ref, lane_block * LANES, piece * slots + lane_block * LANES)
+
+    @pl.when(block == pl.num_programs(0) - 1)
+    def _():
+        for column in range(0, 2 * slots, LANES):
+            lanes = pl.ds(column, LANES)
+            kept = [kept_ref[k, :, lanes] for k in range(TOP_K)]
+            shift = SUBLANES // 2
+            while shift >= 1:
+                rolled = [pltpu.roll(kept[k], shift, 0) for k in range(TOP_K)]
+                kept = merge_sorted(kept, rolled)
+                shift //= 2
+            for k in range(TOP_K):
+                out_ref[pl.ds(k, 1), lanes] = kept[k][0:1, :]
+
+
+def insert_rows_at(scores_ref, kept_ref, score_column, kept_column):
+    score_lanes = pl.ds(score_column, LANES)
+    kept_lanes = pl.ds(kept_column, LANES)
+    kept = tuple(kept_ref[k, :, kept_lanes] for k in range(TOP_K))
+
+    def insert(step, kept):
+        start = pl.multiple_of(step * SUBLANES, SUBLANES)
+        value = scores_ref[pl.ds(start, SUBLANES), score_lanes]
+        updated = []
+        for k in range(TOP_K):
+            updated.append(jnp.maximum(kept[k], value))
+            value = jnp.minimum(kept[k], value)
+        return tuple(updated)
+
+    kept = lax.fori_loop(0, scores_ref.shape[0] // SUBLANES, insert, kept, unroll=8)
+    for k in range(TOP_K):
+        kept_ref[k, :, kept_lanes] = kept[k]
+
+
+def score_topk(library, first, second):
+    rows, bins = library.shape
+    slots = first.shape[0]
+    resident = lambda block: (0, 0)
+    return pl.pallas_call(
+        score_topk_kernel,
+        out_shape=jax.ShapeDtypeStruct((TOP_K, 2 * slots), jnp.float32),
+        grid=(rows // LIB_BLOCK,),
+        in_specs=[
+            pl.BlockSpec((LIB_BLOCK, bins), lambda block: (block, 0)),
+            pl.BlockSpec((slots, bins), resident, pipeline_mode=pl.Buffered(1)),
+            pl.BlockSpec((slots, bins), resident, pipeline_mode=pl.Buffered(1)),
+        ],
+        out_specs=pl.BlockSpec((TOP_K, 2 * slots), resident),
+        scratch_shapes=[
+            pltpu.VMEM((LIB_BLOCK, slots), jnp.float32),
+            pltpu.VMEM((TOP_K, SUBLANES, 2 * slots), jnp.float32),
+        ],
+        compiler_params=pltpu.CompilerParams(
+            dimension_semantics=("arbitrary",), vmem_limit_bytes=48 * 1024 * 1024
+        ),
+        cost_estimate=pl.CostEstimate(
+            flops=2 * rows * 2 * slots * bins,
+            transcendentals=0,
+            bytes_accessed=2 * rows * bins + 2 * 2 * slots * bins,
+        ),
+    )(library, first, second)
 
 
 def ring_gather(block, axis):
@@ -128,21 +220,14 @@
     part = arrived.shape[0] // 2
     part_a = ring_gather(ring_gather(arrived[:part], "x"), "z")
     part_b = ring_gather(ring_gather(arrived[part:], "z"), "x")
-    own_side = jnp.concatenate(
-        [part_a.reshape(-1, arrived.shape[1]), part_b.reshape(-1, arrived.shape[1])], axis=0
-    )
+    bins = arrived.shape[1]
+    own_a = part_a.reshape(-1, bins)
+    own_b = part_b.reshape(-1, bins)
     partner = [(core, core_count - 1 - core) for core in range(core_count)]
-    other_side = lax.ppermute(own_side, "core", partner)
-    own_best = column_topk(
-        lax.dot_general(
-            library, own_side, (((1,), (1,)), ((), ())), preferred_element_type=jnp.float32
-        )
-    )
-    other_best = column_topk(
-        lax.dot_general(
-            library, other_side, (((1,), (1,)), ((), ())), preferred_element_type=jnp.float32
-        )
-    )
+    other_a = lax.ppermute(own_a, "core", partner)
+    other_b = lax.ppermute(own_b, "core", partner)
+    own_best = score_topk(library, own_a, own_b)
+    other_best = score_topk(library, other_a, other_b)
     local_best = jnp.concatenate([own_best, other_best], axis=1).T
     row = jnp.arange(local_best.shape[0], dtype=jnp.int32)
     slot = row % capacity

time: 155 us -> 164 us (1.058)
  Pallas kernels: 9.67 us -> 58.7 us
  matrix products: 32 us -> 0.36 us
  other arithmetic: 22.2 us -> 13.8 us
    pallas_call x2, Pallas kernels: 9.67 us -> 58.7 us  [score_topk(): pl.pallas_call(score_topk_kernel, out_shape=jax.ShapeDtypeStruct((TOP_K,...]
    dot_general x2 -> x0, matrix products: 31.6 us -> none  [the longest x1 15.8 us: per_device(): lax.dot_general(library, own_side, (((1,), (1,)), ((), ())), preferred_el...]
    concatenate x1 -> x0, other arithmetic: 7.67 us -> none  [per_device(): jnp.concatenate([part_a.reshape(-1, arrived.shape[1]), part_b.reshape(-1,...]
    ppermute x1 -> x2, starting transfers between devices: 4.38 us -> 4.37 us  [the longest x1 3.82 us: per_device(): other_b = lax.ppermute(own_b, 'core', partner)]
  transfers between devices with their start and end apart: 18 -> 19, of which waited for: 5 -> 4; matrix products, arithmetic and copies ran while one was open for 12% -> 3% of each run, Pallas kernels for 3% -> 18%
where the time goes in v5:
time: 164 us
  Pallas kernels  58.7 us (36%)
  waiting for transfers between devices  37.2 us (23%)
  starting transfers between devices  32.3 us (20%)
  other arithmetic  13.8 us (8%)
  blocking collectives  13.4 us (8%)
  local copies, waits for them, and re-layouts  7.71 us (5%)
    pallas_call x2, Pallas kernels, score_topk(): pl.pallas_call(score_topk_kernel, out_shape=jax.ShapeDtypeStruct((TOP_K,...  58.7 us
    ppermute x4, waiting for transfers between devices, ring_gather(): from_minus = lax.ppermute(flat, axis, forward)  21.7 us
    all_to_all x1, blocking collectives, per_device(): lax.all_to_all(packed, 'mass', split_axis=0, concat_axis=0, tiled=True)  13.4 us
    ppermute x4, starting transfers between devices, ring_gather(): far_second = lax.ppermute(from_plus[half:], axis, backward)  9.69 us
    all_to_all x1, waiting for transfers between devices, per_device(): lax.all_to_all(outgoing, ('mass', 'x', 'z', 'core'), split_axis=0, concat...  9.42 us
    ppermute x4, starting transfers between devices, ring_gather(): from_plus = lax.ppermute(flat, axis, backward)  8.37 us
    ppermute x4, waiting for transfers between devices, ring_gather(): far_first = lax.ppermute(from_minus[:half], axis, forward)  6.05 us
    another operation x8, other arithmetic, ring_gather(): stacked = jnp.stack([flat, from_plus, far, from_minus])  4.95 us
  transfers between devices with their start and end apart: 19, of which 4 were waited for; matrix products, arithmetic and copies ran while one was open for 3% of the time, Pallas kernels for 18%

profile of v5, /device:TPU:1, one launch (start us, length us, event | category | flops | bytes accessed | tf_op | source)
XLA Modules:
  0.0 164.0 jit_solution(14012776507841315644)
XLA Ops:
  0.0 0.7 and_compare_fusion.12
  0.7 1.0 pad_maximum_fusion.4
  1.7 0.2 slice.109
  1.8 1.1 pad_select_fusion.11
  3.0 0.2 slice.110
  3.3 0.2 slice.111
  3.6 0.2 slice.112
  4.0 0.2 slice.113
  4.7 0.2 slice.115
  6.2 0.4 multiply_reduce_fusion
  6.5 0.2 convert_reduce_fusion
  6.7 0.4 fusion
  7.1 13.4 %all_to_all.14 = bf16[4,8,8192]{2,1,0:T(8,128)(2,1)S(1)} all-to-all(bf16[4,8,8192]{2,1,0:T(8,128)(2,1)S(1)} %fusion), channel_id=1, replica_groups=mesh['mass'=4,'x'=4,'z'=4,'core'=2] {'mass'}, dimensions={0} | all-to-all | bytes 1048576 | tf_op jit(solution)/shard_map/all_to_all | solution.py:219
  20.6 1.7 %collective-permute-start.9 = (bf16[16,8192]{1,0:T(8,128)(2,1)S(1)}, bf16[16,8192]{1,0:T(8,128)(2,1)S(1)}, u32[]{:S(2)}, u32[]{:S(2)}) collective-permute-start(bf16[16,8192]{1,0:T(8,128)(2,1)S(1)} %get-tuple-element.13), channel_id=1, source_target_pairs={{0,2},{2,4},{4,6},{6,0},{1,3},{3,5},{5,7},{7,1},{8,10},{10,12},{12... | collective-permute-start | bytes 786440 | tf_op jit(solution)/shard_map/ppermute | solution.py:195
  22.3 2.2 %collective-permute-start.8 = (bf16[16,8192]{1,0:T(8,128)(2,1)S(1)}, bf16[16,8192]{1,0:T(8,128)(2,1)S(1)}, u32[]{:S(2)}, u32[]{:S(2)}) collective-permute-start(bf16[16,8192]{1,0:T(8,128)(2,1)S(1)} %get-tuple-element.13), channel_id=1, source_target_pairs={{0,6},{2,0},{4,2},{6,4},{1,7},{3,1},{5,3},{7,5},{8,14},{10,8},{12,... | collective-permute-start | bytes 786440 | tf_op jit(solution)/shard_map/ppermute | solution.py:196
  24.5 1.2 collective-permute-start.1
  25.7 1.5 collective-permute-start
  27.2 2.1 %collective-permute-done.9 = bf16[16,8192]{1,0:T(8,128)(2,1)S(1)} collective-permute-done((bf16[16,8192]{1,0:T(8,128)(2,1)S(1)}, bf16[16,8192]{1,0:T(8,128)(2,1)S(1)}, u32[]{:S(2)}, u32[]{:S(2)}) %collective-permute-start.9) | collective-permute-done | bytes 262176 | tf_op jit(solution)/shard_map/ppermute | solution.py:195
  29.4 2.7 %collective-permute-start.11 = (bf16[8,8192]{1,0:T(8,128)(2,1)S(1)}, bf16[8,8192]{1,0:T(8,128)(2,1)S(1)}, u32[]{:S(2)}, u32[]{:S(2)}) collective-permute-start(bf16[8,8192]{1,0:T(8,128)(2,1)S(1)} %slice.130), channel_id=1, source_target_pairs={{0,6},{2,0},{4,2},{6,4},{1,7},{3,1},{5,3},{7,5},{8,14},{10,8},{12,... | collective-permute-start | bytes 393224 | tf_op jit(solution)/shard_map/ppermute | solution.py:198
  32.1 1.3 collective-permute-start.2
  33.4 1.5 collective-permute-start.3
  35.1 0.7 collective-permute-start.13
  35.8 2.1 %collective-permute-start.12 = (bf16[64,8192]{1,0:T(8,128)(2,1)S(1)}, bf16[64,8192]{1,0:T(8,128)(2,1)S(1)}, u32[]{:S(2)}, u32[]{:S(2)}) collective-permute-start(bf16[64,8192]{1,0:T(8,128)(2,1)S(1)} %bitcast.52), channel_id=1, source_target_pairs={{0,24},{8,0},{16,8},{24,16},{1,25},{9,1},{17,9},{25,17},{2,26},{10... | collective-permute-start | bytes 3145736 | tf_op jit(solution)/shard_map/ppermute | solution.py:196
  38.1 2.7 %collective-permute-start.4 = (bf16[64,8192]{1,0:T(8,128)(2,1)S(1)}, bf16[64,8192]{1,0:T(8,128)(2,1)S(1)}, u32[]{:S(2)}, u32[]{:S(2)}) collective-permute-start(bf16[64,8192]{1,0:T(8,128)(2,1)S(1)} %bitcast.55), channel_id=1, source_target_pairs={{0,6},{2,0},{4,2},{6,4},{1,7},{3,1},{5,3},{7,5},{8,14},{10,8},{12,... | collective-permute-start | bytes 3145736 | tf_op jit(solution)/shard_map/ppermute | solution.py:196
  40.8 19.6 %collective-permute-done.13 = bf16[64,8192]{1,0:T(8,128)(2,1)S(1)} collective-permute-done((bf16[64,8192]{1,0:T(8,128)(2,1)S(1)}, bf16[64,8192]{1,0:T(8,128)(2,1)S(1)}, u32[]{:S(2)}, u32[]{:S(2)}) %collective-permute-start.13) | collective-permute-done | bytes 1048608 | tf_op jit(solution)/shard_map/ppermute | solution.py:195
  60.6 2.7 %collective-permute-start.15 = (bf16[32,8192]{1,0:T(8,128)(2,1)S(1)}, bf16[32,8192]{1,0:T(8,128)(2,1)S(1)}, u32[]{:S(2)}, u32[]{:S(2)}) collective-permute-start(bf16[32,8192]{1,0:T(8,128)(2,1)S(1)} %slice.132), channel_id=1, source_target_pairs={{0,24},{8,0},{16,8},{24,16},{1,25},{9,1},{17,9},{25,17},{2,26},{10... | collective-permute-start | bytes 1572872 | tf_op jit(solution)/shard_map/ppermute | solution.py:198
  63.5 2.7 %collective-permute-start.7 = (bf16[32,8192]{1,0:T(8,128)(2,1)S(1)}, bf16[32,8192]{1,0:T(8,128)(2,1)S(1)}, u32[]{:S(2)}, u32[]{:S(2)}) collective-permute-start(bf16[32,8192]{1,0:T(8,128)(2,1)S(1)} %slice.127), channel_id=1, source_target_pairs={{0,6},{2,0},{4,2},{6,4},{1,7},{3,1},{5,3},{7,5},{8,14},{10,8},{12,... | collective-permute-start | bytes 1572872 | tf_op jit(solution)/shard_map/ppermute | solution.py:198
  66.2 6.0 %collective-permute-done.14 = bf16[32,8192]{1,0:T(8,128)(2,1)S(1)} collective-permute-done((bf16[32,8192]{1,0:T(8,128)(2,1)S(1)}, bf16[32,8192]{1,0:T(8,128)(2,1)S(1)}, u32[]{:S(2)}, u32[]{:S(2)}) %collective-permute-start.14) | collective-permute-done | bytes 524320 | tf_op jit(solution)/shard_map/ppermute | solution.py:197
  72.4 2.3 %pad_maximum_fusion.1 = bf16[4,64,8192]{2,1,0:T(8,128)(2,1)} fusion(bf16[1,64,8192]{2,1,0:T(8,128)(2,1)S(1)} %bitcast.57, bf16[1,64,8192]{2,1,0:T(8,128)(2,1)S(1)} %maximum_bitcast_fusion.1, bf16[1,64,8192]{2,1,0:T(8,128)(2,1)S(1)} %bitcast.58, bf16[1,64,8192]{2,1,0:T(8,128)(2,1)S(1)} %bitcast.53), kind=kLoop, calls=%fused_computation.5 | loop fusion | flops 6291456 | bytes 8388608 | tf_op jit(solution)/shard_map/stack | solution.py:200
  74.6 3.8 %collective-permute-start.17 = (bf16[256,8192]{1,0:T(8,128)(2,1)}, bf16[256,8192]{1,0:T(8,128)(2,1)}, u32[]{:S(2)}, u32[]{:S(2)}) collective-permute-start(bf16[256,8192]{1,0:T(8,128)(2,1)} %bitcast.25.second_ref), channel_id=1, source_target_pairs={{0,1},{1,0},{2,3},{3,2},{4,5},{5,4},{6,7},{7,6},{8,9},{9,8},{10,11... | collective-permute-start | bytes 12582920 | tf_op jit(solution)/shard_map/ppermute | solution.py:228
  78.5 2.2 %pad_maximum_fusion = bf16[4,64,8192]{2,1,0:T(8,128)(2,1)} fusion(bf16[1,64,8192]{2,1,0:T(8,128)(2,1)S(1)} %bitcast.59, bf16[1,64,8192]{2,1,0:T(8,128)(2,1)S(1)} %maximum_bitcast_fusion, bf16[1,64,8192]{2,1,0:T(8,128)(2,1)S(1)} %bitcast.60, bf16[1,64,8192]{2,1,0:T(8,128)(2,1)S(1)} %bitcast.56), kind=kLoop, calls=%fused_computation.4 | loop fusion | flops 6291456 | bytes 8388608 | tf_op jit(solution)/shard_map/stack | solution.py:200
  80.8 0.6 collective-permute-start.16
  81.6 29.4 %shard_map.46 = f32[16,512]{1,0:T(8,128)S(1)} custom-call(bf16[1024,8192]{1,0:T(8,128)(2,1)} %library_ref.3, bf16[256,8192]{1,0:T(8,128)(2,1)} %bitcast.14.first_ref, bf16[256,8192]{1,0:T(8,128)(2,1)} %bitcast.25.second_ref), custom_call_target="tpu_custom_call" | custom-call | flops 8589934592 | bytes 25165824 | tf_op jit(solution)/shard_map/pallas_call | solution.py:164
  111.0 29.3 %shard_map.47 = f32[16,512]{1,0:T(8,128)S(1)} custom-call(bf16[1024,8192]{1,0:T(8,128)(2,1)} %library_ref.3, bf16[256,8192]{1,0:T(8,128)(2,1)} %collective-permute-done.16.first_ref, bf16[256,8192]{1,0:T(8,128)(2,1)} %collective-permute-done.17.second_ref), custom_call_target="tpu_custom_call" | custom-call | flops 8589934592 | bytes 25165824 | tf_op jit(solution)/shard_map/pallas_call | solution.py:164
  140.4 0.2 copy.18
  140.6 2.8 %gather_fusion = f32[1024,16]{1,0:T(8,128)S(1)} fusion(f32[1024,16]{1,0:T(8,128)S(1)} %copy.18, s32[1024]{0:T(1024)S(1)} %broadcast_clamp_fusion), kind=kCustom, calls=%fused_computation | custom fusion | bytes 135168 | tf_op jit(solution)/shard_map/jit(_take)/gather | solution.py:246
  143.4 0.2 bitcast_select_fusion
  143.6 0.8 reshape.463
  144.4 4.6 %all-to-all-start.1 = ((f32[128,1,128]{2,1,0:T(1,128)}), f32[128,1,128]{2,1,0:T(1,128)S(1)}, u32[]{:S(2)}, u32[]{:S(2)}) async-start(f32[128,1,128]{2,1,0:T(1,128)} %reshape.463), calls=%async_computation.1 | async-start | bytes 131072 | tf_op jit(solution)/shard_map/all_to_all | solution.py:247
  149.1 9.4 %all-to-all-done.1 = f32[128,1,128]{2,1,0:T(1,128)S(1)} async-done(((f32[128,1,128]{2,1,0:T(1,128)}), f32[128,1,128]{2,1,0:T(1,128)S(1)}, u32[]{:S(2)}, u32[]{:S(2)}) %all-to-all-start.1) | async-done | bytes 65568 | tf_op jit(solution)/shard_map/all_to_all | solution.py:247
  158.5 0.5 broadcast.949
  159.0 0.8 reduce
  159.9 0.2 reshape.464
  160.0 0.2 copy.21
  160.3 0.2 copy.20
  160.5 0.3 reshape.446
  160.8 0.6 gather_fusion.1
  161.5 2.5 %sort_prefixfusion = f32[16,16]{1,0:T(8,128)} fusion(f32[16,512]{1,0:T(8,128)S(1)} %broadcast_select_fusion), kind=kCustom, calls=%top_k.9.sort_prefix | custom fusion | flops 106496 | bytes 33792 | tf_op jit(solution)/shard_map/top_k | solution.py:253
  (67 shorter events, 3.6 us)
Async XLA Ops:
  5.2 1.0 copy-start
  5.3 1.3 copy-start.1
  20.6 8.7 %collective-permute-start.9 = (bf16[16,8192]{1,0:T(8,128)(2,1)S(1)}, bf16[16,8192]{1,0:T(8,128)(2,1)S(1)}, u32[]{:S(2)}, u32[]{:S(2)}) collective-permute-start(bf16[16,8192]{1,0:T(8,128)(2,1)S(1)} %get-tuple-element.13), channel_id=1, source_target_pairs={{0,2},{2,4},{4,6},{6,0},{1,3},{3,5},{5,7},{7,1},{8,10},{10,12},{12... | collective-permute-start | bytes 786440 | tf_op jit(solution)/shard_map/ppermute | solution.py:195
  22.3 7.1 %collective-permute-start.8 = (bf16[16,8192]{1,0:T(8,128)(2,1)S(1)}, bf16[16,8192]{1,0:T(8,128)(2,1)S(1)}, u32[]{:S(2)}, u32[]{:S(2)}) collective-permute-start(bf16[16,8192]{1,0:T(8,128)(2,1)S(1)} %get-tuple-element.13), channel_id=1, source_target_pairs={{0,6},{2,0},{4,2},{6,4},{1,7},{3,1},{5,3},{7,5},{8,14},{10,8},{12,... | collective-permute-start | bytes 786440 | tf_op jit(solution)/shard_map/ppermute | solution.py:196
  24.5 7.6 %collective-permute-start.1 = (bf16[16,8192]{1,0:T(8,128)(2,1)S(1)}, bf16[16,8192]{1,0:T(8,128)(2,1)S(1)}, u32[]{:S(2)}, u32[]{:S(2)}) collective-permute-start(bf16[16,8192]{1,0:T(8,128)(2,1)S(1)} %get-tuple-element.12), channel_id=1, source_target_pairs={{0,8},{8,16},{16,24},{24,0},{1,9},{9,17},{17,25},{25,1},{2,10},{10... | collective-permute-start | bytes 786440 | tf_op jit(solution)/shard_map/ppermute | solution.py:195
  25.7 7.7 %collective-permute-start = (bf16[16,8192]{1,0:T(8,128)(2,1)S(1)}, bf16[16,8192]{1,0:T(8,128)(2,1)S(1)}, u32[]{:S(2)}, u32[]{:S(2)}) collective-permute-start(bf16[16,8192]{1,0:T(8,128)(2,1)S(1)} %get-tuple-element.12), channel_id=1, source_target_pairs={{0,24},{8,0},{16,8},{24,16},{1,25},{9,1},{17,9},{25,17},{2,26},{10... | collective-permute-start | bytes 786440 | tf_op jit(solution)/shard_map/ppermute | solution.py:196
  29.3 5.7 %collective-permute-start.10 = (bf16[8,8192]{1,0:T(8,128)(2,1)S(1)}, bf16[8,8192]{1,0:T(8,128)(2,1)S(1)}, u32[]{:S(2)}, u32[]{:S(2)}) collective-permute-start(bf16[8,8192]{1,0:T(8,128)(2,1)S(1)} %slice.129), channel_id=1, source_target_pairs={{0,2},{2,4},{4,6},{6,0},{1,3},{3,5},{5,7},{7,1},{8,10},{10,12},{12... | collective-permute-start | bytes 393224 | tf_op jit(solution)/shard_map/ppermute | solution.py:197
  29.4 5.6 %collective-permute-start.11 = (bf16[8,8192]{1,0:T(8,128)(2,1)S(1)}, bf16[8,8192]{1,0:T(8,128)(2,1)S(1)}, u32[]{:S(2)}, u32[]{:S(2)}) collective-permute-start(bf16[8,8192]{1,0:T(8,128)(2,1)S(1)} %slice.130), channel_id=1, source_target_pairs={{0,6},{2,0},{4,2},{6,4},{1,7},{3,1},{5,3},{7,5},{8,14},{10,8},{12,... | collective-permute-start | bytes 393224 | tf_op jit(solution)/shard_map/ppermute | solution.py:198
  32.1 5.8 %collective-permute-start.2 = (bf16[8,8192]{1,0:T(8,128)(2,1)S(1)}, bf16[8,8192]{1,0:T(8,128)(2,1)S(1)}, u32[]{:S(2)}, u32[]{:S(2)}) collective-permute-start(bf16[8,8192]{1,0:T(8,128)(2,1)S(1)} %slice.124), channel_id=1, source_target_pairs={{0,8},{8,16},{16,24},{24,0},{1,9},{9,17},{17,25},{25,1},{2,10},{10... | collective-permute-start | bytes 393224 | tf_op jit(solution)/shard_map/ppermute | solution.py:197
  33.4 4.5 %collective-permute-start.3 = (bf16[8,8192]{1,0:T(8,128)(2,1)S(1)}, bf16[8,8192]{1,0:T(8,128)(2,1)S(1)}, u32[]{:S(2)}, u32[]{:S(2)}) collective-permute-start(bf16[8,8192]{1,0:T(8,128)(2,1)S(1)} %slice.125), channel_id=1, source_target_pairs={{0,24},{8,0},{16,8},{24,16},{1,25},{9,1},{17,9},{25,17},{2,26},{10... | collective-permute-start | bytes 393224 | tf_op jit(solution)/shard_map/ppermute | solution.py:198
  35.1 25.3 %collective-permute-start.13 = (bf16[64,8192]{1,0:T(8,128)(2,1)S(1)}, bf16[64,8192]{1,0:T(8,128)(2,1)S(1)}, u32[]{:S(2)}, u32[]{:S(2)}) collective-permute-start(bf16[64,8192]{1,0:T(8,128)(2,1)S(1)} %bitcast.51), channel_id=1, source_target_pairs={{0,8},{8,16},{16,24},{24,0},{1,9},{9,17},{17,25},{25,1},{2,10},{10... | collective-permute-start | bytes 3145736 | tf_op jit(solution)/shard_map/ppermute | solution.py:195
  35.8 24.7 %collective-permute-start.12 = (bf16[64,8192]{1,0:T(8,128)(2,1)S(1)}, bf16[64,8192]{1,0:T(8,128)(2,1)S(1)}, u32[]{:S(2)}, u32[]{:S(2)}) collective-permute-start(bf16[64,8192]{1,0:T(8,128)(2,1)S(1)} %bitcast.52), channel_id=1, source_target_pairs={{0,24},{8,0},{16,8},{24,16},{1,25},{9,1},{17,9},{25,17},{2,26},{10... | collective-permute-start | bytes 3145736 | tf_op jit(solution)/shard_map/ppermute | solution.py:196
  38.1 25.3 %collective-permute-start.5 = (bf16[64,8192]{1,0:T(8,128)(2,1)S(1)}, bf16[64,8192]{1,0:T(8,128)(2,1)S(1)}, u32[]{:S(2)}, u32[]{:S(2)}) collective-permute-start(bf16[64,8192]{1,0:T(8,128)(2,1)S(1)} %bitcast.54), channel_id=1, source_target_pairs={{0,2},{2,4},{4,6},{6,0},{1,3},{3,5},{5,7},{7,1},{8,10},{10,12},{12... | collective-permute-start | bytes 3145736 | tf_op jit(solution)/shard_map/ppermute | solution.py:195
  38.1 25.3 %collective-permute-start.4 = (bf16[64,8192]{1,0:T(8,128)(2,1)S(1)}, bf16[64,8192]{1,0:T(8,128)(2,1)S(1)}, u32[]{:S(2)}, u32[]{:S(2)}) collective-permute-start(bf16[64,8192]{1,0:T(8,128)(2,1)S(1)} %bitcast.55), channel_id=1, source_target_pairs={{0,6},{2,0},{4,2},{6,4},{1,7},{3,1},{5,3},{7,5},{8,14},{10,8},{12,... | collective-permute-start | bytes 3145736 | tf_op jit(solution)/shard_map/ppermute | solution.py:196
  60.5 11.8 %collective-permute-start.14 = (bf16[32,8192]{1,0:T(8,128)(2,1)S(1)}, bf16[32,8192]{1,0:T(8,128)(2,1)S(1)}, u32[]{:S(2)}, u32[]{:S(2)}) collective-permute-start(bf16[32,8192]{1,0:T(8,128)(2,1)S(1)} %slice.131), channel_id=1, source_target_pairs={{0,8},{8,16},{16,24},{24,0},{1,9},{9,17},{17,25},{25,1},{2,10},{10... | collective-permute-start | bytes 1572872 | tf_op jit(solution)/shard_map/ppermute | solution.py:197
  60.6 11.7 %collective-permute-start.15 = (bf16[32,8192]{1,0:T(8,128)(2,1)S(1)}, bf16[32,8192]{1,0:T(8,128)(2,1)S(1)}, u32[]{:S(2)}, u32[]{:S(2)}) collective-permute-start(bf16[32,8192]{1,0:T(8,128)(2,1)S(1)} %slice.132), channel_id=1, source_target_pairs={{0,24},{8,0},{16,8},{24,16},{1,25},{9,1},{17,9},{25,17},{2,26},{10... | collective-permute-start | bytes 1572872 | tf_op jit(solution)/shard_map/ppermute | solution.py:198
  63.4 15.1 %collective-permute-start.6 = (bf16[32,8192]{1,0:T(8,128)(2,1)S(1)}, bf16[32,8192]{1,0:T(8,128)(2,1)S(1)}, u32[]{:S(2)}, u32[]{:S(2)}) collective-permute-start(bf16[32,8192]{1,0:T(8,128)(2,1)S(1)} %slice.126), channel_id=1, source_target_pairs={{0,2},{2,4},{4,6},{6,0},{1,3},{3,5},{5,7},{7,1},{8,10},{10,12},{12... | collective-permute-start | bytes 1572872 | tf_op jit(solution)/shard_map/ppermute | solution.py:197
  63.5 14.9 %collective-permute-start.7 = (bf16[32,8192]{1,0:T(8,128)(2,1)S(1)}, bf16[32,8192]{1,0:T(8,128)(2,1)S(1)}, u32[]{:S(2)}, u32[]{:S(2)}) collective-permute-start(bf16[32,8192]{1,0:T(8,128)(2,1)S(1)} %slice.127), channel_id=1, source_target_pairs={{0,6},{2,0},{4,2},{6,4},{1,7},{3,1},{5,3},{7,5},{8,14},{10,8},{12,... | collective-permute-start | bytes 1572872 | tf_op jit(solution)/shard_map/ppermute | solution.py:198
  74.6 36.4 %collective-permute-start.17 = (bf16[256,8192]{1,0:T(8,128)(2,1)}, bf16[256,8192]{1,0:T(8,128)(2,1)}, u32[]{:S(2)}, u32[]{:S(2)}) collective-permute-start(bf16[256,8192]{1,0:T(8,128)(2,1)} %bitcast.25.second_ref), channel_id=1, source_target_pairs={{0,1},{1,0},{2,3},{3,2},{4,5},{5,4},{6,7},{7,6},{8,9},{9,8},{10,11... | collective-permute-start | bytes 12582920 | tf_op jit(solution)/shard_map/ppermute | solution.py:228
  80.8 30.2 %collective-permute-start.16 = (bf16[256,8192]{1,0:T(8,128)(2,1)}, bf16[256,8192]{1,0:T(8,128)(2,1)}, u32[]{:S(2)}, u32[]{:S(2)}) collective-permute-start(bf16[256,8192]{1,0:T(8,128)(2,1)} %bitcast.14.first_ref), channel_id=1, source_target_pairs={{0,1},{1,0},{2,3},{3,2},{4,5},{5,4},{6,7},{7,6},{8,9},{9,8},{10,11... | collective-permute-start | bytes 12582920 | tf_op jit(solution)/shard_map/ppermute | solution.py:227
  144.4 14.1 %all-to-all-start.1 = ((f32[128,1,128]{2,1,0:T(1,128)}), f32[128,1,128]{2,1,0:T(1,128)S(1)}, u32[]{:S(2)}, u32[]{:S(2)}) async-start(f32[128,1,128]{2,1,0:T(1,128)} %reshape.463), calls=%async_computation.1 | async-start | bytes 131072 | tf_op jit(solution)/shard_map/all_to_all | solution.py:247

commit v6 on v4

--- a/solution.py
+++ b/solution.py
@@ -124,7 +124,19 @@
         jnp.arange(mass_count * capacity, dtype=jnp.int32)[:, None] == slot_index[None, :]
     ).astype(jnp.bfloat16)
     packed = jnp.dot(selector, spectra, preferred_element_type=jnp.float32).astype(jnp.bfloat16)
-    arrived = lax.all_to_all(packed, "mass", split_axis=0, concat_axis=0, tiled=True)
+    packed = packed.reshape(mass_count, capacity, packed.shape[-1])
+    own_mass = lax.axis_index("mass")
+    chunks = []
+    for distance in range(mass_count):
+        outgoing = jnp.take(packed, (own_mass + distance) % mass_count, axis=0)
+        if distance:
+            outgoing = lax.ppermute(
+                outgoing,
+                "mass",
+                [(source, (source + distance) % mass_count) for source in range(mass_count)],
+            )
+        chunks.append(outgoing)
+    arrived = jnp.concatenate(chunks, axis=0)
     part = arrived.shape[0] // 2
     part_a = ring_gather(ring_gather(arrived[:part], "x"), "z")
     part_b = ring_gather(ring_gather(arrived[part:], "z"), "x")
@@ -154,7 +166,7 @@
     step_x = (source_x - lax.axis_index("x")) % x_count
     step_z = (source_z - lax.axis_index("z")) % z_count
     side = jnp.where(source_core == lax.axis_index("core"), 0, 1)
-    in_part = source_mass * capacity + slot
+    in_part = (own_mass - source_mass) % mass_count * capacity + slot
     column_a = (step_z * x_count + step_x) * part + in_part
     column_b = (x_count * z_count + step_x * z_count + step_z) * part + in_part - part
     column = side * (shard_count // core_count) * 2 * part + jnp.where(in_part < part, column_a, column_b)

time: 155 us -> 153 us (0.987)
  waiting for transfers between devices: 36.4 us -> 30.4 us
  blocking collectives: 13.4 us -> 16.8 us
    all_to_all x1 -> x0, waiting for transfers between devices: 9.42 us -> none  [per_device(): lax.all_to_all(outgoing, ('mass', 'x', 'z', 'core'), split_axis=0, concat...]
    ppermute x0 -> x3, starting transfers between devices: none -> 5.87 us  [per_device(): lax.ppermute(outgoing, 'mass', [(source, (source + distance) % mass_count...]
    all_to_all x1 -> x0, starting transfers between devices: 4.86 us -> none  [per_device(): lax.all_to_all(outgoing, ('mass', 'x', 'z', 'core'), split_axis=0, concat...]
    all_to_all x1, blocking collectives: 13.4 us -> 16.8 us  [per_device(): lax.all_to_all(outgoing, ('mass', 'x', 'z', 'core'), split_axis=0, concat...]
    ppermute x0 -> x3, waiting for transfers between devices: none -> 1.87 us  [per_device(): lax.ppermute(outgoing, 'mass', [(source, (source + distance) % mass_count...]
    another operation x8 -> x9, other arithmetic: 4.93 us -> 4.97 us  [ring_gather(): stacked = jnp.stack([flat, from_plus, far, from_minus])]
  transfers between devices with their start and end apart: 18 -> 20, of which waited for: 5 -> 7; matrix products, arithmetic and copies ran while one was open for 12% -> 12% of each run, Pallas kernels for 3% -> 3%
where the time goes in v6:
time: 153 us; the launch traced here: 152 us
  starting transfers between devices  33.7 us (22%)
  matrix products  32 us (21%)
  waiting for transfers between devices  30.4 us (20%)
  other arithmetic  22.3 us (15%)
  blocking collectives  16.8 us (11%)
  Pallas kernels  9.68 us (6%)
  local copies, waits for them, and re-layouts  7.05 us (5%)
    ppermute x4, waiting for transfers between devices, ring_gather(): from_minus = lax.ppermute(flat, axis, forward)  21.8 us
    all_to_all x1, blocking collectives, per_device(): lax.all_to_all(outgoing, ('mass', 'x', 'z', 'core'), split_axis=0, concat...  16.8 us
    dot_general x1, matrix products, per_device(): lax.dot_general(library, own_side, (((1,), (1,)), ((), ())), preferred_el...  15.8 us
    dot_general x1, matrix products, per_device(): lax.dot_general(library, other_side, (((1,), (1,)), ((), ())), preferred_...  15.8 us
    pallas_call x2, Pallas kernels, column_topk(): pl.pallas_call(column_topk_kernel, out_shape=jax.ShapeDtypeStruct((TOP_K,...  9.68 us
    ppermute x4, starting transfers between devices, ring_gather(): far_second = lax.ppermute(from_plus[half:], axis, backward)  9.09 us
    ppermute x4, starting transfers between devices, ring_gather(): from_plus = lax.ppermute(flat, axis, backward)  7.9 us
    concatenate x1, other arithmetic, per_device(): jnp.concatenate([part_a.reshape(-1, arrived.shape[1]), part_b.reshape(-1,...  7.67 us
  transfers between devices with their start and end apart: 20, of which 7 were waited for; matrix products, arithmetic and copies ran while one was open for 12% of the time, Pallas kernels for 3%

profile of v6, /device:TPU:1, one launch (start us, length us, event | category | flops | bytes accessed | tf_op | source)
XLA Modules:
  0.0 152.3 jit_solution(7790990096512377880)
XLA Ops:
  0.0 0.7 and_compare_fusion.12
  0.7 1.0 pad_maximum_fusion.5
  1.8 1.1 pad_select_fusion.11
  6.2 0.4 multiply_reduce_fusion
  6.7 0.4 fusion
  7.2 2.2 %collective-permute-start = (bf16[8,8192]{1,0:T(8,128)(2,1)S(1)}, bf16[8,8192]{1,0:T(8,128)(2,1)S(1)}, u32[]{:S(2)}, u32[]{:S(2)}) collective-permute-start(bf16[8,8192]{1,0:T(8,128)(2,1)S(1)} %get-tuple-element.26), channel_id=1, source_target_pairs={{0,32},{32,64},{64,96},{96,0},{1,33},{33,65},{65,97},{97,1},{2,34}... | collective-permute-start | bytes 393224 | tf_op jit(solution)/shard_map/ppermute | solution.py:133
  9.4 2.6 %collective-permute-start.9 = (bf16[8,8192]{1,0:T(8,128)(2,1)S(1)}, bf16[8,8192]{1,0:T(8,128)(2,1)S(1)}, u32[]{:S(2)}, u32[]{:S(2)}) collective-permute-start(bf16[8,8192]{1,0:T(8,128)(2,1)S(1)} %get-tuple-element.25), channel_id=1, source_target_pairs={{0,64},{32,96},{64,0},{96,32},{1,65},{33,97},{65,1},{97,33},{2,66}... | collective-permute-start | bytes 393224 | tf_op jit(solution)/shard_map/ppermute | solution.py:133
  12.0 1.1 collective-permute-start.10
  13.1 0.8 collective-permute-done
  13.9 1.2 collective-permute-start.2
  15.1 1.6 %collective-permute-start.1 = (bf16[16,8192]{1,0:T(8,128)(2,1)S(1)}, bf16[16,8192]{1,0:T(8,128)(2,1)S(1)}, u32[]{:S(2)}, u32[]{:S(2)}) collective-permute-start(bf16[16,8192]{1,0:T(8,128)(2,1)S(1)} %get-tuple-element.28), channel_id=1, source_target_pairs={{0,24},{8,0},{16,8},{24,16},{1,25},{9,1},{17,9},{25,17},{2,26},{10... | collective-permute-start | bytes 786440 | tf_op jit(solution)/shard_map/ppermute | solution.py:104
  16.7 1.0 collective-permute-done.9
  17.8 1.7 %collective-permute-start.12 = (bf16[16,8192]{1,0:T(8,128)(2,1)S(1)}, bf16[16,8192]{1,0:T(8,128)(2,1)S(1)}, u32[]{:S(2)}, u32[]{:S(2)}) collective-permute-start(bf16[16,8192]{1,0:T(8,128)(2,1)S(1)} %constant_dynamic-update-slice_fusion), channel_id=1, source_target_pairs={{0,2},{2,4},{4,6},{6,0},{1,3},{3,5},{5,7},{7,1},{8,10},{10,12},{12... | collective-permute-start | bytes 786440 | tf_op jit(solution)/shard_map/ppermute | solution.py:103
  19.5 2.2 %collective-permute-start.11 = (bf16[16,8192]{1,0:T(8,128)(2,1)S(1)}, bf16[16,8192]{1,0:T(8,128)(2,1)S(1)}, u32[]{:S(2)}, u32[]{:S(2)}) collective-permute-start(bf16[16,8192]{1,0:T(8,128)(2,1)S(1)} %constant_dynamic-update-slice_fusion), channel_id=1, source_target_pairs={{0,6},{2,0},{4,2},{6,4},{1,7},{3,1},{5,3},{7,5},{8,14},{10,8},{12,... | collective-permute-start | bytes 786440 | tf_op jit(solution)/shard_map/ppermute | solution.py:104
  21.7 1.2 collective-permute-start.3
  23.0 1.6 %collective-permute-start.4 = (bf16[8,8192]{1,0:T(8,128)(2,1)S(1)}, bf16[8,8192]{1,0:T(8,128)(2,1)S(1)}, u32[]{:S(2)}, u32[]{:S(2)}) collective-permute-start(bf16[8,8192]{1,0:T(8,128)(2,1)S(1)} %slice.121), channel_id=1, source_target_pairs={{0,24},{8,0},{16,8},{24,16},{1,25},{9,1},{17,9},{25,17},{2,26},{10... | collective-permute-start | bytes 393224 | tf_op jit(solution)/shard_map/ppermute | solution.py:106
  24.6 2.1 %collective-permute-done.12 = bf16[16,8192]{1,0:T(8,128)(2,1)S(1)} collective-permute-done((bf16[16,8192]{1,0:T(8,128)(2,1)S(1)}, bf16[16,8192]{1,0:T(8,128)(2,1)S(1)}, u32[]{:S(2)}, u32[]{:S(2)}) %collective-permute-start.12) | collective-permute-done | bytes 262176 | tf_op jit(solution)/shard_map/ppermute | solution.py:103
  26.8 2.7 %collective-permute-start.14 = (bf16[8,8192]{1,0:T(8,128)(2,1)S(1)}, bf16[8,8192]{1,0:T(8,128)(2,1)S(1)}, u32[]{:S(2)}, u32[]{:S(2)}) collective-permute-start(bf16[8,8192]{1,0:T(8,128)(2,1)S(1)} %slice.125), channel_id=1, source_target_pairs={{0,6},{2,0},{4,2},{6,4},{1,7},{3,1},{5,3},{7,5},{8,14},{10,8},{12,... | collective-permute-start | bytes 393224 | tf_op jit(solution)/shard_map/ppermute | solution.py:106
  29.8 2.7 %collective-permute-start.5 = (bf16[64,8192]{1,0:T(8,128)(2,1)S(1)}, bf16[64,8192]{1,0:T(8,128)(2,1)S(1)}, u32[]{:S(2)}, u32[]{:S(2)}) collective-permute-start(bf16[64,8192]{1,0:T(8,128)(2,1)S(1)} %bitcast.66), channel_id=1, source_target_pairs={{0,6},{2,0},{4,2},{6,4},{1,7},{3,1},{5,3},{7,5},{8,14},{10,8},{12,... | collective-permute-start | bytes 3145736 | tf_op jit(solution)/shard_map/ppermute | solution.py:104
  32.7 1.3 collective-permute-start.16
  33.9 1.5 collective-permute-start.15
  35.4 19.6 %collective-permute-done.6 = bf16[64,8192]{1,0:T(8,128)(2,1)S(1)} collective-permute-done((bf16[64,8192]{1,0:T(8,128)(2,1)S(1)}, bf16[64,8192]{1,0:T(8,128)(2,1)S(1)}, u32[]{:S(2)}, u32[]{:S(2)}) %collective-permute-start.6) | collective-permute-done | bytes 1048608 | tf_op jit(solution)/shard_map/ppermute | solution.py:103
  55.2 3.1 %collective-permute-start.8 = (bf16[32,8192]{1,0:T(8,128)(2,1)S(1)}, bf16[32,8192]{1,0:T(8,128)(2,1)S(1)}, u32[]{:S(2)}, u32[]{:S(2)}) collective-permute-start(bf16[32,8192]{1,0:T(8,128)(2,1)S(1)} %slice.123), channel_id=1, source_target_pairs={{0,6},{2,0},{4,2},{6,4},{1,7},{3,1},{5,3},{7,5},{8,14},{10,8},{12,... | collective-permute-start | bytes 1572872 | tf_op jit(solution)/shard_map/ppermute | solution.py:106
  58.3 1.3 collective-permute-start.17
  59.6 1.7 %collective-permute-start.18 = (bf16[32,8192]{1,0:T(8,128)(2,1)S(1)}, bf16[32,8192]{1,0:T(8,128)(2,1)S(1)}, u32[]{:S(2)}, u32[]{:S(2)}) collective-permute-start(bf16[32,8192]{1,0:T(8,128)(2,1)S(1)} %slice.127), channel_id=1, source_target_pairs={{0,24},{8,0},{16,8},{24,16},{1,25},{9,1},{17,9},{25,17},{2,26},{10... | collective-permute-start | bytes 1572872 | tf_op jit(solution)/shard_map/ppermute | solution.py:106
  61.3 5.9 %collective-permute-done.7 = bf16[32,8192]{1,0:T(8,128)(2,1)S(1)} collective-permute-done((bf16[32,8192]{1,0:T(8,128)(2,1)S(1)}, bf16[32,8192]{1,0:T(8,128)(2,1)S(1)}, u32[]{:S(2)}, u32[]{:S(2)}) %collective-permute-start.7) | collective-permute-done | bytes 524320 | tf_op jit(solution)/shard_map/ppermute | solution.py:105
  67.3 2.3 %pad_maximum_fusion.1 = bf16[4,64,8192]{2,1,0:T(8,128)(2,1)} fusion(bf16[1,64,8192]{2,1,0:T(8,128)(2,1)S(1)} %bitcast.71, bf16[1,64,8192]{2,1,0:T(8,128)(2,1)S(1)} %maximum_bitcast_fusion, bf16[1,64,8192]{2,1,0:T(8,128)(2,1)S(1)} %bitcast.72, bf16[1,64,8192]{2,1,0:T(8,128)(2,1)S(1)} %bitcast.67), kind=kLoop, calls=%fused_computation.5 | loop fusion | flops 6291456 | bytes 8388608 | tf_op jit(solution)/shard_map/stack | solution.py:108
  69.6 0.7 collective-permute-done.17
  70.4 2.2 %pad_maximum_fusion.2 = bf16[4,64,8192]{2,1,0:T(8,128)(2,1)} fusion(bf16[1,64,8192]{2,1,0:T(8,128)(2,1)S(1)} %bitcast.73, bf16[1,64,8192]{2,1,0:T(8,128)(2,1)S(1)} %maximum_bitcast_fusion.1, bf16[1,64,8192]{2,1,0:T(8,128)(2,1)S(1)} %bitcast.74, bf16[1,64,8192]{2,1,0:T(8,128)(2,1)S(1)} %bitcast.70), kind=kLoop, calls=%fused_computation.6 | loop fusion | flops 6291456 | bytes 8388608 | tf_op jit(solution)/shard_map/stack | solution.py:108
  72.6 7.7 %pad_maximum_fusion = bf16[512,8192]{1,0:T(8,128)(2,1)} fusion(bf16[256,8192]{1,0:T(8,128)(2,1)} %bitcast.63, bf16[256,8192]{1,0:T(8,128)(2,1)} %bitcast.61), kind=kLoop, calls=%fused_computation.4 | loop fusion | flops 16777216 | bytes 16777216 | tf_op jit(solution)/shard_map/concatenate | solution.py:143
  80.3 3.9 %collective-permute-start.19 = (bf16[512,8192]{1,0:T(8,128)(2,1)}, bf16[512,8192]{1,0:T(8,128)(2,1)}, u32[]{:S(2)}, u32[]{:S(2)}) collective-permute-start(bf16[512,8192]{1,0:T(8,128)(2,1)} %pad_maximum_fusion), channel_id=1, source_target_pairs={{0,1},{1,0},{2,3},{3,2},{4,5},{5,4},{6,7},{7,6},{8,9},{9,8},{10,11... | collective-permute-start | bytes 25165832 | tf_op jit(solution)/shard_map/ppermute | solution.py:147
  84.5 15.8 %convolution_bitcast_fusion.1.scores_ref = f32[1024,512]{1,0:T(8,128)} fusion(bf16[1024,8192]{1,0:T(8,128)(2,1)} %param.7, bf16[256,8192]{1,0:T(8,128)(2,1)} %bitcast.64, bf16[256,8192]{1,0:T(8,128)(2,1)} %bitcast.62), kind=kOutput, calls=%fused_computation.8 | convolution fusion | flops 8606711808 | bytes 27262976 | tf_op jit(solution)/shard_map/dot_general | solution.py:149
  100.3 4.8 %shard_map.46 = f32[16,512]{1,0:T(8,128)} custom-call(f32[1024,512]{1,0:T(8,128)} %convolution_bitcast_fusion.1.scores_ref), custom_call_target="tpu_custom_call" | custom-call | flops 16777216 | bytes 2097152 | tf_op jit(solution)/shard_map/pallas_call | solution.py:85
  105.2 15.8 %convolution_bitcast_fusion.scores_ref = f32[1024,512]{1,0:T(8,128)} fusion(bf16[512,8192]{1,0:T(8,128)(2,1)} %collective-permute-done.19, bf16[1024,8192]{1,0:T(8,128)(2,1)} %param.7), kind=kOutput, calls=%fused_computation.7 | convolution fusion | flops 8589934592 | bytes 27262976 | tf_op jit(solution)/shard_map/dot_general | solution.py:154
  121.0 4.8 %shard_map.47 = f32[16,512]{1,0:T(8,128)} custom-call(f32[1024,512]{1,0:T(8,128)} %convolution_bitcast_fusion.scores_ref), custom_call_target="tpu_custom_call" | custom-call | flops 16777216 | bytes 2097152 | tf_op jit(solution)/shard_map/pallas_call | solution.py:85
  125.8 0.8 maximum_bitcast_fusion.4
  126.6 0.2 copy.30
  126.8 2.8 %gather_fusion = f32[1024,16]{1,0:T(8,128)S(1)} fusion(f32[1024,16]{1,0:T(8,128)S(1)} %copy.30, s32[1024]{0:T(1024)S(1)} %get-tuple-element.43), kind=kCustom, calls=%fused_computation | custom fusion | bytes 135168 | tf_op jit(solution)/shard_map/jit(_take)/gather | solution.py:173
  129.6 0.2 bitcast_select_fusion
  129.8 0.2 reshape.573
  130.0 16.8 %all_to_all.5 = f32[128,1,128]{2,1,0:T(1,128)S(1)} all-to-all(f32[128,1,128]{2,1,0:T(1,128)S(1)} %reshape.573), channel_id=1, replica_groups=mesh['mass'=4,'x'=4,'z'=4,'core'=2] {'mass','x','z','core'}, dimensions={0} | all-to-all | bytes 131072 | tf_op jit(solution)/shard_map/all_to_all | solution.py:174
  146.8 0.5 broadcast.1066
  147.4 0.8 reduce
  148.4 0.2 copy.35
  148.6 0.2 copy.32
  148.8 0.3 reshape.481
  149.1 0.6 gather_fusion.1
  149.8 2.5 %sort_prefixfusion = f32[16,16]{1,0:T(8,128)} fusion(f32[16,512]{1,0:T(8,128)S(1)} %broadcast_select_fusion), kind=kCustom, calls=%top_k.9.sort_prefix | custom fusion | flops 106496 | bytes 33792 | tf_op jit(solution)/shard_map/top_k | solution.py:180
  (76 shorter events, 5.1 us)
Async XLA Ops:
  5.2 1.0 copy-start
  5.3 1.3 copy-start.2
  7.2 6.7 %collective-permute-start = (bf16[8,8192]{1,0:T(8,128)(2,1)S(1)}, bf16[8,8192]{1,0:T(8,128)(2,1)S(1)}, u32[]{:S(2)}, u32[]{:S(2)}) collective-permute-start(bf16[8,8192]{1,0:T(8,128)(2,1)S(1)} %get-tuple-element.26), channel_id=1, source_target_pairs={{0,32},{32,64},{64,96},{96,0},{1,33},{33,65},{65,97},{97,1},{2,34}... | collective-permute-start | bytes 393224 | tf_op jit(solution)/shard_map/ppermute | solution.py:133
  9.4 8.3 %collective-permute-start.9 = (bf16[8,8192]{1,0:T(8,128)(2,1)S(1)}, bf16[8,8192]{1,0:T(8,128)(2,1)S(1)}, u32[]{:S(2)}, u32[]{:S(2)}) collective-permute-start(bf16[8,8192]{1,0:T(8,128)(2,1)S(1)} %get-tuple-element.25), channel_id=1, source_target_pairs={{0,64},{32,96},{64,0},{96,32},{1,65},{33,97},{65,1},{97,33},{2,66}... | collective-permute-start | bytes 393224 | tf_op jit(solution)/shard_map/ppermute | solution.py:133
  12.0 5.7 %collective-permute-start.10 = (bf16[8,8192]{1,0:T(8,128)(2,1)S(1)}, bf16[8,8192]{1,0:T(8,128)(2,1)S(1)}, u32[]{:S(2)}, u32[]{:S(2)}) collective-permute-start(bf16[8,8192]{1,0:T(8,128)(2,1)S(1)} %get-tuple-element.24), channel_id=1, source_target_pairs={{0,96},{32,0},{64,32},{96,64},{1,97},{33,1},{65,33},{97,65},{2,98}... | collective-permute-start | bytes 393224 | tf_op jit(solution)/shard_map/ppermute | solution.py:133
  13.9 7.8 %collective-permute-start.2 = (bf16[16,8192]{1,0:T(8,128)(2,1)S(1)}, bf16[16,8192]{1,0:T(8,128)(2,1)S(1)}, u32[]{:S(2)}, u32[]{:S(2)}) collective-permute-start(bf16[16,8192]{1,0:T(8,128)(2,1)S(1)} %get-tuple-element.28), channel_id=1, source_target_pairs={{0,8},{8,16},{16,24},{24,0},{1,9},{9,17},{17,25},{25,1},{2,10},{10... | collective-permute-start | bytes 786440 | tf_op jit(solution)/shard_map/ppermute | solution.py:103
  15.1 7.9 %collective-permute-start.1 = (bf16[16,8192]{1,0:T(8,128)(2,1)S(1)}, bf16[16,8192]{1,0:T(8,128)(2,1)S(1)}, u32[]{:S(2)}, u32[]{:S(2)}) collective-permute-start(bf16[16,8192]{1,0:T(8,128)(2,1)S(1)} %get-tuple-element.28), channel_id=1, source_target_pairs={{0,24},{8,0},{16,8},{24,16},{1,25},{9,1},{17,9},{25,17},{2,26},{10... | collective-permute-start | bytes 786440 | tf_op jit(solution)/shard_map/ppermute | solution.py:104
  17.8 9.0 %collective-permute-start.12 = (bf16[16,8192]{1,0:T(8,128)(2,1)S(1)}, bf16[16,8192]{1,0:T(8,128)(2,1)S(1)}, u32[]{:S(2)}, u32[]{:S(2)}) collective-permute-start(bf16[16,8192]{1,0:T(8,128)(2,1)S(1)} %constant_dynamic-update-slice_fusion), channel_id=1, source_target_pairs={{0,2},{2,4},{4,6},{6,0},{1,3},{3,5},{5,7},{7,1},{8,10},{10,12},{12... | collective-permute-start | bytes 786440 | tf_op jit(solution)/shard_map/ppermute | solution.py:103
  19.5 7.4 %collective-permute-start.11 = (bf16[16,8192]{1,0:T(8,128)(2,1)S(1)}, bf16[16,8192]{1,0:T(8,128)(2,1)S(1)}, u32[]{:S(2)}, u32[]{:S(2)}) collective-permute-start(bf16[16,8192]{1,0:T(8,128)(2,1)S(1)} %constant_dynamic-update-slice_fusion), channel_id=1, source_target_pairs={{0,6},{2,0},{4,2},{6,4},{1,7},{3,1},{5,3},{7,5},{8,14},{10,8},{12,... | collective-permute-start | bytes 786440 | tf_op jit(solution)/shard_map/ppermute | solution.py:104
  21.7 7.8 %collective-permute-start.3 = (bf16[8,8192]{1,0:T(8,128)(2,1)S(1)}, bf16[8,8192]{1,0:T(8,128)(2,1)S(1)}, u32[]{:S(2)}, u32[]{:S(2)}) collective-permute-start(bf16[8,8192]{1,0:T(8,128)(2,1)S(1)} %slice.120), channel_id=1, source_target_pairs={{0,8},{8,16},{16,24},{24,0},{1,9},{9,17},{17,25},{25,1},{2,10},{10... | collective-permute-start | bytes 393224 | tf_op jit(solution)/shard_map/ppermute | solution.py:105
  23.0 6.6 %collective-permute-start.4 = (bf16[8,8192]{1,0:T(8,128)(2,1)S(1)}, bf16[8,8192]{1,0:T(8,128)(2,1)S(1)}, u32[]{:S(2)}, u32[]{:S(2)}) collective-permute-start(bf16[8,8192]{1,0:T(8,128)(2,1)S(1)} %slice.121), channel_id=1, source_target_pairs={{0,24},{8,0},{16,8},{24,16},{1,25},{9,1},{17,9},{25,17},{2,26},{10... | collective-permute-start | bytes 393224 | tf_op jit(solution)/shard_map/ppermute | solution.py:106
  26.7 5.8 %collective-permute-start.13 = (bf16[8,8192]{1,0:T(8,128)(2,1)S(1)}, bf16[8,8192]{1,0:T(8,128)(2,1)S(1)}, u32[]{:S(2)}, u32[]{:S(2)}) collective-permute-start(bf16[8,8192]{1,0:T(8,128)(2,1)S(1)} %slice.124), channel_id=1, source_target_pairs={{0,2},{2,4},{4,6},{6,0},{1,3},{3,5},{5,7},{7,1},{8,10},{10,12},{12... | collective-permute-start | bytes 393224 | tf_op jit(solution)/shard_map/ppermute | solution.py:105
  26.8 5.6 %collective-permute-start.14 = (bf16[8,8192]{1,0:T(8,128)(2,1)S(1)}, bf16[8,8192]{1,0:T(8,128)(2,1)S(1)}, u32[]{:S(2)}, u32[]{:S(2)}) collective-permute-start(bf16[8,8192]{1,0:T(8,128)(2,1)S(1)} %slice.125), channel_id=1, source_target_pairs={{0,6},{2,0},{4,2},{6,4},{1,7},{3,1},{5,3},{7,5},{8,14},{10,8},{12,... | collective-permute-start | bytes 393224 | tf_op jit(solution)/shard_map/ppermute | solution.py:106
  29.7 25.3 %collective-permute-start.6 = (bf16[64,8192]{1,0:T(8,128)(2,1)S(1)}, bf16[64,8192]{1,0:T(8,128)(2,1)S(1)}, u32[]{:S(2)}, u32[]{:S(2)}) collective-permute-start(bf16[64,8192]{1,0:T(8,128)(2,1)S(1)} %bitcast.65), channel_id=1, source_target_pairs={{0,2},{2,4},{4,6},{6,0},{1,3},{3,5},{5,7},{7,1},{8,10},{10,12},{12... | collective-permute-start | bytes 3145736 | tf_op jit(solution)/shard_map/ppermute | solution.py:103
  29.8 25.3 %collective-permute-start.5 = (bf16[64,8192]{1,0:T(8,128)(2,1)S(1)}, bf16[64,8192]{1,0:T(8,128)(2,1)S(1)}, u32[]{:S(2)}, u32[]{:S(2)}) collective-permute-start(bf16[64,8192]{1,0:T(8,128)(2,1)S(1)} %bitcast.66), channel_id=1, source_target_pairs={{0,6},{2,0},{4,2},{6,4},{1,7},{3,1},{5,3},{7,5},{8,14},{10,8},{12,... | collective-permute-start | bytes 3145736 | tf_op jit(solution)/shard_map/ppermute | solution.py:104
  32.7 25.6 %collective-permute-start.16 = (bf16[64,8192]{1,0:T(8,128)(2,1)S(1)}, bf16[64,8192]{1,0:T(8,128)(2,1)S(1)}, u32[]{:S(2)}, u32[]{:S(2)}) collective-permute-start(bf16[64,8192]{1,0:T(8,128)(2,1)S(1)} %bitcast.68), channel_id=1, source_target_pairs={{0,8},{8,16},{16,24},{24,0},{1,9},{9,17},{17,25},{25,1},{2,10},{10... | collective-permute-start | bytes 3145736 | tf_op jit(solution)/shard_map/ppermute | solution.py:103
  33.9 25.6 %collective-permute-start.15 = (bf16[64,8192]{1,0:T(8,128)(2,1)S(1)}, bf16[64,8192]{1,0:T(8,128)(2,1)S(1)}, u32[]{:S(2)}, u32[]{:S(2)}) collective-permute-start(bf16[64,8192]{1,0:T(8,128)(2,1)S(1)} %bitcast.69), channel_id=1, source_target_pairs={{0,24},{8,0},{16,8},{24,16},{1,25},{9,1},{17,9},{25,17},{2,26},{10... | collective-permute-start | bytes 3145736 | tf_op jit(solution)/shard_map/ppermute | solution.py:104
  55.0 12.2 %collective-permute-start.7 = (bf16[32,8192]{1,0:T(8,128)(2,1)S(1)}, bf16[32,8192]{1,0:T(8,128)(2,1)S(1)}, u32[]{:S(2)}, u32[]{:S(2)}) collective-permute-start(bf16[32,8192]{1,0:T(8,128)(2,1)S(1)} %slice.122), channel_id=1, source_target_pairs={{0,2},{2,4},{4,6},{6,0},{1,3},{3,5},{5,7},{7,1},{8,10},{10,12},{12... | collective-permute-start | bytes 1572872 | tf_op jit(solution)/shard_map/ppermute | solution.py:105
  55.2 12.1 %collective-permute-start.8 = (bf16[32,8192]{1,0:T(8,128)(2,1)S(1)}, bf16[32,8192]{1,0:T(8,128)(2,1)S(1)}, u32[]{:S(2)}, u32[]{:S(2)}) collective-permute-start(bf16[32,8192]{1,0:T(8,128)(2,1)S(1)} %slice.123), channel_id=1, source_target_pairs={{0,6},{2,0},{4,2},{6,4},{1,7},{3,1},{5,3},{7,5},{8,14},{10,8},{12,... | collective-permute-start | bytes 1572872 | tf_op jit(solution)/shard_map/ppermute | solution.py:106
  58.3 12.0 %collective-permute-start.17 = (bf16[32,8192]{1,0:T(8,128)(2,1)S(1)}, bf16[32,8192]{1,0:T(8,128)(2,1)S(1)}, u32[]{:S(2)}, u32[]{:S(2)}) collective-permute-start(bf16[32,8192]{1,0:T(8,128)(2,1)S(1)} %slice.126), channel_id=1, source_target_pairs={{0,8},{8,16},{16,24},{24,0},{1,9},{9,17},{17,25},{25,1},{2,10},{10... | collective-permute-start | bytes 1572872 | tf_op jit(solution)/shard_map/ppermute | solution.py:105
  59.6 10.7 %collective-permute-start.18 = (bf16[32,8192]{1,0:T(8,128)(2,1)S(1)}, bf16[32,8192]{1,0:T(8,128)(2,1)S(1)}, u32[]{:S(2)}, u32[]{:S(2)}) collective-permute-start(bf16[32,8192]{1,0:T(8,128)(2,1)S(1)} %slice.127), channel_id=1, source_target_pairs={{0,24},{8,0},{16,8},{24,16},{1,25},{9,1},{17,9},{25,17},{2,26},{10... | collective-permute-start | bytes 1572872 | tf_op jit(solution)/shard_map/ppermute | solution.py:106
  80.3 24.9 %collective-permute-start.19 = (bf16[512,8192]{1,0:T(8,128)(2,1)}, bf16[512,8192]{1,0:T(8,128)(2,1)}, u32[]{:S(2)}, u32[]{:S(2)}) collective-permute-start(bf16[512,8192]{1,0:T(8,128)(2,1)} %pad_maximum_fusion), channel_id=1, source_target_pairs={{0,1},{1,0},{2,3},{3,2},{4,5},{5,4},{6,7},{7,6},{8,9},{9,8},{10,11... | collective-permute-start | bytes 25165832 | tf_op jit(solution)/shard_map/ppermute | solution.py:147
  105.1 20.6 %copy-start.1 = (f32[16,512]{1,0:T(8,128)S(1)}, f32[16,512]{1,0:T(8,128)}, u32[]{:S(2)}) copy-start(f32[16,512]{1,0:T(8,128)} %shard_map.46) | copy-start | bytes 98308

commit v7 on v6

--- a/solution.py
+++ b/solution.py
@@ -104,9 +104,11 @@
     from_plus = lax.ppermute(flat, axis, backward)
     far_first = lax.ppermute(from_minus[:half], axis, forward)
     far_second = lax.ppermute(from_plus[half:], axis, backward)
-    far = jnp.concatenate([far_first, far_second], axis=0)
-    stacked = jnp.stack([flat, from_plus, far, from_minus])
-    return stacked.reshape((size,) + block.shape)
+    return [flat, from_plus, far_first, far_second, from_minus]
+
+
+def stacked_ring(block, axis):
+    return jnp.concatenate(ring_gather(block, axis), axis=0).reshape((4,) + block.shape)
 
 
 def per_device(queries, library, routes, offsets):
@@ -138,11 +140,9 @@
         chunks.append(outgoing)
     arrived = jnp.concatenate(chunks, axis=0)
     part = arrived.shape[0] // 2
-    part_a = ring_gather(ring_gather(arrived[:part], "x"), "z")
-    part_b = ring_gather(ring_gather(arrived[part:], "z"), "x")
-    own_side = jnp.concatenate(
-        [part_a.reshape(-1, arrived.shape[1]), part_b.reshape(-1, arrived.shape[1])], axis=0
-    )
+    pieces_a = ring_gather(stacked_ring(arrived[:part], "x"), "z")
+    pieces_b = ring_gather(stacked_ring(arrived[part:], "z"), "x")
+    own_side = jnp.concatenate(pieces_a + pieces_b, axis=0)
     partner = [(core, core_count - 1 - core) for core in range(core_count)]
     other_side = lax.ppermute(own_side, "core", partner)
     own_best = column_topk(

time: 153 us -> 196 us (1.28)
  waiting for transfers between devices: 30.4 us -> 68 us
  local copies, waits for them, and re-layouts: 7.05 us -> 22.8 us
  other arithmetic: 22.3 us -> 9.73 us
  starting transfers between devices: 33.7 us -> 36.6 us
    ppermute x4, waiting for transfers between devices: 21.8 us -> 44 us  [ring_gather(): from_minus = lax.ppermute(flat, axis, forward)]
    ppermute x4, waiting for transfers between devices: 6.61 us -> 20.1 us  [ring_gather(): far_first = lax.ppermute(from_minus[:half], axis, forward)]
    unnamed x9 -> x25, local copies, waits for them, and re-layouts: 0.54 us -> 13.7 us
    concatenate x1, other arithmetic: 7.67 us -> 0.02 us  [per_device(): arrived = jnp.concatenate(chunks, axis=0)]
    ppermute x1, starting transfers between devices: 3.92 us -> 9.2 us  [per_device(): other_side = lax.ppermute(own_side, 'core', partner)]
    another operation x9 -> x0, other arithmetic: 4.97 us -> none  [ring_gather(): stacked = jnp.stack([flat, from_plus, far, from_minus])]
    ppermute x4, starting transfers between devices: 4.23 us -> 1.63 us  [ring_gather(): from_minus = lax.ppermute(flat, axis, forward)]
    concatenate x1 -> x3, local copies, waits for them, and re-layouts: 0.01 us -> 2.51 us  [the longest x2 1.47 us: stacked_ring(): jnp.concatenate(ring_gather(block, axis), axis=0)]
  transfers between devices with their start and end apart: 20 -> 20, of which waited for: 7 -> 9; matrix products, arithmetic and copies ran while one was open for 12% -> 14% of each run, Pallas kernels for 3% -> 2%
where the time goes in v7:
time: 196 us; the launch traced here: 195 us
  waiting for transfers between devices  68 us (35%)
  starting transfers between devices  36.6 us (19%)
  matrix products  32 us (16%)
  local copies, waits for them, and re-layouts  22.8 us (12%)
  blocking collectives  16.2 us (8%)
  other arithmetic  9.73 us (5%)
  Pallas kernels  9.67 us (5%)
    ppermute x4, waiting for transfers between devices, ring_gather(): from_minus = lax.ppermute(flat, axis, forward)  44 us
    ppermute x4, waiting for transfers between devices, ring_gather(): far_first = lax.ppermute(from_minus[:half], axis, forward)  20.1 us
    all_to_all x1, blocking collectives, per_device(): lax.all_to_all(outgoing, ('mass', 'x', 'z', 'core'), split_axis=0, concat...  16.2 us
    dot_general x1, matrix products, per_device(): lax.dot_general(library, own_side, (((1,), (1,)), ((), ())), preferred_el...  15.8 us
    dot_general x1, matrix products, per_device(): lax.dot_general(library, other_side, (((1,), (1,)), ((), ())), preferred_...  15.8 us
    unnamed x25, local copies, waits for them, and re-layouts  13.7 us
    ppermute x4, starting transfers between devices, ring_gather(): far_second = lax.ppermute(from_plus[half:], axis, backward)  11.1 us
    ppermute x4, starting transfers between devices, ring_gather(): from_plus = lax.ppermute(flat, axis, backward)  9.91 us
  transfers between devices with their start and end apart: 20, of which 9 were waited for; matrix products, arithmetic and copies ran while one was open for 14% of the time, Pallas kernels for 2%

profile of v7, /device:TPU:1, one launch (start us, length us, event | category | flops | bytes accessed | tf_op | source)
XLA Modules:
  0.0 195.2 jit_solution(8514593166439886181)
XLA Ops:
  0.7 1.0 pad_maximum_fusion
  1.8 1.1 pad_select_fusion.11
  7.1 2.2 %collective-permute-start = (bf16[8,8192]{1,0:T(8,128)(2,1)S(1)}, bf16[8,8192]{1,0:T(8,128)(2,1)S(1)}, u32[]{:S(2)}, u32[]{:S(2)}) collective-permute-start(bf16[8,8192]{1,0:T(8,128)(2,1)S(1)} %get-tuple-element.27), channel_id=1, source_target_pairs={{0,32},{32,64},{64,96},{96,0},{1,33},{33,65},{65,97},{97,1},{2,34}... | collective-permute-start | bytes 393224 | tf_op jit(solution)/shard_map/ppermute | solution.py:135
  9.9 3.8 %collective-permute-done = bf16[8,8192]{1,0:T(8,128)(2,1)S(1)} collective-permute-done((bf16[8,8192]{1,0:T(8,128)(2,1)S(1)}, bf16[8,8192]{1,0:T(8,128)(2,1)S(1)}, u32[]{:S(2)}, u32[]{:S(2)}) %collective-permute-start) | collective-permute-done | bytes 131104 | tf_op jit(solution)/shard_map/ppermute | solution.py:135
  13.8 2.4 %collective-permute-start.1 = (bf16[16,8192]{1,0:T(8,128)(2,1)S(1)}, bf16[16,8192]{1,0:T(8,128)(2,1)S(1)}, u32[]{:S(2)}, u32[]{:S(2)}) collective-permute-start(bf16[16,8192]{1,0:T(8,128)(2,1)S(1)} %pad_maximum_fusion.1), channel_id=1, source_target_pairs={{0,24},{8,0},{16,8},{24,16},{1,25},{9,1},{17,9},{25,17},{2,26},{10... | collective-permute-start | bytes 786440 | tf_op jit(solution)/shard_map/ppermute | solution.py:104
  16.9 6.7 %collective-permute-done.2 = bf16[16,8192]{1,0:T(8,128)(2,1)S(1)} collective-permute-done((bf16[16,8192]{1,0:T(8,128)(2,1)S(1)}, bf16[16,8192]{1,0:T(8,128)(2,1)S(1)}, u32[]{:S(2)}, u32[]{:S(2)}) %collective-permute-start.2) | collective-permute-done | bytes 262176 | tf_op jit(solution)/shard_map/ppermute | solution.py:103
  23.7 2.7 %collective-permute-start.4 = (bf16[8,8192]{1,0:T(8,128)(2,1)S(1)}, bf16[8,8192]{1,0:T(8,128)(2,1)S(1)}, u32[]{:S(2)}, u32[]{:S(2)}) collective-permute-start(bf16[8,8192]{1,0:T(8,128)(2,1)S(1)} %slice.121), channel_id=1, source_target_pairs={{0,24},{8,0},{16,8},{24,16},{1,25},{9,1},{17,9},{25,17},{2,26},{10... | collective-permute-start | bytes 393224 | tf_op jit(solution)/shard_map/ppermute | solution.py:106
  26.4 0.8 constant_dynamic-update-slice_fusion.3
  27.2 1.5 collective-permute-done.3
  29.4 0.7 constant_dynamic-update-slice_fusion.1
  30.0 0.7 constant_dynamic-update-slice_fusion
  30.8 1.6 collective-permute-start.6
  32.4 2.1 %collective-permute-start.5 = (bf16[64,8192]{1,0:T(8,128)(2,1)S(1)}, bf16[64,8192]{1,0:T(8,128)(2,1)S(1)}, u32[]{:S(2)}, u32[]{:S(2)}) collective-permute-start(bf16[64,8192]{1,0:T(8,128)(2,1)S(1)} %get-tuple-element.32), channel_id=1, source_target_pairs={{0,6},{2,0},{4,2},{6,4},{1,7},{3,1},{5,3},{7,5},{8,14},{10,8},{12,... | collective-permute-start | bytes 3145736 | tf_op jit(solution)/shard_map/ppermute | solution.py:104
  34.5 1.5 collective-permute-start.9
  36.0 0.8 collective-permute-start.10
  36.8 17.5 %collective-permute-done.6 = bf16[64,8192]{1,0:T(8,128)(2,1)S(1)} collective-permute-done((bf16[64,8192]{1,0:T(8,128)(2,1)S(1)}, bf16[64,8192]{1,0:T(8,128)(2,1)S(1)}, u32[]{:S(2)}, u32[]{:S(2)}) %collective-permute-start.6) | collective-permute-done | bytes 1048608 | tf_op jit(solution)/shard_map/ppermute | solution.py:103
  54.5 2.7 %collective-permute-start.8 = (bf16[32,8192]{1,0:T(8,128)(2,1)S(1)}, bf16[32,8192]{1,0:T(8,128)(2,1)S(1)}, u32[]{:S(2)}, u32[]{:S(2)}) collective-permute-start(bf16[32,8192]{1,0:T(8,128)(2,1)S(1)} %slice.123), channel_id=1, source_target_pairs={{0,6},{2,0},{4,2},{6,4},{1,7},{3,1},{5,3},{7,5},{8,14},{10,8},{12,... | collective-permute-start | bytes 1572872 | tf_op jit(solution)/shard_map/ppermute | solution.py:106
  57.2 1.0 constant_dynamic-update-slice_fusion.27
  58.2 6.5 %collective-permute-done.7 = bf16[32,8192]{1,0:T(8,128)(2,1)S(1)} collective-permute-done((bf16[32,8192]{1,0:T(8,128)(2,1)S(1)}, bf16[32,8192]{1,0:T(8,128)(2,1)S(1)}, u32[]{:S(2)}, u32[]{:S(2)}) %collective-permute-start.7) | collective-permute-done | bytes 524320 | tf_op jit(solution)/shard_map/ppermute | solution.py:105
  64.8 0.8 constant_dynamic-update-slice_fusion.26
  65.6 0.8 constant_dynamic-update-slice_fusion.25
  66.4 1.1 constant_dynamic-update-slice_fusion.24
  67.5 0.7 constant_dynamic-update-slice_fusion.13
  68.2 0.7 constant_dynamic-update-slice_fusion.12
  68.9 2.7 %collective-permute-start.11 = (bf16[16,8192]{1,0:T(8,128)(2,1)S(1)}, bf16[16,8192]{1,0:T(8,128)(2,1)S(1)}, u32[]{:S(2)}, u32[]{:S(2)}) collective-permute-start(bf16[16,8192]{1,0:T(8,128)(2,1)S(1)} %get-tuple-element.42), channel_id=1, source_target_pairs={{0,6},{2,0},{4,2},{6,4},{1,7},{3,1},{5,3},{7,5},{8,14},{10,8},{12,... | collective-permute-start | bytes 786440 | tf_op jit(solution)/shard_map/ppermute | solution.py:104
  71.5 3.8 %collective-permute-done.12 = bf16[16,8192]{1,0:T(8,128)(2,1)S(1)} collective-permute-done((bf16[16,8192]{1,0:T(8,128)(2,1)S(1)}, bf16[16,8192]{1,0:T(8,128)(2,1)S(1)}, u32[]{:S(2)}, u32[]{:S(2)}) %collective-permute-start.12) | collective-permute-done | bytes 262176 | tf_op jit(solution)/shard_map/ppermute | solution.py:103
  75.4 2.7 %collective-permute-start.14 = (bf16[8,8192]{1,0:T(8,128)(2,1)S(1)}, bf16[8,8192]{1,0:T(8,128)(2,1)S(1)}, u32[]{:S(2)}, u32[]{:S(2)}) collective-permute-start(bf16[8,8192]{1,0:T(8,128)(2,1)S(1)} %slice.125), channel_id=1, source_target_pairs={{0,6},{2,0},{4,2},{6,4},{1,7},{3,1},{5,3},{7,5},{8,14},{10,8},{12,... | collective-permute-start | bytes 393224 | tf_op jit(solution)/shard_map/ppermute | solution.py:106
  78.1 0.8 constant_dynamic-update-slice_fusion.11
  78.9 3.2 %collective-permute-done.13 = bf16[8,8192]{1,0:T(8,128)(2,1)S(1)} collective-permute-done((bf16[8,8192]{1,0:T(8,128)(2,1)S(1)}, bf16[8,8192]{1,0:T(8,128)(2,1)S(1)}, u32[]{:S(2)}, u32[]{:S(2)}) %collective-permute-start.13) | collective-permute-done | bytes 131104 | tf_op jit(solution)/shard_map/ppermute | solution.py:105
  83.4 0.7 constant_dynamic-update-slice_fusion.8
  84.2 2.7 %collective-permute-start.15 = (bf16[64,8192]{1,0:T(8,128)(2,1)S(1)}, bf16[64,8192]{1,0:T(8,128)(2,1)S(1)}, u32[]{:S(2)}, u32[]{:S(2)}) collective-permute-start(bf16[64,8192]{1,0:T(8,128)(2,1)S(1)} %get-tuple-element.28), channel_id=1, source_target_pairs={{0,24},{8,0},{16,8},{24,16},{1,25},{9,1},{17,9},{25,17},{2,26},{10... | collective-permute-start | bytes 3145736 | tf_op jit(solution)/shard_map/ppermute | solution.py:104
  86.8 16.1 %collective-permute-done.16 = bf16[64,8192]{1,0:T(8,128)(2,1)S(1)} collective-permute-done((bf16[64,8192]{1,0:T(8,128)(2,1)S(1)}, bf16[64,8192]{1,0:T(8,128)(2,1)S(1)}, u32[]{:S(2)}, u32[]{:S(2)}) %collective-permute-start.16) | collective-permute-done | bytes 1048608 | tf_op jit(solution)/shard_map/ppermute | solution.py:103
  103.1 2.9 %collective-permute-start.18 = (bf16[32,8192]{1,0:T(8,128)(2,1)S(1)}, bf16[32,8192]{1,0:T(8,128)(2,1)S(1)}, u32[]{:S(2)}, u32[]{:S(2)}) collective-permute-start(bf16[32,8192]{1,0:T(8,128)(2,1)S(1)} %slice.127), channel_id=1, source_target_pairs={{0,24},{8,0},{16,8},{24,16},{1,25},{9,1},{17,9},{25,17},{2,26},{10... | collective-permute-start | bytes 1572872 | tf_op jit(solution)/shard_map/ppermute | solution.py:106
  106.0 1.0 constant_dynamic-update-slice_fusion.17
  107.0 8.9 %collective-permute-done.17 = bf16[32,8192]{1,0:T(8,128)(2,1)S(1)} collective-permute-done((bf16[32,8192]{1,0:T(8,128)(2,1)S(1)}, bf16[32,8192]{1,0:T(8,128)(2,1)S(1)}, u32[]{:S(2)}, u32[]{:S(2)}) %collective-permute-start.17) | collective-permute-done | bytes 524320 | tf_op jit(solution)/shard_map/ppermute | solution.py:105
  115.9 0.8 constant_dynamic-update-slice_fusion.16
  116.7 0.8 constant_dynamic-update-slice_fusion.15
  117.6 1.0 constant_dynamic-update-slice_fusion.14
  118.6 9.2 %collective-permute-start.19 = (bf16[512,8192]{1,0:T(8,128)(2,1)}, bf16[512,8192]{1,0:T(8,128)(2,1)}, u32[]{:S(2)}, u32[]{:S(2)}) collective-permute-start(bf16[512,8192]{1,0:T(8,128)(2,1)} %constant_dynamic-update-slice_fusion.14), channel_id=1, source_target_pairs={{0,1},{1,0},{2,3},{3,2},{4,5},{5,4},{6,7},{7,6},{8,9},{9,8},{10,11... | collective-permute-start | bytes 25165832 | tf_op jit(solution)/shard_map/ppermute | solution.py:147
  128.1 15.8 %convolution_bitcast_fusion.1.scores_ref = f32[1024,512]{1,0:T(8,128)} fusion(bf16[512,8192]{1,0:T(8,128)(2,1)} %constant_dynamic-update-slice_fusion.14, bf16[1024,8192]{1,0:T(8,128)(2,1)} %param.7), kind=kOutput, calls=%fused_computation.5 | convolution fusion | flops 8589934592 | bytes 27262976 | tf_op jit(solution)/shard_map/dot_general | solution.py:149
  143.9 4.8 %shard_map.46 = f32[16,512]{1,0:T(8,128)} custom-call(f32[1024,512]{1,0:T(8,128)} %convolution_bitcast_fusion.1.scores_ref), custom_call_target="tpu_custom_call" | custom-call | flops 16777216 | bytes 2097152 | tf_op jit(solution)/shard_map/pallas_call | solution.py:85
  148.8 15.8 %convolution_bitcast_fusion.scores_ref = f32[1024,512]{1,0:T(8,128)} fusion(bf16[512,8192]{1,0:T(8,128)(2,1)} %collective-permute-done.19, bf16[1024,8192]{1,0:T(8,128)(2,1)} %param.7), kind=kOutput, calls=%fused_computation.4 | convolution fusion | flops 8589934592 | bytes 27262976 | tf_op jit(solution)/shard_map/dot_general | solution.py:154
  164.6 4.8 %shard_map.47 = f32[16,512]{1,0:T(8,128)} custom-call(f32[1024,512]{1,0:T(8,128)} %convolution_bitcast_fusion.scores_ref), custom_call_target="tpu_custom_call" | custom-call | flops 16777216 | bytes 2097152 | tf_op jit(solution)/shard_map/pallas_call | solution.py:85
  169.4 0.8 maximum_bitcast_fusion
  170.4 2.8 %gather_fusion = f32[1024,16]{1,0:T(8,128)S(1)} fusion(f32[1024,16]{1,0:T(8,128)S(1)} %copy.30, s32[1024]{0:T(1024)S(1)} %get-tuple-element.66), kind=kCustom, calls=%fused_computation | custom fusion | bytes 135168 | tf_op jit(solution)/shard_map/jit(_take)/gather | solution.py:173
  173.6 16.2 %all_to_all.5 = f32[128,1,128]{2,1,0:T(1,128)S(1)} all-to-all(f32[128,1,128]{2,1,0:T(1,128)S(1)} %reshape.565), channel_id=1, replica_groups=mesh['mass'=4,'x'=4,'z'=4,'core'=2] {'mass','x','z','core'}, dimensions={0} | all-to-all | bytes 131072 | tf_op jit(solution)/shard_map/all_to_all | solution.py:174
  190.3 0.8 reduce
  192.7 2.5 %sort_prefixfusion = f32[16,16]{1,0:T(8,128)} fusion(f32[16,512]{1,0:T(8,128)S(1)} %broadcast_select_fusion), kind=kCustom, calls=%top_k.9.sort_prefix | custom fusion | flops 106496 | bytes 33792 | tf_op jit(solution)/shard_map/top_k | solution.py:180
  (86 shorter events, 11.7 us)
Async XLA Ops:
  3.8 2.2 %copy-start = (bf16[16,8192]{1,0:T(8,128)(2,1)S(1)}, bf16[16,8192]{1,0:T(8,128)(2,1)}, u32[]{:S(2)}) copy-start(bf16[16,8192]{1,0:T(8,128)(2,1)} %param.6) | copy-start | bytes 786436
  4.0 2.4 %copy-start.2 = (s32[16,1]{0,1:T(1,128)S(1)}, s32[16,1]{0,1:T(1,128)}, u32[]{:S(2)}) copy-start(s32[16,1]{0,1:T(1,128)} %param.8) | copy-start | bytes 196
  7.1 6.7 %collective-permute-start = (bf16[8,8192]{1,0:T(8,128)(2,1)S(1)}, bf16[8,8192]{1,0:T(8,128)(2,1)S(1)}, u32[]{:S(2)}, u32[]{:S(2)}) collective-permute-start(bf16[8,8192]{1,0:T(8,128)(2,1)S(1)} %get-tuple-element.27), channel_id=1, source_target_pairs={{0,32},{32,64},{64,96},{96,0},{1,33},{33,65},{65,97},{97,1},{2,34}... | collective-permute-start | bytes 393224 | tf_op jit(solution)/shard_map/ppermute | solution.py:135
  13.8 9.9 %collective-permute-start.1 = (bf16[16,8192]{1,0:T(8,128)(2,1)S(1)}, bf16[16,8192]{1,0:T(8,128)(2,1)S(1)}, u32[]{:S(2)}, u32[]{:S(2)}) collective-permute-start(bf16[16,8192]{1,0:T(8,128)(2,1)S(1)} %pad_maximum_fusion.1), channel_id=1, source_target_pairs={{0,24},{8,0},{16,8},{24,16},{1,25},{9,1},{17,9},{25,17},{2,26},{10... | collective-permute-start | bytes 786440 | tf_op jit(solution)/shard_map/ppermute | solution.py:104
  16.2 7.3 %collective-permute-start.2 = (bf16[16,8192]{1,0:T(8,128)(2,1)S(1)}, bf16[16,8192]{1,0:T(8,128)(2,1)S(1)}, u32[]{:S(2)}, u32[]{:S(2)}) collective-permute-start(bf16[16,8192]{1,0:T(8,128)(2,1)S(1)} %pad_maximum_fusion.1), channel_id=1, source_target_pairs={{0,8},{8,16},{16,24},{24,0},{1,9},{9,17},{17,25},{25,1},{2,10},{10... | collective-permute-start | bytes 786440 | tf_op jit(solution)/shard_map/ppermute | solution.py:103
  23.6 5.1 %collective-permute-start.3 = (bf16[8,8192]{1,0:T(8,128)(2,1)S(1)}, bf16[8,8192]{1,0:T(8,128)(2,1)S(1)}, u32[]{:S(2)}, u32[]{:S(2)}) collective-permute-start(bf16[8,8192]{1,0:T(8,128)(2,1)S(1)} %slice.120), channel_id=1, source_target_pairs={{0,8},{8,16},{16,24},{24,0},{1,9},{9,17},{17,25},{25,1},{2,10},{10... | collective-permute-start | bytes 393224 | tf_op jit(solution)/shard_map/ppermute | solution.py:105
  23.7 5.7 %collective-permute-start.4 = (bf16[8,8192]{1,0:T(8,128)(2,1)S(1)}, bf16[8,8192]{1,0:T(8,128)(2,1)S(1)}, u32[]{:S(2)}, u32[]{:S(2)}) collective-permute-start(bf16[8,8192]{1,0:T(8,128)(2,1)S(1)} %slice.121), channel_id=1, source_target_pairs={{0,24},{8,0},{16,8},{24,16},{1,25},{9,1},{17,9},{25,17},{2,26},{10... | collective-permute-start | bytes 393224 | tf_op jit(solution)/shard_map/ppermute | solution.py:106
  30.8 23.5 %collective-permute-start.6 = (bf16[64,8192]{1,0:T(8,128)(2,1)S(1)}, bf16[64,8192]{1,0:T(8,128)(2,1)S(1)}, u32[]{:S(2)}, u32[]{:S(2)}) collective-permute-start(bf16[64,8192]{1,0:T(8,128)(2,1)S(1)} %get-tuple-element.32), channel_id=1, source_target_pairs={{0,2},{2,4},{4,6},{6,0},{1,3},{3,5},{5,7},{7,1},{8,10},{10,12},{12... | collective-permute-start | bytes 3145736 | tf_op jit(solution)/shard_map/ppermute | solution.py:103
  32.4 22.0 %collective-permute-start.5 = (bf16[64,8192]{1,0:T(8,128)(2,1)S(1)}, bf16[64,8192]{1,0:T(8,128)(2,1)S(1)}, u32[]{:S(2)}, u32[]{:S(2)}) collective-permute-start(bf16[64,8192]{1,0:T(8,128)(2,1)S(1)} %get-tuple-element.32), channel_id=1, source_target_pairs={{0,6},{2,0},{4,2},{6,4},{1,7},{3,1},{5,3},{7,5},{8,14},{10,8},{12,... | collective-permute-start | bytes 3145736 | tf_op jit(solution)/shard_map/ppermute | solution.py:104
  34.5 33.0 %collective-permute-start.9 = (bf16[8,8192]{1,0:T(8,128)(2,1)S(1)}, bf16[8,8192]{1,0:T(8,128)(2,1)S(1)}, u32[]{:S(2)}, u32[]{:S(2)}) collective-permute-start(bf16[8,8192]{1,0:T(8,128)(2,1)S(1)} %get-tuple-element.26), channel_id=1, source_target_pairs={{0,64},{32,96},{64,0},{96,32},{1,65},{33,97},{65,1},{97,33},{2,66}... | collective-permute-start | bytes 393224 | tf_op jit(solution)/shard_map/ppermute | solution.py:135
  36.0 32.1 %collective-permute-start.10 = (bf16[8,8192]{1,0:T(8,128)(2,1)S(1)}, bf16[8,8192]{1,0:T(8,128)(2,1)S(1)}, u32[]{:S(2)}, u32[]{:S(2)}) collective-permute-start(bf16[8,8192]{1,0:T(8,128)(2,1)S(1)} %get-tuple-element.25), channel_id=1, source_target_pairs={{0,96},{32,0},{64,32},{96,64},{1,97},{33,1},{65,33},{97,65},{2,98}... | collective-permute-start | bytes 393224 | tf_op jit(solution)/shard_map/ppermute | solution.py:135
  54.3 10.4 %collective-permute-start.7 = (bf16[32,8192]{1,0:T(8,128)(2,1)S(1)}, bf16[32,8192]{1,0:T(8,128)(2,1)S(1)}, u32[]{:S(2)}, u32[]{:S(2)}) collective-permute-start(bf16[32,8192]{1,0:T(8,128)(2,1)S(1)} %slice.122), channel_id=1, source_target_pairs={{0,2},{2,4},{4,6},{6,0},{1,3},{3,5},{5,7},{7,1},{8,10},{10,12},{12... | collective-permute-start | bytes 1572872 | tf_op jit(solution)/shard_map/ppermute | solution.py:105
  54.5 11.1 %collective-permute-start.8 = (bf16[32,8192]{1,0:T(8,128)(2,1)S(1)}, bf16[32,8192]{1,0:T(8,128)(2,1)S(1)}, u32[]{:S(2)}, u32[]{:S(2)}) collective-permute-start(bf16[32,8192]{1,0:T(8,128)(2,1)S(1)} %slice.123), channel_id=1, source_target_pairs={{0,6},{2,0},{4,2},{6,4},{1,7},{3,1},{5,3},{7,5},{8,14},{10,8},{12,... | collective-permute-start | bytes 1572872 | tf_op jit(solution)/shard_map/ppermute | solution.py:106
  68.9 6.4 %collective-permute-start.12 = (bf16[16,8192]{1,0:T(8,128)(2,1)S(1)}, bf16[16,8192]{1,0:T(8,128)(2,1)S(1)}, u32[]{:S(2)}, u32[]{:S(2)}) collective-permute-start(bf16[16,8192]{1,0:T(8,128)(2,1)S(1)} %get-tuple-element.42), channel_id=1, source_target_pairs={{0,2},{2,4},{4,6},{6,0},{1,3},{3,5},{5,7},{7,1},{8,10},{10,12},{12... | collective-permute-start | bytes 786440 | tf_op jit(solution)/shard_map/ppermute | solution.py:103
  68.9 6.5 %collective-permute-start.11 = (bf16[16,8192]{1,0:T(8,128)(2,1)S(1)}, bf16[16,8192]{1,0:T(8,128)(2,1)S(1)}, u32[]{:S(2)}, u32[]{:S(2)}) collective-permute-start(bf16[16,8192]{1,0:T(8,128)(2,1)S(1)} %get-tuple-element.42), channel_id=1, source_target_pairs={{0,6},{2,0},{4,2},{6,4},{1,7},{3,1},{5,3},{7,5},{8,14},{10,8},{12,... | collective-permute-start | bytes 786440 | tf_op jit(solution)/shard_map/ppermute | solution.py:104
  75.3 6.8 %collective-permute-start.13 = (bf16[8,8192]{1,0:T(8,128)(2,1)S(1)}, bf16[8,8192]{1,0:T(8,128)(2,1)S(1)}, u32[]{:S(2)}, u32[]{:S(2)}) collective-permute-start(bf16[8,8192]{1,0:T(8,128)(2,1)S(1)} %slice.124), channel_id=1, source_target_pairs={{0,2},{2,4},{4,6},{6,0},{1,3},{3,5},{5,7},{7,1},{8,10},{10,12},{12... | collective-permute-start | bytes 393224 | tf_op jit(solution)/shard_map/ppermute | solution.py:105
  75.4 7.4 %collective-permute-start.14 = (bf16[8,8192]{1,0:T(8,128)(2,1)S(1)}, bf16[8,8192]{1,0:T(8,128)(2,1)S(1)}, u32[]{:S(2)}, u32[]{:S(2)}) collective-permute-start(bf16[8,8192]{1,0:T(8,128)(2,1)S(1)} %slice.125), channel_id=1, source_target_pairs={{0,6},{2,0},{4,2},{6,4},{1,7},{3,1},{5,3},{7,5},{8,14},{10,8},{12,... | collective-permute-start | bytes 393224 | tf_op jit(solution)/shard_map/ppermute | solution.py:106
  84.2 18.7 %collective-permute-start.16 = (bf16[64,8192]{1,0:T(8,128)(2,1)S(1)}, bf16[64,8192]{1,0:T(8,128)(2,1)S(1)}, u32[]{:S(2)}, u32[]{:S(2)}) collective-permute-start(bf16[64,8192]{1,0:T(8,128)(2,1)S(1)} %get-tuple-element.28), channel_id=1, source_target_pairs={{0,8},{8,16},{16,24},{24,0},{1,9},{9,17},{17,25},{25,1},{2,10},{10... | collective-permute-start | bytes 3145736 | tf_op jit(solution)/shard_map/ppermute | solution.py:103
  84.2 18.9 %collective-permute-start.15 = (bf16[64,8192]{1,0:T(8,128)(2,1)S(1)}, bf16[64,8192]{1,0:T(8,128)(2,1)S(1)}, u32[]{:S(2)}, u32[]{:S(2)}) collective-permute-start(bf16[64,8192]{1,0:T(8,128)(2,1)S(1)} %get-tuple-element.28), channel_id=1, source_target_pairs={{0,24},{8,0},{16,8},{24,16},{1,25},{9,1},{17,9},{25,17},{2,26},{10... | collective-permute-start | bytes 3145736 | tf_op jit(solution)/shard_map/ppermute | solution.py:104
  102.9 12.9 %collective-permute-start.17 = (bf16[32,8192]{1,0:T(8,128)(2,1)S(1)}, bf16[32,8192]{1,0:T(8,128)(2,1)S(1)}, u32[]{:S(2)}, u32[]{:S(2)}) collective-permute-start(bf16[32,8192]{1,0:T(8,128)(2,1)S(1)} %slice.126), channel_id=1, source_target_pairs={{0,8},{8,16},{16,24},{24,0},{1,9},{9,17},{17,25},{25,1},{2,10},{10... | collective-permute-start | bytes 1572872 | tf_op jit(solution)/shard_map/ppermute | solution.py:105
  103.1 13.6 %collective-permute-start.18 = (bf16[32,8192]{1,0:T(8,128)(2,1)S(1)}, bf16[32,8192]{1,0:T(8,128)(2,1)S(1)}, u32[]{:S(2)}, u32[]{:S(2)}) collective-permute-start(bf16[32,8192]{1,0:T(8,128)(2,1)S(1)} %slice.127), channel_id=1, source_target_pairs={{0,24},{8,0},{16,8},{24,16},{1,25},{9,1},{17,9},{25,17},{2,26},{10... | collective-permute-start | bytes 1572872 | tf_op jit(solution)/shard_map/ppermute | solution.py:106
  118.6 30.2 %collective-permute-start.19 = (bf16[512,8192]{1,0:T(8,128)(2,1)}, bf16[512,8192]{1,0:T(8,128)(2,1)}, u32[]{:S(2)}, u32[]{:S(2)}) collective-permute-start(bf16[512,8192]{1,0:T(8,128)(2,1)} %constant_dynamic-update-slice_fusion.14), channel_id=1, source_target_pairs={{0,1},{1,0},{2,3},{3,2},{4,5},{5,4},{6,7},{7,6},{8,9},{9,8},{10,11... | collective-permute-start | bytes 25165832 | tf_op jit(solution)/shard_map/ppermute | solution.py:147
  148.8 20.6 %copy-start.1 = (f32[16,512]{1,0:T(8,128)S(1)}, f32[16,512]{1,0:T(8,128)}, u32[]{:S(2)}) copy-start(f32[16,512]{1,0:T(8,128)} %shard_map.46) | copy-start | bytes 98308

commit v8 on v6

--- a/solution.py
+++ b/solution.py
@@ -56,20 +56,37 @@
     return merged
 
 
+def bitonic_sort(values):
+    values = list(values)
+    width = 2
+    while width <= TOP_K:
+        span = width // 2
+        while span >= 1:
+            for i in range(TOP_K):
+                j = i ^ span
+                if j > i:
+                    high = jnp.maximum(values[i], values[j])
+                    low = jnp.minimum(values[i], values[j])
+                    if i & width == 0:
+                        values[i], values[j] = high, low
+                    else:
+                        values[i], values[j] = low, high
+            span //= 2
+        width *= 2
+    return values
+
+
 def column_topk_kernel(scores_ref, out_ref):
-    steps = scores_ref.shape[0] // SUBLANES
+    group = SUBLANES * TOP_K
+    steps = scores_ref.shape[0] // group
     lowest = jnp.full((SUBLANES, LANES), -jnp.inf, jnp.float32)
 
     def insert(step, kept):
-        start = pl.multiple_of(step * SUBLANES, SUBLANES)
-        value = scores_ref[pl.ds(start, SUBLANES), :]
-        updated = []
-        for k in range(TOP_K):
-            updated.append(jnp.maximum(kept[k], value))
-            value = jnp.minimum(kept[k], value)
-        return tuple(updated)
-
-    kept = lax.fori_loop(0, steps, insert, (lowest,) * TOP_K, unroll=8)
+        start = pl.multiple_of(step * group, group)
+        values = [scores_ref[pl.ds(start + SUBLANES * k, SUBLANES), :] for k in range(TOP_K)]
+        return tuple(merge_sorted(list(kept), bitonic_sort(values)))
+
+    kept = lax.fori_loop(0, steps, insert, (lowest,) * TOP_K, unroll=2)
     kept = list(kept)
     shift = SUBLANES // 2
     while shift >= 1:

time: 153 us -> 151 us (0.987)
  Pallas kernels: 9.68 us -> 7.86 us
    pallas_call x2, Pallas kernels: 9.68 us -> 7.86 us  [column_topk(): pl.pallas_call(column_topk_kernel, out_shape=jax.ShapeDtypeStruct((TOP_K,...]
  transfers between devices with their start and end apart: 20 -> 20, of which waited for: 7 -> 7; matrix products, arithmetic and copies ran while one was open for 12% -> 13% of each run, Pallas kernels for 3% -> 3%
where the time goes in v8:
time: 151 us; the launch traced here: 150 us
  starting transfers between devices  33.7 us (22%)
  matrix products  32 us (21%)
  waiting for transfers between devices  30.3 us (20%)
  other arithmetic  22.3 us (15%)
  blocking collectives  16.8 us (11%)
  Pallas kernels  7.86 us (5%)
  local copies, waits for them, and re-layouts  7.05 us (5%)
    ppermute x4, waiting for transfers between devices, ring_gather(): from_minus = lax.ppermute(flat, axis, forward)  21.8 us
    all_to_all x1, blocking collectives, per_device(): lax.all_to_all(outgoing, ('mass', 'x', 'z', 'core'), split_axis=0, concat...  16.8 us
    dot_general x1, matrix products, per_device(): lax.dot_general(library, own_side, (((1,), (1,)), ((), ())), preferred_el...  15.8 us
    dot_general x1, matrix products, per_device(): lax.dot_general(library, other_side, (((1,), (1,)), ((), ())), preferred_...  15.8 us
    ppermute x4, starting transfers between devices, ring_gather(): far_second = lax.ppermute(from_plus[half:], axis, backward)  9.09 us
    ppermute x4, starting transfers between devices, ring_gather(): from_plus = lax.ppermute(flat, axis, backward)  7.9 us
    pallas_call x2, Pallas kernels, column_topk(): pl.pallas_call(column_topk_kernel, out_shape=jax.ShapeDtypeStruct((TOP_K,...  7.86 us
    concatenate x1, other arithmetic, per_device(): jnp.concatenate([part_a.reshape(-1, arrived.shape[1]), part_b.reshape(-1,...  7.67 us
  transfers between devices with their start and end apart: 20, of which 7 were waited for; matrix products, arithmetic and copies ran while one was open for 13% of the time, Pallas kernels for 3%

profile of v8, /device:TPU:1, one launch (start us, length us, event | category | flops | bytes accessed | tf_op | source)
XLA Modules:
  0.0 150.5 jit_solution(441375244236108717)
XLA Ops:
  0.0 0.7 and_compare_fusion.12
  0.7 1.0 pad_maximum_fusion.5
  1.8 1.1 pad_select_fusion.11
  6.2 0.4 multiply_reduce_fusion
  6.7 0.4 fusion
  7.2 2.2 %collective-permute-start = (bf16[8,8192]{1,0:T(8,128)(2,1)S(1)}, bf16[8,8192]{1,0:T(8,128)(2,1)S(1)}, u32[]{:S(2)}, u32[]{:S(2)}) collective-permute-start(bf16[8,8192]{1,0:T(8,128)(2,1)S(1)} %get-tuple-element.26), channel_id=1, source_target_pairs={{0,32},{32,64},{64,96},{96,0},{1,33},{33,65},{65,97},{97,1},{2,34}... | collective-permute-start | bytes 393224 | tf_op jit(solution)/shard_map/ppermute | solution.py:150
  9.4 2.6 %collective-permute-start.9 = (bf16[8,8192]{1,0:T(8,128)(2,1)S(1)}, bf16[8,8192]{1,0:T(8,128)(2,1)S(1)}, u32[]{:S(2)}, u32[]{:S(2)}) collective-permute-start(bf16[8,8192]{1,0:T(8,128)(2,1)S(1)} %get-tuple-element.25), channel_id=1, source_target_pairs={{0,64},{32,96},{64,0},{96,32},{1,65},{33,97},{65,1},{97,33},{2,66}... | collective-permute-start | bytes 393224 | tf_op jit(solution)/shard_map/ppermute | solution.py:150
  12.0 1.1 collective-permute-start.10
  13.1 0.8 collective-permute-done
  13.9 1.2 collective-permute-start.2
  15.1 1.6 %collective-permute-start.1 = (bf16[16,8192]{1,0:T(8,128)(2,1)S(1)}, bf16[16,8192]{1,0:T(8,128)(2,1)S(1)}, u32[]{:S(2)}, u32[]{:S(2)}) collective-permute-start(bf16[16,8192]{1,0:T(8,128)(2,1)S(1)} %get-tuple-element.28), channel_id=1, source_target_pairs={{0,24},{8,0},{16,8},{24,16},{1,25},{9,1},{17,9},{25,17},{2,26},{10... | collective-permute-start | bytes 786440 | tf_op jit(solution)/shard_map/ppermute | solution.py:121
  16.7 1.0 collective-permute-done.9
  17.8 1.7 %collective-permute-start.12 = (bf16[16,8192]{1,0:T(8,128)(2,1)S(1)}, bf16[16,8192]{1,0:T(8,128)(2,1)S(1)}, u32[]{:S(2)}, u32[]{:S(2)}) collective-permute-start(bf16[16,8192]{1,0:T(8,128)(2,1)S(1)} %constant_dynamic-update-slice_fusion), channel_id=1, source_target_pairs={{0,2},{2,4},{4,6},{6,0},{1,3},{3,5},{5,7},{7,1},{8,10},{10,12},{12... | collective-permute-start | bytes 786440 | tf_op jit(solution)/shard_map/ppermute | solution.py:120
  19.5 2.2 %collective-permute-start.11 = (bf16[16,8192]{1,0:T(8,128)(2,1)S(1)}, bf16[16,8192]{1,0:T(8,128)(2,1)S(1)}, u32[]{:S(2)}, u32[]{:S(2)}) collective-permute-start(bf16[16,8192]{1,0:T(8,128)(2,1)S(1)} %constant_dynamic-update-slice_fusion), channel_id=1, source_target_pairs={{0,6},{2,0},{4,2},{6,4},{1,7},{3,1},{5,3},{7,5},{8,14},{10,8},{12,... | collective-permute-start | bytes 786440 | tf_op jit(solution)/shard_map/ppermute | solution.py:121
  21.7 1.2 collective-permute-start.3
  23.0 1.6 %collective-permute-start.4 = (bf16[8,8192]{1,0:T(8,128)(2,1)S(1)}, bf16[8,8192]{1,0:T(8,128)(2,1)S(1)}, u32[]{:S(2)}, u32[]{:S(2)}) collective-permute-start(bf16[8,8192]{1,0:T(8,128)(2,1)S(1)} %slice.121), channel_id=1, source_target_pairs={{0,24},{8,0},{16,8},{24,16},{1,25},{9,1},{17,9},{25,17},{2,26},{10... | collective-permute-start | bytes 393224 | tf_op jit(solution)/shard_map/ppermute | solution.py:123
  24.6 2.1 %collective-permute-done.12 = bf16[16,8192]{1,0:T(8,128)(2,1)S(1)} collective-permute-done((bf16[16,8192]{1,0:T(8,128)(2,1)S(1)}, bf16[16,8192]{1,0:T(8,128)(2,1)S(1)}, u32[]{:S(2)}, u32[]{:S(2)}) %collective-permute-start.12) | collective-permute-done | bytes 262176 | tf_op jit(solution)/shard_map/ppermute | solution.py:120
  26.8 2.7 %collective-permute-start.14 = (bf16[8,8192]{1,0:T(8,128)(2,1)S(1)}, bf16[8,8192]{1,0:T(8,128)(2,1)S(1)}, u32[]{:S(2)}, u32[]{:S(2)}) collective-permute-start(bf16[8,8192]{1,0:T(8,128)(2,1)S(1)} %slice.125), channel_id=1, source_target_pairs={{0,6},{2,0},{4,2},{6,4},{1,7},{3,1},{5,3},{7,5},{8,14},{10,8},{12,... | collective-permute-start | bytes 393224 | tf_op jit(solution)/shard_map/ppermute | solution.py:123
  29.8 2.7 %collective-permute-start.5 = (bf16[64,8192]{1,0:T(8,128)(2,1)S(1)}, bf16[64,8192]{1,0:T(8,128)(2,1)S(1)}, u32[]{:S(2)}, u32[]{:S(2)}) collective-permute-start(bf16[64,8192]{1,0:T(8,128)(2,1)S(1)} %bitcast.66), channel_id=1, source_target_pairs={{0,6},{2,0},{4,2},{6,4},{1,7},{3,1},{5,3},{7,5},{8,14},{10,8},{12,... | collective-permute-start | bytes 3145736 | tf_op jit(solution)/shard_map/ppermute | solution.py:121
  32.7 1.3 collective-permute-start.16
  33.9 1.5 collective-permute-start.15
  35.4 19.6 %collective-permute-done.6 = bf16[64,8192]{1,0:T(8,128)(2,1)S(1)} collective-permute-done((bf16[64,8192]{1,0:T(8,128)(2,1)S(1)}, bf16[64,8192]{1,0:T(8,128)(2,1)S(1)}, u32[]{:S(2)}, u32[]{:S(2)}) %collective-permute-start.6) | collective-permute-done | bytes 1048608 | tf_op jit(solution)/shard_map/ppermute | solution.py:120
  55.2 3.1 %collective-permute-start.8 = (bf16[32,8192]{1,0:T(8,128)(2,1)S(1)}, bf16[32,8192]{1,0:T(8,128)(2,1)S(1)}, u32[]{:S(2)}, u32[]{:S(2)}) collective-permute-start(bf16[32,8192]{1,0:T(8,128)(2,1)S(1)} %slice.123), channel_id=1, source_target_pairs={{0,6},{2,0},{4,2},{6,4},{1,7},{3,1},{5,3},{7,5},{8,14},{10,8},{12,... | collective-permute-start | bytes 1572872 | tf_op jit(solution)/shard_map/ppermute | solution.py:123
  58.3 1.3 collective-permute-start.17
  59.6 1.7 %collective-permute-start.18 = (bf16[32,8192]{1,0:T(8,128)(2,1)S(1)}, bf16[32,8192]{1,0:T(8,128)(2,1)S(1)}, u32[]{:S(2)}, u32[]{:S(2)}) collective-permute-start(bf16[32,8192]{1,0:T(8,128)(2,1)S(1)} %slice.127), channel_id=1, source_target_pairs={{0,24},{8,0},{16,8},{24,16},{1,25},{9,1},{17,9},{25,17},{2,26},{10... | collective-permute-start | bytes 1572872 | tf_op jit(solution)/shard_map/ppermute | solution.py:123
  61.3 5.9 %collective-permute-done.7 = bf16[32,8192]{1,0:T(8,128)(2,1)S(1)} collective-permute-done((bf16[32,8192]{1,0:T(8,128)(2,1)S(1)}, bf16[32,8192]{1,0:T(8,128)(2,1)S(1)}, u32[]{:S(2)}, u32[]{:S(2)}) %collective-permute-start.7) | collective-permute-done | bytes 524320 | tf_op jit(solution)/shard_map/ppermute | solution.py:122
  67.3 2.3 %pad_maximum_fusion.1 = bf16[4,64,8192]{2,1,0:T(8,128)(2,1)} fusion(bf16[1,64,8192]{2,1,0:T(8,128)(2,1)S(1)} %bitcast.71, bf16[1,64,8192]{2,1,0:T(8,128)(2,1)S(1)} %maximum_bitcast_fusion, bf16[1,64,8192]{2,1,0:T(8,128)(2,1)S(1)} %bitcast.72, bf16[1,64,8192]{2,1,0:T(8,128)(2,1)S(1)} %bitcast.67), kind=kLoop, calls=%fused_computation.5 | loop fusion | flops 6291456 | bytes 8388608 | tf_op jit(solution)/shard_map/stack | solution.py:125
  69.6 0.7 collective-permute-done.17
  70.4 2.2 %pad_maximum_fusion.2 = bf16[4,64,8192]{2,1,0:T(8,128)(2,1)} fusion(bf16[1,64,8192]{2,1,0:T(8,128)(2,1)S(1)} %bitcast.73, bf16[1,64,8192]{2,1,0:T(8,128)(2,1)S(1)} %maximum_bitcast_fusion.1, bf16[1,64,8192]{2,1,0:T(8,128)(2,1)S(1)} %bitcast.74, bf16[1,64,8192]{2,1,0:T(8,128)(2,1)S(1)} %bitcast.70), kind=kLoop, calls=%fused_computation.6 | loop fusion | flops 6291456 | bytes 8388608 | tf_op jit(solution)/shard_map/stack | solution.py:125
  72.6 7.7 %pad_maximum_fusion = bf16[512,8192]{1,0:T(8,128)(2,1)} fusion(bf16[256,8192]{1,0:T(8,128)(2,1)} %bitcast.63, bf16[256,8192]{1,0:T(8,128)(2,1)} %bitcast.61), kind=kLoop, calls=%fused_computation.4 | loop fusion | flops 16777216 | bytes 16777216 | tf_op jit(solution)/shard_map/concatenate | solution.py:160
  80.3 3.9 %collective-permute-start.19 = (bf16[512,8192]{1,0:T(8,128)(2,1)}, bf16[512,8192]{1,0:T(8,128)(2,1)}, u32[]{:S(2)}, u32[]{:S(2)}) collective-permute-start(bf16[512,8192]{1,0:T(8,128)(2,1)} %pad_maximum_fusion), channel_id=1, source_target_pairs={{0,1},{1,0},{2,3},{3,2},{4,5},{5,4},{6,7},{7,6},{8,9},{9,8},{10,11... | collective-permute-start | bytes 25165832 | tf_op jit(solution)/shard_map/ppermute | solution.py:164
  84.5 15.8 %convolution_bitcast_fusion.1.scores_ref = f32[1024,512]{1,0:T(8,128)} fusion(bf16[1024,8192]{1,0:T(8,128)(2,1)} %param.7, bf16[256,8192]{1,0:T(8,128)(2,1)} %bitcast.64, bf16[256,8192]{1,0:T(8,128)(2,1)} %bitcast.62), kind=kOutput, calls=%fused_computation.8 | convolution fusion | flops 8606711808 | bytes 27262976 | tf_op jit(solution)/shard_map/dot_general | solution.py:166
  100.3 3.9 %shard_map.46 = f32[16,512]{1,0:T(8,128)} custom-call(f32[1024,512]{1,0:T(8,128)} %convolution_bitcast_fusion.1.scores_ref), custom_call_target="tpu_custom_call" | custom-call | flops 16777216 | bytes 2097152 | tf_op jit(solution)/shard_map/pallas_call | solution.py:102
  104.2 15.8 %convolution_bitcast_fusion.scores_ref = f32[1024,512]{1,0:T(8,128)} fusion(bf16[512,8192]{1,0:T(8,128)(2,1)} %collective-permute-done.19, bf16[1024,8192]{1,0:T(8,128)(2,1)} %param.7), kind=kOutput, calls=%fused_computation.7 | convolution fusion | flops 8589934592 | bytes 27262976 | tf_op jit(solution)/shard_map/dot_general | solution.py:171
  120.0 3.9 %shard_map.47 = f32[16,512]{1,0:T(8,128)} custom-call(f32[1024,512]{1,0:T(8,128)} %convolution_bitcast_fusion.scores_ref), custom_call_target="tpu_custom_call" | custom-call | flops 16777216 | bytes 2097152 | tf_op jit(solution)/shard_map/pallas_call | solution.py:102
  124.0 0.8 maximum_bitcast_fusion.4
  124.7 0.2 copy.30
  124.9 2.8 %gather_fusion = f32[1024,16]{1,0:T(8,128)S(1)} fusion(f32[1024,16]{1,0:T(8,128)S(1)} %copy.30, s32[1024]{0:T(1024)S(1)} %get-tuple-element.43), kind=kCustom, calls=%fused_computation | custom fusion | bytes 135168 | tf_op jit(solution)/shard_map/jit(_take)/gather | solution.py:190
  127.8 0.2 bitcast_select_fusion
  128.0 0.2 reshape.573
  128.2 16.8 %all_to_all.5 = f32[128,1,128]{2,1,0:T(1,128)S(1)} all-to-all(f32[128,1,128]{2,1,0:T(1,128)S(1)} %reshape.573), channel_id=1, replica_groups=mesh['mass'=4,'x'=4,'z'=4,'core'=2] {'mass','x','z','core'}, dimensions={0} | all-to-all | bytes 131072 | tf_op jit(solution)/shard_map/all_to_all | solution.py:191
  145.0 0.5 broadcast.1066
  145.5 0.8 reduce
  146.5 0.2 copy.35
  146.8 0.2 copy.32
  147.0 0.3 reshape.481
  147.3 0.6 gather_fusion.1
  147.9 2.5 %sort_prefixfusion = f32[16,16]{1,0:T(8,128)} fusion(f32[16,512]{1,0:T(8,128)S(1)} %broadcast_select_fusion), kind=kCustom, calls=%top_k.9.sort_prefix | custom fusion | flops 106496 | bytes 33792 | tf_op jit(solution)/shard_map/top_k | solution.py:197
  (76 shorter events, 5.1 us)
Async XLA Ops:
  5.2 1.0 copy-start
  5.3 1.3 copy-start.2
  7.2 6.7 %collective-permute-start = (bf16[8,8192]{1,0:T(8,128)(2,1)S(1)}, bf16[8,8192]{1,0:T(8,128)(2,1)S(1)}, u32[]{:S(2)}, u32[]{:S(2)}) collective-permute-start(bf16[8,8192]{1,0:T(8,128)(2,1)S(1)} %get-tuple-element.26), channel_id=1, source_target_pairs={{0,32},{32,64},{64,96},{96,0},{1,33},{33,65},{65,97},{97,1},{2,34}... | collective-permute-start | bytes 393224 | tf_op jit(solution)/shard_map/ppermute | solution.py:150
  9.4 8.3 %collective-permute-start.9 = (bf16[8,8192]{1,0:T(8,128)(2,1)S(1)}, bf16[8,8192]{1,0:T(8,128)(2,1)S(1)}, u32[]{:S(2)}, u32[]{:S(2)}) collective-permute-start(bf16[8,8192]{1,0:T(8,128)(2,1)S(1)} %get-tuple-element.25), channel_id=1, source_target_pairs={{0,64},{32,96},{64,0},{96,32},{1,65},{33,97},{65,1},{97,33},{2,66}... | collective-permute-start | bytes 393224 | tf_op jit(solution)/shard_map/ppermute | solution.py:150
  12.0 5.7 %collective-permute-start.10 = (bf16[8,8192]{1,0:T(8,128)(2,1)S(1)}, bf16[8,8192]{1,0:T(8,128)(2,1)S(1)}, u32[]{:S(2)}, u32[]{:S(2)}) collective-permute-start(bf16[8,8192]{1,0:T(8,128)(2,1)S(1)} %get-tuple-element.24), channel_id=1, source_target_pairs={{0,96},{32,0},{64,32},{96,64},{1,97},{33,1},{65,33},{97,65},{2,98}... | collective-permute-start | bytes 393224 | tf_op jit(solution)/shard_map/ppermute | solution.py:150
  13.9 7.8 %collective-permute-start.2 = (bf16[16,8192]{1,0:T(8,128)(2,1)S(1)}, bf16[16,8192]{1,0:T(8,128)(2,1)S(1)}, u32[]{:S(2)}, u32[]{:S(2)}) collective-permute-start(bf16[16,8192]{1,0:T(8,128)(2,1)S(1)} %get-tuple-element.28), channel_id=1, source_target_pairs={{0,8},{8,16},{16,24},{24,0},{1,9},{9,17},{17,25},{25,1},{2,10},{10... | collective-permute-start | bytes 786440 | tf_op jit(solution)/shard_map/ppermute | solution.py:120
  15.1 7.9 %collective-permute-start.1 = (bf16[16,8192]{1,0:T(8,128)(2,1)S(1)}, bf16[16,8192]{1,0:T(8,128)(2,1)S(1)}, u32[]{:S(2)}, u32[]{:S(2)}) collective-permute-start(bf16[16,8192]{1,0:T(8,128)(2,1)S(1)} %get-tuple-element.28), channel_id=1, source_target_pairs={{0,24},{8,0},{16,8},{24,16},{1,25},{9,1},{17,9},{25,17},{2,26},{10... | collective-permute-start | bytes 786440 | tf_op jit(solution)/shard_map/ppermute | solution.py:121
  17.8 9.0 %collective-permute-start.12 = (bf16[16,8192]{1,0:T(8,128)(2,1)S(1)}, bf16[16,8192]{1,0:T(8,128)(2,1)S(1)}, u32[]{:S(2)}, u32[]{:S(2)}) collective-permute-start(bf16[16,8192]{1,0:T(8,128)(2,1)S(1)} %constant_dynamic-update-slice_fusion), channel_id=1, source_target_pairs={{0,2},{2,4},{4,6},{6,0},{1,3},{3,5},{5,7},{7,1},{8,10},{10,12},{12... | collective-permute-start | bytes 786440 | tf_op jit(solution)/shard_map/ppermute | solution.py:120
  19.5 7.4 %collective-permute-start.11 = (bf16[16,8192]{1,0:T(8,128)(2,1)S(1)}, bf16[16,8192]{1,0:T(8,128)(2,1)S(1)}, u32[]{:S(2)}, u32[]{:S(2)}) collective-permute-start(bf16[16,8192]{1,0:T(8,128)(2,1)S(1)} %constant_dynamic-update-slice_fusion), channel_id=1, source_target_pairs={{0,6},{2,0},{4,2},{6,4},{1,7},{3,1},{5,3},{7,5},{8,14},{10,8},{12,... | collective-permute-start | bytes 786440 | tf_op jit(solution)/shard_map/ppermute | solution.py:121
  21.7 7.8 %collective-permute-start.3 = (bf16[8,8192]{1,0:T(8,128)(2,1)S(1)}, bf16[8,8192]{1,0:T(8,128)(2,1)S(1)}, u32[]{:S(2)}, u32[]{:S(2)}) collective-permute-start(bf16[8,8192]{1,0:T(8,128)(2,1)S(1)} %slice.120), channel_id=1, source_target_pairs={{0,8},{8,16},{16,24},{24,0},{1,9},{9,17},{17,25},{25,1},{2,10},{10... | collective-permute-start | bytes 393224 | tf_op jit(solution)/shard_map/ppermute | solution.py:122
  23.0 6.6 %collective-permute-start.4 = (bf16[8,8192]{1,0:T(8,128)(2,1)S(1)}, bf16[8,8192]{1,0:T(8,128)(2,1)S(1)}, u32[]{:S(2)}, u32[]{:S(2)}) collective-permute-start(bf16[8,8192]{1,0:T(8,128)(2,1)S(1)} %slice.121), channel_id=1, source_target_pairs={{0,24},{8,0},{16,8},{24,16},{1,25},{9,1},{17,9},{25,17},{2,26},{10... | collective-permute-start | bytes 393224 | tf_op jit(solution)/shard_map/ppermute | solution.py:123
  26.7 5.8 %collective-permute-start.13 = (bf16[8,8192]{1,0:T(8,128)(2,1)S(1)}, bf16[8,8192]{1,0:T(8,128)(2,1)S(1)}, u32[]{:S(2)}, u32[]{:S(2)}) collective-permute-start(bf16[8,8192]{1,0:T(8,128)(2,1)S(1)} %slice.124), channel_id=1, source_target_pairs={{0,2},{2,4},{4,6},{6,0},{1,3},{3,5},{5,7},{7,1},{8,10},{10,12},{12... | collective-permute-start | bytes 393224 | tf_op jit(solution)/shard_map/ppermute | solution.py:122
  26.8 5.6 %collective-permute-start.14 = (bf16[8,8192]{1,0:T(8,128)(2,1)S(1)}, bf16[8,8192]{1,0:T(8,128)(2,1)S(1)}, u32[]{:S(2)}, u32[]{:S(2)}) collective-permute-start(bf16[8,8192]{1,0:T(8,128)(2,1)S(1)} %slice.125), channel_id=1, source_target_pairs={{0,6},{2,0},{4,2},{6,4},{1,7},{3,1},{5,3},{7,5},{8,14},{10,8},{12,... | collective-permute-start | bytes 393224 | tf_op jit(solution)/shard_map/ppermute | solution.py:123
  29.7 25.3 %collective-permute-start.6 = (bf16[64,8192]{1,0:T(8,128)(2,1)S(1)}, bf16[64,8192]{1,0:T(8,128)(2,1)S(1)}, u32[]{:S(2)}, u32[]{:S(2)}) collective-permute-start(bf16[64,8192]{1,0:T(8,128)(2,1)S(1)} %bitcast.65), channel_id=1, source_target_pairs={{0,2},{2,4},{4,6},{6,0},{1,3},{3,5},{5,7},{7,1},{8,10},{10,12},{12... | collective-permute-start | bytes 3145736 | tf_op jit(solution)/shard_map/ppermute | solution.py:120
  29.8 25.3 %collective-permute-start.5 = (bf16[64,8192]{1,0:T(8,128)(2,1)S(1)}, bf16[64,8192]{1,0:T(8,128)(2,1)S(1)}, u32[]{:S(2)}, u32[]{:S(2)}) collective-permute-start(bf16[64,8192]{1,0:T(8,128)(2,1)S(1)} %bitcast.66), channel_id=1, source_target_pairs={{0,6},{2,0},{4,2},{6,4},{1,7},{3,1},{5,3},{7,5},{8,14},{10,8},{12,... | collective-permute-start | bytes 3145736 | tf_op jit(solution)/shard_map/ppermute | solution.py:121
  32.7 25.6 %collective-permute-start.16 = (bf16[64,8192]{1,0:T(8,128)(2,1)S(1)}, bf16[64,8192]{1,0:T(8,128)(2,1)S(1)}, u32[]{:S(2)}, u32[]{:S(2)}) collective-permute-start(bf16[64,8192]{1,0:T(8,128)(2,1)S(1)} %bitcast.68), channel_id=1, source_target_pairs={{0,8},{8,16},{16,24},{24,0},{1,9},{9,17},{17,25},{25,1},{2,10},{10... | collective-permute-start | bytes 3145736 | tf_op jit(solution)/shard_map/ppermute | solution.py:120
  33.9 25.6 %collective-permute-start.15 = (bf16[64,8192]{1,0:T(8,128)(2,1)S(1)}, bf16[64,8192]{1,0:T(8,128)(2,1)S(1)}, u32[]{:S(2)}, u32[]{:S(2)}) collective-permute-start(bf16[64,8192]{1,0:T(8,128)(2,1)S(1)} %bitcast.69), channel_id=1, source_target_pairs={{0,24},{8,0},{16,8},{24,16},{1,25},{9,1},{17,9},{25,17},{2,26},{10... | collective-permute-start | bytes 3145736 | tf_op jit(solution)/shard_map/ppermute | solution.py:121
  55.0 12.2 %collective-permute-start.7 = (bf16[32,8192]{1,0:T(8,128)(2,1)S(1)}, bf16[32,8192]{1,0:T(8,128)(2,1)S(1)}, u32[]{:S(2)}, u32[]{:S(2)}) collective-permute-start(bf16[32,8192]{1,0:T(8,128)(2,1)S(1)} %slice.122), channel_id=1, source_target_pairs={{0,2},{2,4},{4,6},{6,0},{1,3},{3,5},{5,7},{7,1},{8,10},{10,12},{12... | collective-permute-start | bytes 1572872 | tf_op jit(solution)/shard_map/ppermute | solution.py:122
  55.2 12.1 %collective-permute-start.8 = (bf16[32,8192]{1,0:T(8,128)(2,1)S(1)}, bf16[32,8192]{1,0:T(8,128)(2,1)S(1)}, u32[]{:S(2)}, u32[]{:S(2)}) collective-permute-start(bf16[32,8192]{1,0:T(8,128)(2,1)S(1)} %slice.123), channel_id=1, source_target_pairs={{0,6},{2,0},{4,2},{6,4},{1,7},{3,1},{5,3},{7,5},{8,14},{10,8},{12,... | collective-permute-start | bytes 1572872 | tf_op jit(solution)/shard_map/ppermute | solution.py:123
  58.3 12.0 %collective-permute-start.17 = (bf16[32,8192]{1,0:T(8,128)(2,1)S(1)}, bf16[32,8192]{1,0:T(8,128)(2,1)S(1)}, u32[]{:S(2)}, u32[]{:S(2)}) collective-permute-start(bf16[32,8192]{1,0:T(8,128)(2,1)S(1)} %slice.126), channel_id=1, source_target_pairs={{0,8},{8,16},{16,24},{24,0},{1,9},{9,17},{17,25},{25,1},{2,10},{10... | collective-permute-start | bytes 1572872 | tf_op jit(solution)/shard_map/ppermute | solution.py:122
  59.6 10.7 %collective-permute-start.18 = (bf16[32,8192]{1,0:T(8,128)(2,1)S(1)}, bf16[32,8192]{1,0:T(8,128)(2,1)S(1)}, u32[]{:S(2)}, u32[]{:S(2)}) collective-permute-start(bf16[32,8192]{1,0:T(8,128)(2,1)S(1)} %slice.127), channel_id=1, source_target_pairs={{0,24},{8,0},{16,8},{24,16},{1,25},{9,1},{17,9},{25,17},{2,26},{10... | collective-permute-start | bytes 1572872 | tf_op jit(solution)/shard_map/ppermute | solution.py:123
  80.3 24.0 %collective-permute-start.19 = (bf16[512,8192]{1,0:T(8,128)(2,1)}, bf16[512,8192]{1,0:T(8,128)(2,1)}, u32[]{:S(2)}, u32[]{:S(2)}) collective-permute-start(bf16[512,8192]{1,0:T(8,128)(2,1)} %pad_maximum_fusion), channel_id=1, source_target_pairs={{0,1},{1,0},{2,3},{3,2},{4,5},{5,4},{6,7},{7,6},{8,9},{9,8},{10,11... | collective-permute-start | bytes 25165832 | tf_op jit(solution)/shard_map/ppermute | solution.py:164
  104.2 19.7 %copy-start.1 = (f32[16,512]{1,0:T(8,128)S(1)}, f32[16,512]{1,0:T(8,128)}, u32[]{:S(2)}) copy-start(f32[16,512]{1,0:T(8,128)} %shard_map.46) | copy-start | bytes 98308

commit v9 on v8

--- a/solution.py
+++ b/solution.py
@@ -20,14 +20,21 @@
     margin = jnp.zeros((row_count, MAX_SHIFT), queries.dtype)
     current = jnp.concatenate([margin, queries, margin], axis=1)
     window_start = MAX_SHIFT - offsets
-    bit_total = (2 * MAX_SHIFT).bit_length()
-    for bit_number in range(bit_total):
-        step_size = 1 << bit_number
-        moved = jnp.concatenate(
-            [current[:, step_size:], jnp.zeros((row_count, step_size), current.dtype)], axis=1
-        )
-        taken = window_start >> bit_number & 1 == 1
-        current = jnp.where(taken[:, None], moved, current)
+    position = 0
+    while (1 << position) <= 2 * MAX_SHIFT:
+        step_size = 1 << position
+        digit = window_start >> position & 3
+        result = current
+        for multiple in (1, 2, 3):
+            amount = multiple * step_size
+            if amount > 2 * MAX_SHIFT:
+                break
+            moved = jnp.concatenate(
+                [current[:, amount:], jnp.zeros((row_count, amount), current.dtype)], axis=1
+            )
+            result = jnp.where((digit == multiple)[:, None], moved, result)
+        current = result
+        position += 2
     shifted = current[:, :bin_count]
     combined = queries.astype(jnp.float32) + shifted.astype(jnp.float32)
     scale_factor = lax.rsqrt(jnp.mean(combined * combined, axis=1, keepdims=True) + 1e-06)

time: 151 us -> 151 us (level)
  no operation moved by 1% of the time
where the time goes in v9:
time: 151 us
  starting transfers between devices  33.7 us (22%)
  matrix products  32 us (21%)
  waiting for transfers between devices  30.4 us (20%)
  other arithmetic  22 us (15%)
  blocking collectives  16.8 us (11%)
  Pallas kernels  7.86 us (5%)
  local copies, waits for them, and re-layouts  7.76 us (5%)
    ppermute x4, waiting for transfers between devices, ring_gather(): from_minus = lax.ppermute(flat, axis, forward)  21.8 us
    all_to_all x1, blocking collectives, per_device(): lax.all_to_all(outgoing, ('mass', 'x', 'z', 'core'), split_axis=0, concat...  16.8 us
    dot_general x1, matrix products, per_device(): lax.dot_general(library, own_side, (((1,), (1,)), ((), ())), preferred_el...  15.8 us
    dot_general x1, matrix products, per_device(): lax.dot_general(library, other_side, (((1,), (1,)), ((), ())), preferred_...  15.8 us
    ppermute x4, starting transfers between devices, ring_gather(): far_second = lax.ppermute(from_plus[half:], axis, backward)  9.08 us
    ppermute x4, starting transfers between devices, ring_gather(): from_plus = lax.ppermute(flat, axis, backward)  7.9 us
    pallas_call x2, Pallas kernels, column_topk(): pl.pallas_call(column_topk_kernel, out_shape=jax.ShapeDtypeStruct((TOP_K,...  7.86 us
    concatenate x1, other arithmetic, per_device(): jnp.concatenate([part_a.reshape(-1, arrived.shape[1]), part_b.reshape(-1,...  7.67 us
  transfers between devices with their start and end apart: 20, of which 7 were waited for; matrix products, arithmetic and copies ran while one was open for 13% of the time, Pallas kernels for 3%

profile of v9, /device:TPU:1, one launch (start us, length us, event | category | flops | bytes accessed | tf_op | source)
XLA Modules:
  0.0 150.9 jit_solution(13257541098232885658)
XLA Ops:
  0.0 1.0 pad_maximum_fusion.5
  1.5 0.7 and_compare_fusion
  2.2 1.2 select_select_fusion.5
  3.9 0.3 select_select_fusion.4
  4.7 0.3 select_select_fusion.3
  5.4 0.3 select_select_fusion.2
  5.8 0.3 select_select_fusion.1
  6.3 0.3 select_select_fusion
  6.6 0.4 multiply_reduce_fusion
  7.2 0.4 fusion
  7.7 2.2 %collective-permute-start = (bf16[8,8192]{1,0:T(8,128)(2,1)S(1)}, bf16[8,8192]{1,0:T(8,128)(2,1)S(1)}, u32[]{:S(2)}, u32[]{:S(2)}) collective-permute-start(bf16[8,8192]{1,0:T(8,128)(2,1)S(1)} %get-tuple-element.26), channel_id=1, source_target_pairs={{0,32},{32,64},{64,96},{96,0},{1,33},{33,65},{65,97},{97,1},{2,34}... | collective-permute-start | bytes 393224 | tf_op jit(solution)/shard_map/ppermute | solution.py:157
  9.8 2.6 %collective-permute-start.9 = (bf16[8,8192]{1,0:T(8,128)(2,1)S(1)}, bf16[8,8192]{1,0:T(8,128)(2,1)S(1)}, u32[]{:S(2)}, u32[]{:S(2)}) collective-permute-start(bf16[8,8192]{1,0:T(8,128)(2,1)S(1)} %get-tuple-element.25), channel_id=1, source_target_pairs={{0,64},{32,96},{64,0},{96,32},{1,65},{33,97},{65,1},{97,33},{2,66}... | collective-permute-start | bytes 393224 | tf_op jit(solution)/shard_map/ppermute | solution.py:157
  12.5 1.1 collective-permute-start.10
  13.5 0.8 collective-permute-done
  14.4 1.2 collective-permute-start.2
  15.6 1.6 %collective-permute-start.1 = (bf16[16,8192]{1,0:T(8,128)(2,1)S(1)}, bf16[16,8192]{1,0:T(8,128)(2,1)S(1)}, u32[]{:S(2)}, u32[]{:S(2)}) collective-permute-start(bf16[16,8192]{1,0:T(8,128)(2,1)S(1)} %get-tuple-element.28), channel_id=1, source_target_pairs={{0,24},{8,0},{16,8},{24,16},{1,25},{9,1},{17,9},{25,17},{2,26},{10... | collective-permute-start | bytes 786440 | tf_op jit(solution)/shard_map/ppermute | solution.py:128
  17.2 1.0 collective-permute-done.9
  18.2 1.7 %collective-permute-start.12 = (bf16[16,8192]{1,0:T(8,128)(2,1)S(1)}, bf16[16,8192]{1,0:T(8,128)(2,1)S(1)}, u32[]{:S(2)}, u32[]{:S(2)}) collective-permute-start(bf16[16,8192]{1,0:T(8,128)(2,1)S(1)} %constant_dynamic-update-slice_fusion), channel_id=1, source_target_pairs={{0,2},{2,4},{4,6},{6,0},{1,3},{3,5},{5,7},{7,1},{8,10},{10,12},{12... | collective-permute-start | bytes 786440 | tf_op jit(solution)/shard_map/ppermute | solution.py:127
  19.9 2.2 %collective-permute-start.11 = (bf16[16,8192]{1,0:T(8,128)(2,1)S(1)}, bf16[16,8192]{1,0:T(8,128)(2,1)S(1)}, u32[]{:S(2)}, u32[]{:S(2)}) collective-permute-start(bf16[16,8192]{1,0:T(8,128)(2,1)S(1)} %constant_dynamic-update-slice_fusion), channel_id=1, source_target_pairs={{0,6},{2,0},{4,2},{6,4},{1,7},{3,1},{5,3},{7,5},{8,14},{10,8},{12,... | collective-permute-start | bytes 786440 | tf_op jit(solution)/shard_map/ppermute | solution.py:128
  22.2 1.2 collective-permute-start.3
  23.5 1.6 %collective-permute-start.4 = (bf16[8,8192]{1,0:T(8,128)(2,1)S(1)}, bf16[8,8192]{1,0:T(8,128)(2,1)S(1)}, u32[]{:S(2)}, u32[]{:S(2)}) collective-permute-start(bf16[8,8192]{1,0:T(8,128)(2,1)S(1)} %slice.151), channel_id=1, source_target_pairs={{0,24},{8,0},{16,8},{24,16},{1,25},{9,1},{17,9},{25,17},{2,26},{10... | collective-permute-start | bytes 393224 | tf_op jit(solution)/shard_map/ppermute | solution.py:130
  25.1 2.1 %collective-permute-done.12 = bf16[16,8192]{1,0:T(8,128)(2,1)S(1)} collective-permute-done((bf16[16,8192]{1,0:T(8,128)(2,1)S(1)}, bf16[16,8192]{1,0:T(8,128)(2,1)S(1)}, u32[]{:S(2)}, u32[]{:S(2)}) %collective-permute-start.12) | collective-permute-done | bytes 262176 | tf_op jit(solution)/shard_map/ppermute | solution.py:127
  27.3 2.7 %collective-permute-start.14 = (bf16[8,8192]{1,0:T(8,128)(2,1)S(1)}, bf16[8,8192]{1,0:T(8,128)(2,1)S(1)}, u32[]{:S(2)}, u32[]{:S(2)}) collective-permute-start(bf16[8,8192]{1,0:T(8,128)(2,1)S(1)} %slice.155), channel_id=1, source_target_pairs={{0,6},{2,0},{4,2},{6,4},{1,7},{3,1},{5,3},{7,5},{8,14},{10,8},{12,... | collective-permute-start | bytes 393224 | tf_op jit(solution)/shard_map/ppermute | solution.py:130
  30.3 2.7 %collective-permute-start.5 = (bf16[64,8192]{1,0:T(8,128)(2,1)S(1)}, bf16[64,8192]{1,0:T(8,128)(2,1)S(1)}, u32[]{:S(2)}, u32[]{:S(2)}) collective-permute-start(bf16[64,8192]{1,0:T(8,128)(2,1)S(1)} %bitcast.66), channel_id=1, source_target_pairs={{0,6},{2,0},{4,2},{6,4},{1,7},{3,1},{5,3},{7,5},{8,14},{10,8},{12,... | collective-permute-start | bytes 3145736 | tf_op jit(solution)/shard_map/ppermute | solution.py:128
  33.1 1.3 collective-permute-start.16
  34.4 1.5 collective-permute-start.15
  35.9 19.6 %collective-permute-done.6 = bf16[64,8192]{1,0:T(8,128)(2,1)S(1)} collective-permute-done((bf16[64,8192]{1,0:T(8,128)(2,1)S(1)}, bf16[64,8192]{1,0:T(8,128)(2,1)S(1)}, u32[]{:S(2)}, u32[]{:S(2)}) %collective-permute-start.6) | collective-permute-done | bytes 1048608 | tf_op jit(solution)/shard_map/ppermute | solution.py:127
  55.7 3.1 %collective-permute-start.8 = (bf16[32,8192]{1,0:T(8,128)(2,1)S(1)}, bf16[32,8192]{1,0:T(8,128)(2,1)S(1)}, u32[]{:S(2)}, u32[]{:S(2)}) collective-permute-start(bf16[32,8192]{1,0:T(8,128)(2,1)S(1)} %slice.153), channel_id=1, source_target_pairs={{0,6},{2,0},{4,2},{6,4},{1,7},{3,1},{5,3},{7,5},{8,14},{10,8},{12,... | collective-permute-start | bytes 1572872 | tf_op jit(solution)/shard_map/ppermute | solution.py:130
  58.8 1.3 collective-permute-start.17
  60.1 1.7 %collective-permute-start.18 = (bf16[32,8192]{1,0:T(8,128)(2,1)S(1)}, bf16[32,8192]{1,0:T(8,128)(2,1)S(1)}, u32[]{:S(2)}, u32[]{:S(2)}) collective-permute-start(bf16[32,8192]{1,0:T(8,128)(2,1)S(1)} %slice.157), channel_id=1, source_target_pairs={{0,24},{8,0},{16,8},{24,16},{1,25},{9,1},{17,9},{25,17},{2,26},{10... | collective-permute-start | bytes 1572872 | tf_op jit(solution)/shard_map/ppermute | solution.py:130
  61.8 5.9 %collective-permute-done.7 = bf16[32,8192]{1,0:T(8,128)(2,1)S(1)} collective-permute-done((bf16[32,8192]{1,0:T(8,128)(2,1)S(1)}, bf16[32,8192]{1,0:T(8,128)(2,1)S(1)}, u32[]{:S(2)}, u32[]{:S(2)}) %collective-permute-start.7) | collective-permute-done | bytes 524320 | tf_op jit(solution)/shard_map/ppermute | solution.py:129
  67.8 2.3 %pad_maximum_fusion.1 = bf16[4,64,8192]{2,1,0:T(8,128)(2,1)} fusion(bf16[1,64,8192]{2,1,0:T(8,128)(2,1)S(1)} %bitcast.71, bf16[1,64,8192]{2,1,0:T(8,128)(2,1)S(1)} %maximum_bitcast_fusion, bf16[1,64,8192]{2,1,0:T(8,128)(2,1)S(1)} %bitcast.72, bf16[1,64,8192]{2,1,0:T(8,128)(2,1)S(1)} %bitcast.67), kind=kLoop, calls=%fused_computation.5 | loop fusion | flops 6291456 | bytes 8388608 | tf_op jit(solution)/shard_map/stack | solution.py:132
  70.1 0.7 collective-permute-done.17
  70.8 2.2 %pad_maximum_fusion.2 = bf16[4,64,8192]{2,1,0:T(8,128)(2,1)} fusion(bf16[1,64,8192]{2,1,0:T(8,128)(2,1)S(1)} %bitcast.73, bf16[1,64,8192]{2,1,0:T(8,128)(2,1)S(1)} %maximum_bitcast_fusion.1, bf16[1,64,8192]{2,1,0:T(8,128)(2,1)S(1)} %bitcast.74, bf16[1,64,8192]{2,1,0:T(8,128)(2,1)S(1)} %bitcast.70), kind=kLoop, calls=%fused_computation.6 | loop fusion | flops 6291456 | bytes 8388608 | tf_op jit(solution)/shard_map/stack | solution.py:132
  73.1 7.7 %pad_maximum_fusion = bf16[512,8192]{1,0:T(8,128)(2,1)} fusion(bf16[256,8192]{1,0:T(8,128)(2,1)} %bitcast.63, bf16[256,8192]{1,0:T(8,128)(2,1)} %bitcast.61), kind=kLoop, calls=%fused_computation.4 | loop fusion | flops 16777216 | bytes 16777216 | tf_op jit(solution)/shard_map/concatenate | solution.py:167
  80.8 3.9 %collective-permute-start.19 = (bf16[512,8192]{1,0:T(8,128)(2,1)}, bf16[512,8192]{1,0:T(8,128)(2,1)}, u32[]{:S(2)}, u32[]{:S(2)}) collective-permute-start(bf16[512,8192]{1,0:T(8,128)(2,1)} %pad_maximum_fusion), channel_id=1, source_target_pairs={{0,1},{1,0},{2,3},{3,2},{4,5},{5,4},{6,7},{7,6},{8,9},{9,8},{10,11... | collective-permute-start | bytes 25165832 | tf_op jit(solution)/shard_map/ppermute | solution.py:171
  85.0 15.8 %convolution_bitcast_fusion.1.scores_ref = f32[1024,512]{1,0:T(8,128)} fusion(bf16[1024,8192]{1,0:T(8,128)(2,1)} %param.7, bf16[256,8192]{1,0:T(8,128)(2,1)} %bitcast.64, bf16[256,8192]{1,0:T(8,128)(2,1)} %bitcast.62), kind=kOutput, calls=%fused_computation.8 | convolution fusion | flops 8606711808 | bytes 27262976 | tf_op jit(solution)/shard_map/dot_general | solution.py:173
  100.8 3.9 %shard_map.46 = f32[16,512]{1,0:T(8,128)} custom-call(f32[1024,512]{1,0:T(8,128)} %convolution_bitcast_fusion.1.scores_ref), custom_call_target="tpu_custom_call" | custom-call | flops 16777216 | bytes 2097152 | tf_op jit(solution)/shard_map/pallas_call | solution.py:109
  104.7 15.8 %convolution_bitcast_fusion.scores_ref = f32[1024,512]{1,0:T(8,128)} fusion(bf16[512,8192]{1,0:T(8,128)(2,1)} %collective-permute-done.19, bf16[1024,8192]{1,0:T(8,128)(2,1)} %param.7), kind=kOutput, calls=%fused_computation.7 | convolution fusion | flops 8589934592 | bytes 27262976 | tf_op jit(solution)/shard_map/dot_general | solution.py:178
  120.5 3.9 %shard_map.47 = f32[16,512]{1,0:T(8,128)} custom-call(f32[1024,512]{1,0:T(8,128)} %convolution_bitcast_fusion.scores_ref), custom_call_target="tpu_custom_call" | custom-call | flops 16777216 | bytes 2097152 | tf_op jit(solution)/shard_map/pallas_call | solution.py:109
  124.5 0.8 maximum_bitcast_fusion.4
  125.4 2.8 %gather_fusion = f32[1024,16]{1,0:T(8,128)S(1)} fusion(f32[1024,16]{1,0:T(8,128)S(1)} %copy.30, s32[1024]{0:T(1024)S(1)} %get-tuple-element.49), kind=kCustom, calls=%fused_computation | custom fusion | bytes 135168 | tf_op jit(solution)/shard_map/jit(_take)/gather | solution.py:197
  128.7 16.8 %all_to_all.5 = f32[128,1,128]{2,1,0:T(1,128)S(1)} all-to-all(f32[128,1,128]{2,1,0:T(1,128)S(1)} %reshape.579), channel_id=1, replica_groups=mesh['mass'=4,'x'=4,'z'=4,'core'=2] {'mass','x','z','core'}, dimensions={0} | all-to-all | bytes 131072 | tf_op jit(solution)/shard_map/all_to_all | solution.py:198
  145.5 0.5 broadcast.1154
  146.0 0.8 reduce
  147.5 0.3 reshape.487
  147.8 0.6 gather_fusion.1
  148.4 2.5 %sort_prefixfusion = f32[16,16]{1,0:T(8,128)} fusion(f32[16,512]{1,0:T(8,128)S(1)} %broadcast_select_fusion), kind=kCustom, calls=%top_k.9.sort_prefix | custom fusion | flops 106496 | bytes 33792 | tf_op jit(solution)/shard_map/top_k | solution.py:204
  (76 shorter events, 5.1 us)
Async XLA Ops:
  5.7 1.0 copy-start
  5.7 1.3 copy-start.2
  7.7 6.7 %collective-permute-start = (bf16[8,8192]{1,0:T(8,128)(2,1)S(1)}, bf16[8,8192]{1,0:T(8,128)(2,1)S(1)}, u32[]{:S(2)}, u32[]{:S(2)}) collective-permute-start(bf16[8,8192]{1,0:T(8,128)(2,1)S(1)} %get-tuple-element.26), channel_id=1, source_target_pairs={{0,32},{32,64},{64,96},{96,0},{1,33},{33,65},{65,97},{97,1},{2,34}... | collective-permute-start | bytes 393224 | tf_op jit(solution)/shard_map/ppermute | solution.py:157
  9.8 8.3 %collective-permute-start.9 = (bf16[8,8192]{1,0:T(8,128)(2,1)S(1)}, bf16[8,8192]{1,0:T(8,128)(2,1)S(1)}, u32[]{:S(2)}, u32[]{:S(2)}) collective-permute-start(bf16[8,8192]{1,0:T(8,128)(2,1)S(1)} %get-tuple-element.25), channel_id=1, source_target_pairs={{0,64},{32,96},{64,0},{96,32},{1,65},{33,97},{65,1},{97,33},{2,66}... | collective-permute-start | bytes 393224 | tf_op jit(solution)/shard_map/ppermute | solution.py:157
  12.5 5.7 %collective-permute-start.10 = (bf16[8,8192]{1,0:T(8,128)(2,1)S(1)}, bf16[8,8192]{1,0:T(8,128)(2,1)S(1)}, u32[]{:S(2)}, u32[]{:S(2)}) collective-permute-start(bf16[8,8192]{1,0:T(8,128)(2,1)S(1)} %get-tuple-element.24), channel_id=1, source_target_pairs={{0,96},{32,0},{64,32},{96,64},{1,97},{33,1},{65,33},{97,65},{2,98}... | collective-permute-start | bytes 393224 | tf_op jit(solution)/shard_map/ppermute | solution.py:157
  14.4 7.8 %collective-permute-start.2 = (bf16[16,8192]{1,0:T(8,128)(2,1)S(1)}, bf16[16,8192]{1,0:T(8,128)(2,1)S(1)}, u32[]{:S(2)}, u32[]{:S(2)}) collective-permute-start(bf16[16,8192]{1,0:T(8,128)(2,1)S(1)} %get-tuple-element.28), channel_id=1, source_target_pairs={{0,8},{8,16},{16,24},{24,0},{1,9},{9,17},{17,25},{25,1},{2,10},{10... | collective-permute-start | bytes 786440 | tf_op jit(solution)/shard_map/ppermute | solution.py:127
  15.6 7.9 %collective-permute-start.1 = (bf16[16,8192]{1,0:T(8,128)(2,1)S(1)}, bf16[16,8192]{1,0:T(8,128)(2,1)S(1)}, u32[]{:S(2)}, u32[]{:S(2)}) collective-permute-start(bf16[16,8192]{1,0:T(8,128)(2,1)S(1)} %get-tuple-element.28), channel_id=1, source_target_pairs={{0,24},{8,0},{16,8},{24,16},{1,25},{9,1},{17,9},{25,17},{2,26},{10... | collective-permute-start | bytes 786440 | tf_op jit(solution)/shard_map/ppermute | solution.py:128
  18.2 9.0 %collective-permute-start.12 = (bf16[16,8192]{1,0:T(8,128)(2,1)S(1)}, bf16[16,8192]{1,0:T(8,128)(2,1)S(1)}, u32[]{:S(2)}, u32[]{:S(2)}) collective-permute-start(bf16[16,8192]{1,0:T(8,128)(2,1)S(1)} %constant_dynamic-update-slice_fusion), channel_id=1, source_target_pairs={{0,2},{2,4},{4,6},{6,0},{1,3},{3,5},{5,7},{7,1},{8,10},{10,12},{12... | collective-permute-start | bytes 786440 | tf_op jit(solution)/shard_map/ppermute | solution.py:127
  19.9 7.4 %collective-permute-start.11 = (bf16[16,8192]{1,0:T(8,128)(2,1)S(1)}, bf16[16,8192]{1,0:T(8,128)(2,1)S(1)}, u32[]{:S(2)}, u32[]{:S(2)}) collective-permute-start(bf16[16,8192]{1,0:T(8,128)(2,1)S(1)} %constant_dynamic-update-slice_fusion), channel_id=1, source_target_pairs={{0,6},{2,0},{4,2},{6,4},{1,7},{3,1},{5,3},{7,5},{8,14},{10,8},{12,... | collective-permute-start | bytes 786440 | tf_op jit(solution)/shard_map/ppermute | solution.py:128
  22.2 7.8 %collective-permute-start.3 = (bf16[8,8192]{1,0:T(8,128)(2,1)S(1)}, bf16[8,8192]{1,0:T(8,128)(2,1)S(1)}, u32[]{:S(2)}, u32[]{:S(2)}) collective-permute-start(bf16[8,8192]{1,0:T(8,128)(2,1)S(1)} %slice.150), channel_id=1, source_target_pairs={{0,8},{8,16},{16,24},{24,0},{1,9},{9,17},{17,25},{25,1},{2,10},{10... | collective-permute-start | bytes 393224 | tf_op jit(solution)/shard_map/ppermute | solution.py:129
  23.5 6.6 %collective-permute-start.4 = (bf16[8,8192]{1,0:T(8,128)(2,1)S(1)}, bf16[8,8192]{1,0:T(8,128)(2,1)S(1)}, u32[]{:S(2)}, u32[]{:S(2)}) collective-permute-start(bf16[8,8192]{1,0:T(8,128)(2,1)S(1)} %slice.151), channel_id=1, source_target_pairs={{0,24},{8,0},{16,8},{24,16},{1,25},{9,1},{17,9},{25,17},{2,26},{10... | collective-permute-start | bytes 393224 | tf_op jit(solution)/shard_map/ppermute | solution.py:130
  27.2 5.8 %collective-permute-start.13 = (bf16[8,8192]{1,0:T(8,128)(2,1)S(1)}, bf16[8,8192]{1,0:T(8,128)(2,1)S(1)}, u32[]{:S(2)}, u32[]{:S(2)}) collective-permute-start(bf16[8,8192]{1,0:T(8,128)(2,1)S(1)} %slice.154), channel_id=1, source_target_pairs={{0,2},{2,4},{4,6},{6,0},{1,3},{3,5},{5,7},{7,1},{8,10},{10,12},{12... | collective-permute-start | bytes 393224 | tf_op jit(solution)/shard_map/ppermute | solution.py:129
  27.3 5.6 %collective-permute-start.14 = (bf16[8,8192]{1,0:T(8,128)(2,1)S(1)}, bf16[8,8192]{1,0:T(8,128)(2,1)S(1)}, u32[]{:S(2)}, u32[]{:S(2)}) collective-permute-start(bf16[8,8192]{1,0:T(8,128)(2,1)S(1)} %slice.155), channel_id=1, source_target_pairs={{0,6},{2,0},{4,2},{6,4},{1,7},{3,1},{5,3},{7,5},{8,14},{10,8},{12,... | collective-permute-start | bytes 393224 | tf_op jit(solution)/shard_map/ppermute | solution.py:130
  30.2 25.3 %collective-permute-start.6 = (bf16[64,8192]{1,0:T(8,128)(2,1)S(1)}, bf16[64,8192]{1,0:T(8,128)(2,1)S(1)}, u32[]{:S(2)}, u32[]{:S(2)}) collective-permute-start(bf16[64,8192]{1,0:T(8,128)(2,1)S(1)} %bitcast.65), channel_id=1, source_target_pairs={{0,2},{2,4},{4,6},{6,0},{1,3},{3,5},{5,7},{7,1},{8,10},{10,12},{12... | collective-permute-start | bytes 3145736 | tf_op jit(solution)/shard_map/ppermute | solution.py:127
  30.3 25.3 %collective-permute-start.5 = (bf16[64,8192]{1,0:T(8,128)(2,1)S(1)}, bf16[64,8192]{1,0:T(8,128)(2,1)S(1)}, u32[]{:S(2)}, u32[]{:S(2)}) collective-permute-start(bf16[64,8192]{1,0:T(8,128)(2,1)S(1)} %bitcast.66), channel_id=1, source_target_pairs={{0,6},{2,0},{4,2},{6,4},{1,7},{3,1},{5,3},{7,5},{8,14},{10,8},{12,... | collective-permute-start | bytes 3145736 | tf_op jit(solution)/shard_map/ppermute | solution.py:128
  33.1 25.6 %collective-permute-start.16 = (bf16[64,8192]{1,0:T(8,128)(2,1)S(1)}, bf16[64,8192]{1,0:T(8,128)(2,1)S(1)}, u32[]{:S(2)}, u32[]{:S(2)}) collective-permute-start(bf16[64,8192]{1,0:T(8,128)(2,1)S(1)} %bitcast.68), channel_id=1, source_target_pairs={{0,8},{8,16},{16,24},{24,0},{1,9},{9,17},{17,25},{25,1},{2,10},{10... | collective-permute-start | bytes 3145736 | tf_op jit(solution)/shard_map/ppermute | solution.py:127
  34.4 25.6 %collective-permute-start.15 = (bf16[64,8192]{1,0:T(8,128)(2,1)S(1)}, bf16[64,8192]{1,0:T(8,128)(2,1)S(1)}, u32[]{:S(2)}, u32[]{:S(2)}) collective-permute-start(bf16[64,8192]{1,0:T(8,128)(2,1)S(1)} %bitcast.69), channel_id=1, source_target_pairs={{0,24},{8,0},{16,8},{24,16},{1,25},{9,1},{17,9},{25,17},{2,26},{10... | collective-permute-start | bytes 3145736 | tf_op jit(solution)/shard_map/ppermute | solution.py:128
  55.5 12.2 %collective-permute-start.7 = (bf16[32,8192]{1,0:T(8,128)(2,1)S(1)}, bf16[32,8192]{1,0:T(8,128)(2,1)S(1)}, u32[]{:S(2)}, u32[]{:S(2)}) collective-permute-start(bf16[32,8192]{1,0:T(8,128)(2,1)S(1)} %slice.152), channel_id=1, source_target_pairs={{0,2},{2,4},{4,6},{6,0},{1,3},{3,5},{5,7},{7,1},{8,10},{10,12},{12... | collective-permute-start | bytes 1572872 | tf_op jit(solution)/shard_map/ppermute | solution.py:129
  55.7 12.1 %collective-permute-start.8 = (bf16[32,8192]{1,0:T(8,128)(2,1)S(1)}, bf16[32,8192]{1,0:T(8,128)(2,1)S(1)}, u32[]{:S(2)}, u32[]{:S(2)}) collective-permute-start(bf16[32,8192]{1,0:T(8,128)(2,1)S(1)} %slice.153), channel_id=1, source_target_pairs={{0,6},{2,0},{4,2},{6,4},{1,7},{3,1},{5,3},{7,5},{8,14},{10,8},{12,... | collective-permute-start | bytes 1572872 | tf_op jit(solution)/shard_map/ppermute | solution.py:130
  58.8 12.0 %collective-permute-start.17 = (bf16[32,8192]{1,0:T(8,128)(2,1)S(1)}, bf16[32,8192]{1,0:T(8,128)(2,1)S(1)}, u32[]{:S(2)}, u32[]{:S(2)}) collective-permute-start(bf16[32,8192]{1,0:T(8,128)(2,1)S(1)} %slice.156), channel_id=1, source_target_pairs={{0,8},{8,16},{16,24},{24,0},{1,9},{9,17},{17,25},{25,1},{2,10},{10... | collective-permute-start | bytes 1572872 | tf_op jit(solution)/shard_map/ppermute | solution.py:129
  60.1 10.7 %collective-permute-start.18 = (bf16[32,8192]{1,0:T(8,128)(2,1)S(1)}, bf16[32,8192]{1,0:T(8,128)(2,1)S(1)}, u32[]{:S(2)}, u32[]{:S(2)}) collective-permute-start(bf16[32,8192]{1,0:T(8,128)(2,1)S(1)} %slice.157), channel_id=1, source_target_pairs={{0,24},{8,0},{16,8},{24,16},{1,25},{9,1},{17,9},{25,17},{2,26},{10... | collective-permute-start | bytes 1572872 | tf_op jit(solution)/shard_map/ppermute | solution.py:130
  80.8 24.0 %collective-permute-start.19 = (bf16[512,8192]{1,0:T(8,128)(2,1)}, bf16[512,8192]{1,0:T(8,128)(2,1)}, u32[]{:S(2)}, u32[]{:S(2)}) collective-permute-start(bf16[512,8192]{1,0:T(8,128)(2,1)} %pad_maximum_fusion), channel_id=1, source_target_pairs={{0,1},{1,0},{2,3},{3,2},{4,5},{5,4},{6,7},{7,6},{8,9},{9,8},{10,11... | collective-permute-start | bytes 25165832 | tf_op jit(solution)/shard_map/ppermute | solution.py:171
  104.7 19.7 %copy-start.1 = (f32[16,512]{1,0:T(8,128)S(1)}, f32[16,512]{1,0:T(8,128)}, u32[]{:S(2)}) copy-start(f32[16,512]{1,0:T(8,128)} %shard_map.46) | copy-start | bytes 98308

commit v10 on v8

--- a/solution.py
+++ b/solution.py
@@ -80,35 +80,46 @@
     group = SUBLANES * TOP_K
     steps = scores_ref.shape[0] // group
     lowest = jnp.full((SUBLANES, LANES), -jnp.inf, jnp.float32)
-
-    def insert(step, kept):
-        start = pl.multiple_of(step * group, group)
-        values = [scores_ref[pl.ds(start + SUBLANES * k, SUBLANES), :] for k in range(TOP_K)]
-        return tuple(merge_sorted(list(kept), bitonic_sort(values)))
-
-    kept = lax.fori_loop(0, steps, insert, (lowest,) * TOP_K, unroll=2)
-    kept = list(kept)
-    shift = SUBLANES // 2
-    while shift >= 1:
-        rolled = [pltpu.roll(kept[k], shift, 0) for k in range(TOP_K)]
-        kept = merge_sorted(kept, rolled)
-        shift //= 2
-    for k in range(TOP_K):
-        out_ref[pl.ds(k, 1), :] = kept[k][0:1, :]
+    for column in range(0, scores_ref.shape[1], LANES):
+        lanes = pl.ds(column, LANES)
+
+        def insert(step, kept):
+            start = pl.multiple_of(step * group, group)
+            values = [
+                scores_ref[pl.ds(start + SUBLANES * k, SUBLANES), lanes] for k in range(TOP_K)
+            ]
+            return tuple(merge_sorted(list(kept), bitonic_sort(values)))
+
+        kept = lax.fori_loop(0, steps, insert, (lowest,) * TOP_K, unroll=2)
+        kept = list(kept)
+        shift = SUBLANES // 2
+        while shift >= 1:
+            rolled = [pltpu.roll(kept[k], shift, 0) for k in range(TOP_K)]
+            kept = merge_sorted(kept, rolled)
+            shift //= 2
+        for k in range(TOP_K):
+            out_ref[pl.ds(k, 1), lanes] = kept[k][0:1, :]
 
 
 def column_topk(scores):
     rows, columns = scores.shape
+    width = 2 * LANES if columns % (2 * LANES) == 0 else LANES
     return pl.pallas_call(
         column_topk_kernel,
         out_shape=jax.ShapeDtypeStruct((TOP_K, columns), jnp.float32),
-        grid=(columns // LANES,),
-        in_specs=[pl.BlockSpec((rows, LANES), lambda j: (0, j))],
-        out_specs=pl.BlockSpec((TOP_K, LANES), lambda j: (0, j)),
+        grid=(columns // width,),
+        in_specs=[pl.BlockSpec((rows, width), lambda j: (0, j))],
+        out_specs=pl.BlockSpec((TOP_K, width), lambda j: (0, j)),
         cost_estimate=pl.CostEstimate(
             flops=2 * TOP_K * rows * columns, transcendentals=0, bytes_accessed=4 * rows * columns
         ),
     )(scores)
+
+
+def row_topk(values):
+    count = values.shape[0]
+    padded = jnp.pad(values.T, ((0, 0), (0, LANES - count)), constant_values=-jnp.inf)
+    return column_topk(padded)[:, :count].T
 
 
 def ring_gather(block, axis):
@@ -194,7 +205,7 @@
     received = received.reshape(mass_count, shard_count, capacity, TOP_K)
     received = received.transpose(0, 2, 1, 3).reshape(mass_count * capacity, -1)
     candidates = jnp.take(received, slot_index, axis=0)
-    return lax.top_k(candidates, TOP_K)[0]
+    return row_topk(candidates)
 
 
 def solution(mesh):

time: 151 us -> 151 us (level)
  other arithmetic: 22.3 us -> 19.8 us
  local copies, waits for them, and re-layouts: 7.05 us -> 9.26 us
    top_k x1 -> x0, other arithmetic: 2.52 us -> none  [per_device(): return lax.top_k(candidates, TOP_K)[0]]
    pallas_call x2 -> x3, Pallas kernels: 7.86 us -> 8.24 us  [column_topk(): pl.pallas_call(column_topk_kernel, out_shape=jax.ShapeDtypeStruct((TOP_K,...]
  transfers between devices with their start and end apart: 20 -> 20, of which waited for: 7 -> 7; matrix products, arithmetic and copies ran while one was open for 13% -> 13% of each run, Pallas kernels for 3% -> 2%
where the time goes in v10:
time: 151 us
  starting transfers between devices  33.7 us (22%)
  matrix products  32 us (21%)
  waiting for transfers between devices  30.4 us (20%)
  other arithmetic  19.8 us (13%)
  blocking collectives  16.8 us (11%)
  local copies, waits for them, and re-layouts  9.26 us (6%)
  Pallas kernels  8.24 us (5%)
    ppermute x4, waiting for transfers between devices, ring_gather(): from_minus = lax.ppermute(flat, axis, forward)  21.8 us
    all_to_all x1, blocking collectives, per_device(): lax.all_to_all(outgoing, ('mass', 'x', 'z', 'core'), split_axis=0, concat...  16.8 us
    dot_general x1, matrix products, per_device(): lax.dot_general(library, own_side, (((1,), (1,)), ((), ())), preferred_el...  15.8 us
    dot_general x1, matrix products, per_device(): lax.dot_general(library, other_side, (((1,), (1,)), ((), ())), preferred_...  15.8 us
    ppermute x4, starting transfers between devices, ring_gather(): far_second = lax.ppermute(from_plus[half:], axis, backward)  9.09 us
    pallas_call x3, Pallas kernels, column_topk(): pl.pallas_call(column_topk_kernel, out_shape=jax.ShapeDtypeStruct((TOP_K,...  8.24 us
    ppermute x4, starting transfers between devices, ring_gather(): from_plus = lax.ppermute(flat, axis, backward)  7.9 us
    concatenate x1, other arithmetic, per_device(): jnp.concatenate([part_a.reshape(-1, arrived.shape[1]), part_b.reshape(-1,...  7.7 us
  transfers between devices with their start and end apart: 20, of which 7 were waited for; matrix products, arithmetic and copies ran while one was open for 13% of the time, Pallas kernels for 2%

profile of v10, /device:TPU:1, one launch (start us, length us, event | category | flops | bytes accessed | tf_op | source)
XLA Modules:
  0.0 150.6 jit_solution(5600265417758305903)
XLA Ops:
  0.0 0.7 and_compare_fusion.12
  0.7 1.0 pad_maximum_fusion.5
  1.8 1.1 pad_select_fusion.11
  6.2 0.4 multiply_reduce_fusion
  6.7 0.4 fusion
  7.2 2.2 %collective-permute-start = (bf16[8,8192]{1,0:T(8,128)(2,1)S(1)}, bf16[8,8192]{1,0:T(8,128)(2,1)S(1)}, u32[]{:S(2)}, u32[]{:S(2)}) collective-permute-start(bf16[8,8192]{1,0:T(8,128)(2,1)S(1)} %get-tuple-element.22), channel_id=1, source_target_pairs={{0,32},{32,64},{64,96},{96,0},{1,33},{33,65},{65,97},{97,1},{2,34}... | collective-permute-start | bytes 393224 | tf_op jit(solution)/shard_map/ppermute | solution.py:161
  9.4 2.6 %collective-permute-start.9 = (bf16[8,8192]{1,0:T(8,128)(2,1)S(1)}, bf16[8,8192]{1,0:T(8,128)(2,1)S(1)}, u32[]{:S(2)}, u32[]{:S(2)}) collective-permute-start(bf16[8,8192]{1,0:T(8,128)(2,1)S(1)} %get-tuple-element.21), channel_id=1, source_target_pairs={{0,64},{32,96},{64,0},{96,32},{1,65},{33,97},{65,1},{97,33},{2,66}... | collective-permute-start | bytes 393224 | tf_op jit(solution)/shard_map/ppermute | solution.py:161
  12.0 1.1 collective-permute-start.10
  13.1 0.8 collective-permute-done
  13.9 1.2 collective-permute-start.2
  15.1 1.6 %collective-permute-start.1 = (bf16[16,8192]{1,0:T(8,128)(2,1)S(1)}, bf16[16,8192]{1,0:T(8,128)(2,1)S(1)}, u32[]{:S(2)}, u32[]{:S(2)}) collective-permute-start(bf16[16,8192]{1,0:T(8,128)(2,1)S(1)} %get-tuple-element.24), channel_id=1, source_target_pairs={{0,24},{8,0},{16,8},{24,16},{1,25},{9,1},{17,9},{25,17},{2,26},{10... | collective-permute-start | bytes 786440 | tf_op jit(solution)/shard_map/ppermute | solution.py:132
  16.7 1.0 collective-permute-done.9
  17.8 1.7 %collective-permute-start.12 = (bf16[16,8192]{1,0:T(8,128)(2,1)S(1)}, bf16[16,8192]{1,0:T(8,128)(2,1)S(1)}, u32[]{:S(2)}, u32[]{:S(2)}) collective-permute-start(bf16[16,8192]{1,0:T(8,128)(2,1)S(1)} %constant_dynamic-update-slice_fusion), channel_id=1, source_target_pairs={{0,2},{2,4},{4,6},{6,0},{1,3},{3,5},{5,7},{7,1},{8,10},{10,12},{12... | collective-permute-start | bytes 786440 | tf_op jit(solution)/shard_map/ppermute | solution.py:131
  19.5 2.2 %collective-permute-start.11 = (bf16[16,8192]{1,0:T(8,128)(2,1)S(1)}, bf16[16,8192]{1,0:T(8,128)(2,1)S(1)}, u32[]{:S(2)}, u32[]{:S(2)}) collective-permute-start(bf16[16,8192]{1,0:T(8,128)(2,1)S(1)} %constant_dynamic-update-slice_fusion), channel_id=1, source_target_pairs={{0,6},{2,0},{4,2},{6,4},{1,7},{3,1},{5,3},{7,5},{8,14},{10,8},{12,... | collective-permute-start | bytes 786440 | tf_op jit(solution)/shard_map/ppermute | solution.py:132
  21.7 1.2 collective-permute-start.3
  23.0 1.6 %collective-permute-start.4 = (bf16[8,8192]{1,0:T(8,128)(2,1)S(1)}, bf16[8,8192]{1,0:T(8,128)(2,1)S(1)}, u32[]{:S(2)}, u32[]{:S(2)}) collective-permute-start(bf16[8,8192]{1,0:T(8,128)(2,1)S(1)} %slice.124), channel_id=1, source_target_pairs={{0,24},{8,0},{16,8},{24,16},{1,25},{9,1},{17,9},{25,17},{2,26},{10... | collective-permute-start | bytes 393224 | tf_op jit(solution)/shard_map/ppermute | solution.py:134
  24.6 2.1 %collective-permute-done.12 = bf16[16,8192]{1,0:T(8,128)(2,1)S(1)} collective-permute-done((bf16[16,8192]{1,0:T(8,128)(2,1)S(1)}, bf16[16,8192]{1,0:T(8,128)(2,1)S(1)}, u32[]{:S(2)}, u32[]{:S(2)}) %collective-permute-start.12) | collective-permute-done | bytes 262176 | tf_op jit(solution)/shard_map/ppermute | solution.py:131
  26.8 2.7 %collective-permute-start.14 = (bf16[8,8192]{1,0:T(8,128)(2,1)S(1)}, bf16[8,8192]{1,0:T(8,128)(2,1)S(1)}, u32[]{:S(2)}, u32[]{:S(2)}) collective-permute-start(bf16[8,8192]{1,0:T(8,128)(2,1)S(1)} %slice.128), channel_id=1, source_target_pairs={{0,6},{2,0},{4,2},{6,4},{1,7},{3,1},{5,3},{7,5},{8,14},{10,8},{12,... | collective-permute-start | bytes 393224 | tf_op jit(solution)/shard_map/ppermute | solution.py:134
  29.8 2.7 %collective-permute-start.5 = (bf16[64,8192]{1,0:T(8,128)(2,1)S(1)}, bf16[64,8192]{1,0:T(8,128)(2,1)S(1)}, u32[]{:S(2)}, u32[]{:S(2)}) collective-permute-start(bf16[64,8192]{1,0:T(8,128)(2,1)S(1)} %bitcast.69), channel_id=1, source_target_pairs={{0,6},{2,0},{4,2},{6,4},{1,7},{3,1},{5,3},{7,5},{8,14},{10,8},{12,... | collective-permute-start | bytes 3145736 | tf_op jit(solution)/shard_map/ppermute | solution.py:132
  32.7 1.3 collective-permute-start.16
  33.9 1.5 collective-permute-start.15
  35.4 19.6 %collective-permute-done.6 = bf16[64,8192]{1,0:T(8,128)(2,1)S(1)} collective-permute-done((bf16[64,8192]{1,0:T(8,128)(2,1)S(1)}, bf16[64,8192]{1,0:T(8,128)(2,1)S(1)}, u32[]{:S(2)}, u32[]{:S(2)}) %collective-permute-start.6) | collective-permute-done | bytes 1048608 | tf_op jit(solution)/shard_map/ppermute | solution.py:131
  55.2 3.1 %collective-permute-start.8 = (bf16[32,8192]{1,0:T(8,128)(2,1)S(1)}, bf16[32,8192]{1,0:T(8,128)(2,1)S(1)}, u32[]{:S(2)}, u32[]{:S(2)}) collective-permute-start(bf16[32,8192]{1,0:T(8,128)(2,1)S(1)} %slice.126), channel_id=1, source_target_pairs={{0,6},{2,0},{4,2},{6,4},{1,7},{3,1},{5,3},{7,5},{8,14},{10,8},{12,... | collective-permute-start | bytes 1572872 | tf_op jit(solution)/shard_map/ppermute | solution.py:134
  58.3 1.3 collective-permute-start.17
  59.6 1.7 %collective-permute-start.18 = (bf16[32,8192]{1,0:T(8,128)(2,1)S(1)}, bf16[32,8192]{1,0:T(8,128)(2,1)S(1)}, u32[]{:S(2)}, u32[]{:S(2)}) collective-permute-start(bf16[32,8192]{1,0:T(8,128)(2,1)S(1)} %slice.130), channel_id=1, source_target_pairs={{0,24},{8,0},{16,8},{24,16},{1,25},{9,1},{17,9},{25,17},{2,26},{10... | collective-permute-start | bytes 1572872 | tf_op jit(solution)/shard_map/ppermute | solution.py:134
  61.3 5.9 %collective-permute-done.7 = bf16[32,8192]{1,0:T(8,128)(2,1)S(1)} collective-permute-done((bf16[32,8192]{1,0:T(8,128)(2,1)S(1)}, bf16[32,8192]{1,0:T(8,128)(2,1)S(1)}, u32[]{:S(2)}, u32[]{:S(2)}) %collective-permute-start.7) | collective-permute-done | bytes 524320 | tf_op jit(solution)/shard_map/ppermute | solution.py:133
  67.3 2.2 %pad_maximum_fusion.1 = bf16[4,64,8192]{2,1,0:T(8,128)(2,1)} fusion(bf16[1,64,8192]{2,1,0:T(8,128)(2,1)S(1)} %bitcast.74, bf16[1,64,8192]{2,1,0:T(8,128)(2,1)S(1)} %maximum_bitcast_fusion, bf16[1,64,8192]{2,1,0:T(8,128)(2,1)S(1)} %bitcast.75, bf16[1,64,8192]{2,1,0:T(8,128)(2,1)S(1)} %bitcast.70), kind=kLoop, calls=%fused_computation.5 | loop fusion | flops 6291456 | bytes 8388608 | tf_op jit(solution)/shard_map/stack | solution.py:136
  69.6 0.7 collective-permute-done.17
  70.4 2.2 %pad_maximum_fusion.2 = bf16[4,64,8192]{2,1,0:T(8,128)(2,1)} fusion(bf16[1,64,8192]{2,1,0:T(8,128)(2,1)S(1)} %bitcast.76, bf16[1,64,8192]{2,1,0:T(8,128)(2,1)S(1)} %maximum_bitcast_fusion.1, bf16[1,64,8192]{2,1,0:T(8,128)(2,1)S(1)} %bitcast.77, bf16[1,64,8192]{2,1,0:T(8,128)(2,1)S(1)} %bitcast.73), kind=kLoop, calls=%fused_computation.6 | loop fusion | flops 6291456 | bytes 8388608 | tf_op jit(solution)/shard_map/stack | solution.py:136
  72.6 7.7 %pad_maximum_fusion = bf16[512,8192]{1,0:T(8,128)(2,1)} fusion(bf16[256,8192]{1,0:T(8,128)(2,1)} %bitcast.66, bf16[256,8192]{1,0:T(8,128)(2,1)} %bitcast.64), kind=kLoop, calls=%fused_computation.4 | loop fusion | flops 16777216 | bytes 16777216 | tf_op jit(solution)/shard_map/concatenate | solution.py:171
  80.3 3.9 %collective-permute-start.19 = (bf16[512,8192]{1,0:T(8,128)(2,1)}, bf16[512,8192]{1,0:T(8,128)(2,1)}, u32[]{:S(2)}, u32[]{:S(2)}) collective-permute-start(bf16[512,8192]{1,0:T(8,128)(2,1)} %pad_maximum_fusion), channel_id=1, source_target_pairs={{0,1},{1,0},{2,3},{3,2},{4,5},{5,4},{6,7},{7,6},{8,9},{9,8},{10,11... | collective-permute-start | bytes 25165832 | tf_op jit(solution)/shard_map/ppermute | solution.py:175
  84.5 15.8 %convolution_bitcast_fusion.1.scores_ref = f32[1024,512]{1,0:T(8,128)} fusion(bf16[1024,8192]{1,0:T(8,128)(2,1)} %param.7, bf16[256,8192]{1,0:T(8,128)(2,1)} %bitcast.67, bf16[256,8192]{1,0:T(8,128)(2,1)} %bitcast.65), kind=kOutput, calls=%fused_computation.8 | convolution fusion | flops 8606711808 | bytes 27262976 | tf_op jit(solution)/shard_map/dot_general | solution.py:177
  100.3 3.3 %shard_map.46 = f32[16,512]{1,0:T(8,128)} custom-call(f32[1024,512]{1,0:T(8,128)} %convolution_bitcast_fusion.1.scores_ref), custom_call_target="tpu_custom_call" | custom-call | flops 16777216 | bytes 2097152 | tf_op jit(solution)/shard_map/pallas_call | solution.py:107
  103.6 15.8 %convolution_bitcast_fusion.scores_ref = f32[1024,512]{1,0:T(8,128)} fusion(bf16[512,8192]{1,0:T(8,128)(2,1)} %collective-permute-done.19, bf16[1024,8192]{1,0:T(8,128)(2,1)} %param.7), kind=kOutput, calls=%fused_computation.7 | convolution fusion | flops 8589934592 | bytes 27262976 | tf_op jit(solution)/shard_map/dot_general | solution.py:182
  119.4 3.3 %shard_map.47 = f32[16,512]{1,0:T(8,128)} custom-call(f32[1024,512]{1,0:T(8,128)} %convolution_bitcast_fusion.scores_ref), custom_call_target="tpu_custom_call" | custom-call | flops 16777216 | bytes 2097152 | tf_op jit(solution)/shard_map/pallas_call | solution.py:107
  122.7 0.8 maximum_bitcast_fusion.4
  123.6 2.8 %gather_fusion = f32[1024,16]{1,0:T(8,128)S(1)} fusion(f32[1024,16]{1,0:T(8,128)S(1)} %copy.50, s32[1024]{0:T(1024)S(1)} %get-tuple-element.39), kind=kCustom, calls=%fused_computation | custom fusion | bytes 135168 | tf_op jit(solution)/shard_map/jit(_take)/gather | solution.py:201
  126.9 16.8 %all_to_all.5 = f32[128,1,128]{2,1,0:T(1,128)S(1)} all-to-all(f32[128,1,128]{2,1,0:T(1,128)S(1)} %reshape.573), channel_id=1, replica_groups=mesh['mass'=4,'x'=4,'z'=4,'core'=2] {'mass','x','z','core'}, dimensions={0} | all-to-all | bytes 131072 | tf_op jit(solution)/shard_map/all_to_all | solution.py:202
  143.7 0.5 broadcast.1070
  144.2 0.8 reduce
  145.2 0.2 copy.57
  145.4 0.2 copy.52
  145.7 0.3 reshape.481
  146.0 0.6 gather_fusion.1
  146.7 0.7 pad.17.scores_ref
  147.5 1.7 %shard_map.48 = f32[16,128]{1,0:T(8,128)} custom-call(f32[512,128]{1,0:T(8,128)} %pad.17.scores_ref), custom_call_target="tpu_custom_call" | custom-call | flops 2097152 | bytes 262144 | tf_op jit(solution)/shard_map/pallas_call | solution.py:107
  149.2 0.7 slice_bitcast_fusion
  149.9 0.7 copy.54
  (80 shorter events, 5.8 us)
Async XLA Ops:
  5.2 1.0 copy-start
  5.3 1.3 copy-start.2
  7.2 6.7 %collective-permute-start = (bf16[8,8192]{1,0:T(8,128)(2,1)S(1)}, bf16[8,8192]{1,0:T(8,128)(2,1)S(1)}, u32[]{:S(2)}, u32[]{:S(2)}) collective-permute-start(bf16[8,8192]{1,0:T(8,128)(2,1)S(1)} %get-tuple-element.22), channel_id=1, source_target_pairs={{0,32},{32,64},{64,96},{96,0},{1,33},{33,65},{65,97},{97,1},{2,34}... | collective-permute-start | bytes 393224 | tf_op jit(solution)/shard_map/ppermute | solution.py:161
  9.4 8.3 %collective-permute-start.9 = (bf16[8,8192]{1,0:T(8,128)(2,1)S(1)}, bf16[8,8192]{1,0:T(8,128)(2,1)S(1)}, u32[]{:S(2)}, u32[]{:S(2)}) collective-permute-start(bf16[8,8192]{1,0:T(8,128)(2,1)S(1)} %get-tuple-element.21), channel_id=1, source_target_pairs={{0,64},{32,96},{64,0},{96,32},{1,65},{33,97},{65,1},{97,33},{2,66}... | collective-permute-start | bytes 393224 | tf_op jit(solution)/shard_map/ppermute | solution.py:161
  12.0 5.7 %collective-permute-start.10 = (bf16[8,8192]{1,0:T(8,128)(2,1)S(1)}, bf16[8,8192]{1,0:T(8,128)(2,1)S(1)}, u32[]{:S(2)}, u32[]{:S(2)}) collective-permute-start(bf16[8,8192]{1,0:T(8,128)(2,1)S(1)} %get-tuple-element.20), channel_id=1, source_target_pairs={{0,96},{32,0},{64,32},{96,64},{1,97},{33,1},{65,33},{97,65},{2,98}... | collective-permute-start | bytes 393224 | tf_op jit(solution)/shard_map/ppermute | solution.py:161
  13.9 7.8 %collective-permute-start.2 = (bf16[16,8192]{1,0:T(8,128)(2,1)S(1)}, bf16[16,8192]{1,0:T(8,128)(2,1)S(1)}, u32[]{:S(2)}, u32[]{:S(2)}) collective-permute-start(bf16[16,8192]{1,0:T(8,128)(2,1)S(1)} %get-tuple-element.24), channel_id=1, source_target_pairs={{0,8},{8,16},{16,24},{24,0},{1,9},{9,17},{17,25},{25,1},{2,10},{10... | collective-permute-start | bytes 786440 | tf_op jit(solution)/shard_map/ppermute | solution.py:131
  15.1 7.9 %collective-permute-start.1 = (bf16[16,8192]{1,0:T(8,128)(2,1)S(1)}, bf16[16,8192]{1,0:T(8,128)(2,1)S(1)}, u32[]{:S(2)}, u32[]{:S(2)}) collective-permute-start(bf16[16,8192]{1,0:T(8,128)(2,1)S(1)} %get-tuple-element.24), channel_id=1, source_target_pairs={{0,24},{8,0},{16,8},{24,16},{1,25},{9,1},{17,9},{25,17},{2,26},{10... | collective-permute-start | bytes 786440 | tf_op jit(solution)/shard_map/ppermute | solution.py:132
  17.8 9.0 %collective-permute-start.12 = (bf16[16,8192]{1,0:T(8,128)(2,1)S(1)}, bf16[16,8192]{1,0:T(8,128)(2,1)S(1)}, u32[]{:S(2)}, u32[]{:S(2)}) collective-permute-start(bf16[16,8192]{1,0:T(8,128)(2,1)S(1)} %constant_dynamic-update-slice_fusion), channel_id=1, source_target_pairs={{0,2},{2,4},{4,6},{6,0},{1,3},{3,5},{5,7},{7,1},{8,10},{10,12},{12... | collective-permute-start | bytes 786440 | tf_op jit(solution)/shard_map/ppermute | solution.py:131
  19.5 7.4 %collective-permute-start.11 = (bf16[16,8192]{1,0:T(8,128)(2,1)S(1)}, bf16[16,8192]{1,0:T(8,128)(2,1)S(1)}, u32[]{:S(2)}, u32[]{:S(2)}) collective-permute-start(bf16[16,8192]{1,0:T(8,128)(2,1)S(1)} %constant_dynamic-update-slice_fusion), channel_id=1, source_target_pairs={{0,6},{2,0},{4,2},{6,4},{1,7},{3,1},{5,3},{7,5},{8,14},{10,8},{12,... | collective-permute-start | bytes 786440 | tf_op jit(solution)/shard_map/ppermute | solution.py:132
  21.7 7.8 %collective-permute-start.3 = (bf16[8,8192]{1,0:T(8,128)(2,1)S(1)}, bf16[8,8192]{1,0:T(8,128)(2,1)S(1)}, u32[]{:S(2)}, u32[]{:S(2)}) collective-permute-start(bf16[8,8192]{1,0:T(8,128)(2,1)S(1)} %slice.123), channel_id=1, source_target_pairs={{0,8},{8,16},{16,24},{24,0},{1,9},{9,17},{17,25},{25,1},{2,10},{10... | collective-permute-start | bytes 393224 | tf_op jit(solution)/shard_map/ppermute | solution.py:133
  23.0 6.6 %collective-permute-start.4 = (bf16[8,8192]{1,0:T(8,128)(2,1)S(1)}, bf16[8,8192]{1,0:T(8,128)(2,1)S(1)}, u32[]{:S(2)}, u32[]{:S(2)}) collective-permute-start(bf16[8,8192]{1,0:T(8,128)(2,1)S(1)} %slice.124), channel_id=1, source_target_pairs={{0,24},{8,0},{16,8},{24,16},{1,25},{9,1},{17,9},{25,17},{2,26},{10... | collective-permute-start | bytes 393224 | tf_op jit(solution)/shard_map/ppermute | solution.py:134
  26.7 5.8 %collective-permute-start.13 = (bf16[8,8192]{1,0:T(8,128)(2,1)S(1)}, bf16[8,8192]{1,0:T(8,128)(2,1)S(1)}, u32[]{:S(2)}, u32[]{:S(2)}) collective-permute-start(bf16[8,8192]{1,0:T(8,128)(2,1)S(1)} %slice.127), channel_id=1, source_target_pairs={{0,2},{2,4},{4,6},{6,0},{1,3},{3,5},{5,7},{7,1},{8,10},{10,12},{12... | collective-permute-start | bytes 393224 | tf_op jit(solution)/shard_map/ppermute | solution.py:133
  26.8 5.6 %collective-permute-start.14 = (bf16[8,8192]{1,0:T(8,128)(2,1)S(1)}, bf16[8,8192]{1,0:T(8,128)(2,1)S(1)}, u32[]{:S(2)}, u32[]{:S(2)}) collective-permute-start(bf16[8,8192]{1,0:T(8,128)(2,1)S(1)} %slice.128), channel_id=1, source_target_pairs={{0,6},{2,0},{4,2},{6,4},{1,7},{3,1},{5,3},{7,5},{8,14},{10,8},{12,... | collective-permute-start | bytes 393224 | tf_op jit(solution)/shard_map/ppermute | solution.py:134
  29.7 25.3 %collective-permute-start.6 = (bf16[64,8192]{1,0:T(8,128)(2,1)S(1)}, bf16[64,8192]{1,0:T(8,128)(2,1)S(1)}, u32[]{:S(2)}, u32[]{:S(2)}) collective-permute-start(bf16[64,8192]{1,0:T(8,128)(2,1)S(1)} %bitcast.68), channel_id=1, source_target_pairs={{0,2},{2,4},{4,6},{6,0},{1,3},{3,5},{5,7},{7,1},{8,10},{10,12},{12... | collective-permute-start | bytes 3145736 | tf_op jit(solution)/shard_map/ppermute | solution.py:131
  29.8 25.3 %collective-permute-start.5 = (bf16[64,8192]{1,0:T(8,128)(2,1)S(1)}, bf16[64,8192]{1,0:T(8,128)(2,1)S(1)}, u32[]{:S(2)}, u32[]{:S(2)}) collective-permute-start(bf16[64,8192]{1,0:T(8,128)(2,1)S(1)} %bitcast.69), channel_id=1, source_target_pairs={{0,6},{2,0},{4,2},{6,4},{1,7},{3,1},{5,3},{7,5},{8,14},{10,8},{12,... | collective-permute-start | bytes 3145736 | tf_op jit(solution)/shard_map/ppermute | solution.py:132
  32.7 25.6 %collective-permute-start.16 = (bf16[64,8192]{1,0:T(8,128)(2,1)S(1)}, bf16[64,8192]{1,0:T(8,128)(2,1)S(1)}, u32[]{:S(2)}, u32[]{:S(2)}) collective-permute-start(bf16[64,8192]{1,0:T(8,128)(2,1)S(1)} %bitcast.71), channel_id=1, source_target_pairs={{0,8},{8,16},{16,24},{24,0},{1,9},{9,17},{17,25},{25,1},{2,10},{10... | collective-permute-start | bytes 3145736 | tf_op jit(solution)/shard_map/ppermute | solution.py:131
  33.9 25.6 %collective-permute-start.15 = (bf16[64,8192]{1,0:T(8,128)(2,1)S(1)}, bf16[64,8192]{1,0:T(8,128)(2,1)S(1)}, u32[]{:S(2)}, u32[]{:S(2)}) collective-permute-start(bf16[64,8192]{1,0:T(8,128)(2,1)S(1)} %bitcast.72), channel_id=1, source_target_pairs={{0,24},{8,0},{16,8},{24,16},{1,25},{9,1},{17,9},{25,17},{2,26},{10... | collective-permute-start | bytes 3145736 | tf_op jit(solution)/shard_map/ppermute | solution.py:132
  55.0 12.2 %collective-permute-start.7 = (bf16[32,8192]{1,0:T(8,128)(2,1)S(1)}, bf16[32,8192]{1,0:T(8,128)(2,1)S(1)}, u32[]{:S(2)}, u32[]{:S(2)}) collective-permute-start(bf16[32,8192]{1,0:T(8,128)(2,1)S(1)} %slice.125), channel_id=1, source_target_pairs={{0,2},{2,4},{4,6},{6,0},{1,3},{3,5},{5,7},{7,1},{8,10},{10,12},{12... | collective-permute-start | bytes 1572872 | tf_op jit(solution)/shard_map/ppermute | solution.py:133
  55.2 12.1 %collective-permute-start.8 = (bf16[32,8192]{1,0:T(8,128)(2,1)S(1)}, bf16[32,8192]{1,0:T(8,128)(2,1)S(1)}, u32[]{:S(2)}, u32[]{:S(2)}) collective-permute-start(bf16[32,8192]{1,0:T(8,128)(2,1)S(1)} %slice.126), channel_id=1, source_target_pairs={{0,6},{2,0},{4,2},{6,4},{1,7},{3,1},{5,3},{7,5},{8,14},{10,8},{12,... | collective-permute-start | bytes 1572872 | tf_op jit(solution)/shard_map/ppermute | solution.py:134
  58.3 12.0 %collective-permute-start.17 = (bf16[32,8192]{1,0:T(8,128)(2,1)S(1)}, bf16[32,8192]{1,0:T(8,128)(2,1)S(1)}, u32[]{:S(2)}, u32[]{:S(2)}) collective-permute-start(bf16[32,8192]{1,0:T(8,128)(2,1)S(1)} %slice.129), channel_id=1, source_target_pairs={{0,8},{8,16},{16,24},{24,0},{1,9},{9,17},{17,25},{25,1},{2,10},{10... | collective-permute-start | bytes 1572872 | tf_op jit(solution)/shard_map/ppermute | solution.py:133
  59.6 10.7 %collective-permute-start.18 = (bf16[32,8192]{1,0:T(8,128)(2,1)S(1)}, bf16[32,8192]{1,0:T(8,128)(2,1)S(1)}, u32[]{:S(2)}, u32[]{:S(2)}) collective-permute-start(bf16[32,8192]{1,0:T(8,128)(2,1)S(1)} %slice.130), channel_id=1, source_target_pairs={{0,24},{8,0},{16,8},{24,16},{1,25},{9,1},{17,9},{25,17},{2,26},{10... | collective-permute-start | bytes 1572872 | tf_op jit(solution)/shard_map/ppermute | solution.py:134
  80.3 23.3 %collective-permute-start.19 = (bf16[512,8192]{1,0:T(8,128)(2,1)}, bf16[512,8192]{1,0:T(8,128)(2,1)}, u32[]{:S(2)}, u32[]{:S(2)}) collective-permute-start(bf16[512,8192]{1,0:T(8,128)(2,1)} %pad_maximum_fusion), channel_id=1, source_target_pairs={{0,1},{1,0},{2,3},{3,2},{4,5},{5,4},{6,7},{7,6},{8,9},{9,8},{10,11... | collective-permute-start | bytes 25165832 | tf_op jit(solution)/shard_map/ppermute | solution.py:175
  103.6 19.1 %copy-start.1 = (f32[16,512]{1,0:T(8,128)S(1)}, f32[16,512]{1,0:T(8,128)}, u32[]{:S(2)}) copy-start(f32[16,512]{1,0:T(8,128)} %shard_map.46) | copy-start | bytes 98308

commit v11 on v10

--- a/solution.py
+++ b/solution.py
@@ -114,12 +114,6 @@
             flops=2 * TOP_K * rows * columns, transcendentals=0, bytes_accessed=4 * rows * columns
         ),
     )(scores)
-
-
-def row_topk(values):
-    count = values.shape[0]
-    padded = jnp.pad(values.T, ((0, 0), (0, LANES - count)), constant_values=-jnp.inf)
-    return column_topk(padded)[:, :count].T
 
 
 def ring_gather(block, axis):
@@ -205,7 +199,7 @@
     received = received.reshape(mass_count, shard_count, capacity, TOP_K)
     received = received.transpose(0, 2, 1, 3).reshape(mass_count * capacity, -1)
     candidates = jnp.take(received, slot_index, axis=0)
-    return row_topk(candidates)
+    return lax.top_k(candidates, TOP_K)[0]
 
 
 def solution(mesh):

time: 151 us -> 149 us (0.987)
  other arithmetic: 19.8 us -> 22.3 us
  local copies, waits for them, and re-layouts: 9.26 us -> 7.05 us
  Pallas kernels: 8.24 us -> 6.51 us
    top_k x0 -> x1, other arithmetic: none -> 2.52 us  [per_device(): return lax.top_k(candidates, TOP_K)[0]]
    pallas_call x3 -> x2, Pallas kernels: 8.24 us -> 6.51 us  [column_topk(): pl.pallas_call(column_topk_kernel, out_shape=jax.ShapeDtypeStruct((TOP_K,...]
where the time goes in v11:
time: 149 us
  starting transfers between devices  33.7 us (23%)
  matrix products  32 us (21%)
  waiting for transfers between devices  30.4 us (20%)
  other arithmetic  22.3 us (15%)
  blocking collectives  16.8 us (11%)
  local copies, waits for them, and re-layouts  7.05 us (5%)
  Pallas kernels  6.51 us (4%)
    ppermute x4, waiting for transfers between devices, ring_gather(): from_minus = lax.ppermute(flat, axis, forward)  21.8 us
    all_to_all x1, blocking collectives, per_device(): lax.all_to_all(outgoing, ('mass', 'x', 'z', 'core'), split_axis=0, concat...  16.8 us
    dot_general x1, matrix products, per_device(): lax.dot_general(library, own_side, (((1,), (1,)), ((), ())), preferred_el...  15.8 us
    dot_general x1, matrix products, per_device(): lax.dot_general(library, other_side, (((1,), (1,)), ((), ())), preferred_...  15.8 us
    ppermute x4, starting transfers between devices, ring_gather(): far_second = lax.ppermute(from_plus[half:], axis, backward)  9.09 us
    ppermute x4, starting transfers between devices, ring_gather(): from_plus = lax.ppermute(flat, axis, backward)  7.9 us
    concatenate x1, other arithmetic, per_device(): jnp.concatenate([part_a.reshape(-1, arrived.shape[1]), part_b.reshape(-1,...  7.67 us
    ppermute x4, waiting for transfers between devices, ring_gather(): far_first = lax.ppermute(from_minus[:half], axis, forward)  6.61 us
  transfers between devices with their start and end apart: 20, of which 7 were waited for; matrix products, arithmetic and copies ran while one was open for 13% of the time, Pallas kernels for 2%

profile of v11, /device:TPU:1, one launch (start us, length us, event | category | flops | bytes accessed | tf_op | source)
XLA Modules:
  0.0 149.1 jit_solution(9082372559578851693)
XLA Ops:
  0.0 0.7 and_compare_fusion.12
  0.7 1.0 pad_maximum_fusion.5
  1.8 1.1 pad_select_fusion.11
  6.2 0.4 multiply_reduce_fusion
  6.7 0.4 fusion
  7.2 2.2 %collective-permute-start = (bf16[8,8192]{1,0:T(8,128)(2,1)S(1)}, bf16[8,8192]{1,0:T(8,128)(2,1)S(1)}, u32[]{:S(2)}, u32[]{:S(2)}) collective-permute-start(bf16[8,8192]{1,0:T(8,128)(2,1)S(1)} %get-tuple-element.26), channel_id=1, source_target_pairs={{0,32},{32,64},{64,96},{96,0},{1,33},{33,65},{65,97},{97,1},{2,34}... | collective-permute-start | bytes 393224 | tf_op jit(solution)/shard_map/ppermute | solution.py:155
  9.4 2.6 %collective-permute-start.9 = (bf16[8,8192]{1,0:T(8,128)(2,1)S(1)}, bf16[8,8192]{1,0:T(8,128)(2,1)S(1)}, u32[]{:S(2)}, u32[]{:S(2)}) collective-permute-start(bf16[8,8192]{1,0:T(8,128)(2,1)S(1)} %get-tuple-element.25), channel_id=1, source_target_pairs={{0,64},{32,96},{64,0},{96,32},{1,65},{33,97},{65,1},{97,33},{2,66}... | collective-permute-start | bytes 393224 | tf_op jit(solution)/shard_map/ppermute | solution.py:155
  12.0 1.1 collective-permute-start.10
  13.1 0.8 collective-permute-done
  13.9 1.2 collective-permute-start.2
  15.1 1.6 %collective-permute-start.1 = (bf16[16,8192]{1,0:T(8,128)(2,1)S(1)}, bf16[16,8192]{1,0:T(8,128)(2,1)S(1)}, u32[]{:S(2)}, u32[]{:S(2)}) collective-permute-start(bf16[16,8192]{1,0:T(8,128)(2,1)S(1)} %get-tuple-element.28), channel_id=1, source_target_pairs={{0,24},{8,0},{16,8},{24,16},{1,25},{9,1},{17,9},{25,17},{2,26},{10... | collective-permute-start | bytes 786440 | tf_op jit(solution)/shard_map/ppermute | solution.py:126
  16.7 1.0 collective-permute-done.9
  17.8 1.7 %collective-permute-start.12 = (bf16[16,8192]{1,0:T(8,128)(2,1)S(1)}, bf16[16,8192]{1,0:T(8,128)(2,1)S(1)}, u32[]{:S(2)}, u32[]{:S(2)}) collective-permute-start(bf16[16,8192]{1,0:T(8,128)(2,1)S(1)} %constant_dynamic-update-slice_fusion), channel_id=1, source_target_pairs={{0,2},{2,4},{4,6},{6,0},{1,3},{3,5},{5,7},{7,1},{8,10},{10,12},{12... | collective-permute-start | bytes 786440 | tf_op jit(solution)/shard_map/ppermute | solution.py:125
  19.5 2.2 %collective-permute-start.11 = (bf16[16,8192]{1,0:T(8,128)(2,1)S(1)}, bf16[16,8192]{1,0:T(8,128)(2,1)S(1)}, u32[]{:S(2)}, u32[]{:S(2)}) collective-permute-start(bf16[16,8192]{1,0:T(8,128)(2,1)S(1)} %constant_dynamic-update-slice_fusion), channel_id=1, source_target_pairs={{0,6},{2,0},{4,2},{6,4},{1,7},{3,1},{5,3},{7,5},{8,14},{10,8},{12,... | collective-permute-start | bytes 786440 | tf_op jit(solution)/shard_map/ppermute | solution.py:126
  21.7 1.2 collective-permute-start.3
  23.0 1.6 %collective-permute-start.4 = (bf16[8,8192]{1,0:T(8,128)(2,1)S(1)}, bf16[8,8192]{1,0:T(8,128)(2,1)S(1)}, u32[]{:S(2)}, u32[]{:S(2)}) collective-permute-start(bf16[8,8192]{1,0:T(8,128)(2,1)S(1)} %slice.121), channel_id=1, source_target_pairs={{0,24},{8,0},{16,8},{24,16},{1,25},{9,1},{17,9},{25,17},{2,26},{10... | collective-permute-start | bytes 393224 | tf_op jit(solution)/shard_map/ppermute | solution.py:128
  24.6 2.1 %collective-permute-done.12 = bf16[16,8192]{1,0:T(8,128)(2,1)S(1)} collective-permute-done((bf16[16,8192]{1,0:T(8,128)(2,1)S(1)}, bf16[16,8192]{1,0:T(8,128)(2,1)S(1)}, u32[]{:S(2)}, u32[]{:S(2)}) %collective-permute-start.12) | collective-permute-done | bytes 262176 | tf_op jit(solution)/shard_map/ppermute | solution.py:125
  26.8 2.7 %collective-permute-start.14 = (bf16[8,8192]{1,0:T(8,128)(2,1)S(1)}, bf16[8,8192]{1,0:T(8,128)(2,1)S(1)}, u32[]{:S(2)}, u32[]{:S(2)}) collective-permute-start(bf16[8,8192]{1,0:T(8,128)(2,1)S(1)} %slice.125), channel_id=1, source_target_pairs={{0,6},{2,0},{4,2},{6,4},{1,7},{3,1},{5,3},{7,5},{8,14},{10,8},{12,... | collective-permute-start | bytes 393224 | tf_op jit(solution)/shard_map/ppermute | solution.py:128
  29.8 2.7 %collective-permute-start.5 = (bf16[64,8192]{1,0:T(8,128)(2,1)S(1)}, bf16[64,8192]{1,0:T(8,128)(2,1)S(1)}, u32[]{:S(2)}, u32[]{:S(2)}) collective-permute-start(bf16[64,8192]{1,0:T(8,128)(2,1)S(1)} %bitcast.66), channel_id=1, source_target_pairs={{0,6},{2,0},{4,2},{6,4},{1,7},{3,1},{5,3},{7,5},{8,14},{10,8},{12,... | collective-permute-start | bytes 3145736 | tf_op jit(solution)/shard_map/ppermute | solution.py:126
  32.7 1.3 collective-permute-start.16
  33.9 1.5 collective-permute-start.15
  35.4 19.6 %collective-permute-done.6 = bf16[64,8192]{1,0:T(8,128)(2,1)S(1)} collective-permute-done((bf16[64,8192]{1,0:T(8,128)(2,1)S(1)}, bf16[64,8192]{1,0:T(8,128)(2,1)S(1)}, u32[]{:S(2)}, u32[]{:S(2)}) %collective-permute-start.6) | collective-permute-done | bytes 1048608 | tf_op jit(solution)/shard_map/ppermute | solution.py:125
  55.2 3.1 %collective-permute-start.8 = (bf16[32,8192]{1,0:T(8,128)(2,1)S(1)}, bf16[32,8192]{1,0:T(8,128)(2,1)S(1)}, u32[]{:S(2)}, u32[]{:S(2)}) collective-permute-start(bf16[32,8192]{1,0:T(8,128)(2,1)S(1)} %slice.123), channel_id=1, source_target_pairs={{0,6},{2,0},{4,2},{6,4},{1,7},{3,1},{5,3},{7,5},{8,14},{10,8},{12,... | collective-permute-start | bytes 1572872 | tf_op jit(solution)/shard_map/ppermute | solution.py:128
  58.3 1.3 collective-permute-start.17
  59.6 1.7 %collective-permute-start.18 = (bf16[32,8192]{1,0:T(8,128)(2,1)S(1)}, bf16[32,8192]{1,0:T(8,128)(2,1)S(1)}, u32[]{:S(2)}, u32[]{:S(2)}) collective-permute-start(bf16[32,8192]{1,0:T(8,128)(2,1)S(1)} %slice.127), channel_id=1, source_target_pairs={{0,24},{8,0},{16,8},{24,16},{1,25},{9,1},{17,9},{25,17},{2,26},{10... | collective-permute-start | bytes 1572872 | tf_op jit(solution)/shard_map/ppermute | solution.py:128
  61.3 5.9 %collective-permute-done.7 = bf16[32,8192]{1,0:T(8,128)(2,1)S(1)} collective-permute-done((bf16[32,8192]{1,0:T(8,128)(2,1)S(1)}, bf16[32,8192]{1,0:T(8,128)(2,1)S(1)}, u32[]{:S(2)}, u32[]{:S(2)}) %collective-permute-start.7) | collective-permute-done | bytes 524320 | tf_op jit(solution)/shard_map/ppermute | solution.py:127
  67.3 2.3 %pad_maximum_fusion.1 = bf16[4,64,8192]{2,1,0:T(8,128)(2,1)} fusion(bf16[1,64,8192]{2,1,0:T(8,128)(2,1)S(1)} %bitcast.71, bf16[1,64,8192]{2,1,0:T(8,128)(2,1)S(1)} %maximum_bitcast_fusion, bf16[1,64,8192]{2,1,0:T(8,128)(2,1)S(1)} %bitcast.72, bf16[1,64,8192]{2,1,0:T(8,128)(2,1)S(1)} %bitcast.67), kind=kLoop, calls=%fused_computation.5 | loop fusion | flops 6291456 | bytes 8388608 | tf_op jit(solution)/shard_map/stack | solution.py:130
  69.6 0.7 collective-permute-done.17
  70.4 2.2 %pad_maximum_fusion.2 = bf16[4,64,8192]{2,1,0:T(8,128)(2,1)} fusion(bf16[1,64,8192]{2,1,0:T(8,128)(2,1)S(1)} %bitcast.73, bf16[1,64,8192]{2,1,0:T(8,128)(2,1)S(1)} %maximum_bitcast_fusion.1, bf16[1,64,8192]{2,1,0:T(8,128)(2,1)S(1)} %bitcast.74, bf16[1,64,8192]{2,1,0:T(8,128)(2,1)S(1)} %bitcast.70), kind=kLoop, calls=%fused_computation.6 | loop fusion | flops 6291456 | bytes 8388608 | tf_op jit(solution)/shard_map/stack | solution.py:130
  72.6 7.7 %pad_maximum_fusion = bf16[512,8192]{1,0:T(8,128)(2,1)} fusion(bf16[256,8192]{1,0:T(8,128)(2,1)} %bitcast.63, bf16[256,8192]{1,0:T(8,128)(2,1)} %bitcast.61), kind=kLoop, calls=%fused_computation.4 | loop fusion | flops 16777216 | bytes 16777216 | tf_op jit(solution)/shard_map/concatenate | solution.py:165
  80.3 3.9 %collective-permute-start.19 = (bf16[512,8192]{1,0:T(8,128)(2,1)}, bf16[512,8192]{1,0:T(8,128)(2,1)}, u32[]{:S(2)}, u32[]{:S(2)}) collective-permute-start(bf16[512,8192]{1,0:T(8,128)(2,1)} %pad_maximum_fusion), channel_id=1, source_target_pairs={{0,1},{1,0},{2,3},{3,2},{4,5},{5,4},{6,7},{7,6},{8,9},{9,8},{10,11... | collective-permute-start | bytes 25165832 | tf_op jit(solution)/shard_map/ppermute | solution.py:169
  84.5 15.8 %convolution_bitcast_fusion.1.scores_ref = f32[1024,512]{1,0:T(8,128)} fusion(bf16[1024,8192]{1,0:T(8,128)(2,1)} %param.7, bf16[256,8192]{1,0:T(8,128)(2,1)} %bitcast.64, bf16[256,8192]{1,0:T(8,128)(2,1)} %bitcast.62), kind=kOutput, calls=%fused_computation.8 | convolution fusion | flops 8606711808 | bytes 27262976 | tf_op jit(solution)/shard_map/dot_general | solution.py:171
  100.3 3.3 %shard_map.46 = f32[16,512]{1,0:T(8,128)} custom-call(f32[1024,512]{1,0:T(8,128)} %convolution_bitcast_fusion.1.scores_ref), custom_call_target="tpu_custom_call" | custom-call | flops 16777216 | bytes 2097152 | tf_op jit(solution)/shard_map/pallas_call | solution.py:107
  103.6 15.8 %convolution_bitcast_fusion.scores_ref = f32[1024,512]{1,0:T(8,128)} fusion(bf16[512,8192]{1,0:T(8,128)(2,1)} %collective-permute-done.19, bf16[1024,8192]{1,0:T(8,128)(2,1)} %param.7), kind=kOutput, calls=%fused_computation.7 | convolution fusion | flops 8589934592 | bytes 27262976 | tf_op jit(solution)/shard_map/dot_general | solution.py:176
  119.4 3.3 %shard_map.47 = f32[16,512]{1,0:T(8,128)} custom-call(f32[1024,512]{1,0:T(8,128)} %convolution_bitcast_fusion.scores_ref), custom_call_target="tpu_custom_call" | custom-call | flops 16777216 | bytes 2097152 | tf_op jit(solution)/shard_map/pallas_call | solution.py:107
  122.6 0.8 maximum_bitcast_fusion.4
  123.4 0.2 copy.30
  123.6 2.8 %gather_fusion = f32[1024,16]{1,0:T(8,128)S(1)} fusion(f32[1024,16]{1,0:T(8,128)S(1)} %copy.30, s32[1024]{0:T(1024)S(1)} %get-tuple-element.43), kind=kCustom, calls=%fused_computation | custom fusion | bytes 135168 | tf_op jit(solution)/shard_map/jit(_take)/gather | solution.py:195
  126.4 0.2 bitcast_select_fusion
  126.6 0.2 reshape.573
  126.9 16.8 %all_to_all.5 = f32[128,1,128]{2,1,0:T(1,128)S(1)} all-to-all(f32[128,1,128]{2,1,0:T(1,128)S(1)} %reshape.573), channel_id=1, replica_groups=mesh['mass'=4,'x'=4,'z'=4,'core'=2] {'mass','x','z','core'}, dimensions={0} | all-to-all | bytes 131072 | tf_op jit(solution)/shard_map/all_to_all | solution.py:196
  143.7 0.5 broadcast.1066
  144.2 0.8 reduce
  145.2 0.2 copy.35
  145.4 0.2 copy.32
  145.7 0.3 reshape.481
  145.9 0.6 gather_fusion.1
  146.6 2.5 %sort_prefixfusion = f32[16,16]{1,0:T(8,128)} fusion(f32[16,512]{1,0:T(8,128)S(1)} %broadcast_select_fusion), kind=kCustom, calls=%top_k.9.sort_prefix | custom fusion | flops 106496 | bytes 33792 | tf_op jit(solution)/shard_map/top_k | solution.py:202
  (76 shorter events, 5.1 us)
Async XLA Ops:
  5.2 1.0 copy-start
  5.3 1.3 copy-start.2
  7.2 6.7 %collective-permute-start = (bf16[8,8192]{1,0:T(8,128)(2,1)S(1)}, bf16[8,8192]{1,0:T(8,128)(2,1)S(1)}, u32[]{:S(2)}, u32[]{:S(2)}) collective-permute-start(bf16[8,8192]{1,0:T(8,128)(2,1)S(1)} %get-tuple-element.26), channel_id=1, source_target_pairs={{0,32},{32,64},{64,96},{96,0},{1,33},{33,65},{65,97},{97,1},{2,34}... | collective-permute-start | bytes 393224 | tf_op jit(solution)/shard_map/ppermute | solution.py:155
  9.4 8.3 %collective-permute-start.9 = (bf16[8,8192]{1,0:T(8,128)(2,1)S(1)}, bf16[8,8192]{1,0:T(8,128)(2,1)S(1)}, u32[]{:S(2)}, u32[]{:S(2)}) collective-permute-start(bf16[8,8192]{1,0:T(8,128)(2,1)S(1)} %get-tuple-element.25), channel_id=1, source_target_pairs={{0,64},{32,96},{64,0},{96,32},{1,65},{33,97},{65,1},{97,33},{2,66}... | collective-permute-start | bytes 393224 | tf_op jit(solution)/shard_map/ppermute | solution.py:155
  12.0 5.7 %collective-permute-start.10 = (bf16[8,8192]{1,0:T(8,128)(2,1)S(1)}, bf16[8,8192]{1,0:T(8,128)(2,1)S(1)}, u32[]{:S(2)}, u32[]{:S(2)}) collective-permute-start(bf16[8,8192]{1,0:T(8,128)(2,1)S(1)} %get-tuple-element.24), channel_id=1, source_target_pairs={{0,96},{32,0},{64,32},{96,64},{1,97},{33,1},{65,33},{97,65},{2,98}... | collective-permute-start | bytes 393224 | tf_op jit(solution)/shard_map/ppermute | solution.py:155
  13.9 7.8 %collective-permute-start.2 = (bf16[16,8192]{1,0:T(8,128)(2,1)S(1)}, bf16[16,8192]{1,0:T(8,128)(2,1)S(1)}, u32[]{:S(2)}, u32[]{:S(2)}) collective-permute-start(bf16[16,8192]{1,0:T(8,128)(2,1)S(1)} %get-tuple-element.28), channel_id=1, source_target_pairs={{0,8},{8,16},{16,24},{24,0},{1,9},{9,17},{17,25},{25,1},{2,10},{10... | collective-permute-start | bytes 786440 | tf_op jit(solution)/shard_map/ppermute | solution.py:125
  15.1 7.9 %collective-permute-start.1 = (bf16[16,8192]{1,0:T(8,128)(2,1)S(1)}, bf16[16,8192]{1,0:T(8,128)(2,1)S(1)}, u32[]{:S(2)}, u32[]{:S(2)}) collective-permute-start(bf16[16,8192]{1,0:T(8,128)(2,1)S(1)} %get-tuple-element.28), channel_id=1, source_target_pairs={{0,24},{8,0},{16,8},{24,16},{1,25},{9,1},{17,9},{25,17},{2,26},{10... | collective-permute-start | bytes 786440 | tf_op jit(solution)/shard_map/ppermute | solution.py:126
  17.8 9.0 %collective-permute-start.12 = (bf16[16,8192]{1,0:T(8,128)(2,1)S(1)}, bf16[16,8192]{1,0:T(8,128)(2,1)S(1)}, u32[]{:S(2)}, u32[]{:S(2)}) collective-permute-start(bf16[16,8192]{1,0:T(8,128)(2,1)S(1)} %constant_dynamic-update-slice_fusion), channel_id=1, source_target_pairs={{0,2},{2,4},{4,6},{6,0},{1,3},{3,5},{5,7},{7,1},{8,10},{10,12},{12... | collective-permute-start | bytes 786440 | tf_op jit(solution)/shard_map/ppermute | solution.py:125
  19.5 7.4 %collective-permute-start.11 = (bf16[16,8192]{1,0:T(8,128)(2,1)S(1)}, bf16[16,8192]{1,0:T(8,128)(2,1)S(1)}, u32[]{:S(2)}, u32[]{:S(2)}) collective-permute-start(bf16[16,8192]{1,0:T(8,128)(2,1)S(1)} %constant_dynamic-update-slice_fusion), channel_id=1, source_target_pairs={{0,6},{2,0},{4,2},{6,4},{1,7},{3,1},{5,3},{7,5},{8,14},{10,8},{12,... | collective-permute-start | bytes 786440 | tf_op jit(solution)/shard_map/ppermute | solution.py:126
  21.7 7.8 %collective-permute-start.3 = (bf16[8,8192]{1,0:T(8,128)(2,1)S(1)}, bf16[8,8192]{1,0:T(8,128)(2,1)S(1)}, u32[]{:S(2)}, u32[]{:S(2)}) collective-permute-start(bf16[8,8192]{1,0:T(8,128)(2,1)S(1)} %slice.120), channel_id=1, source_target_pairs={{0,8},{8,16},{16,24},{24,0},{1,9},{9,17},{17,25},{25,1},{2,10},{10... | collective-permute-start | bytes 393224 | tf_op jit(solution)/shard_map/ppermute | solution.py:127
  23.0 6.6 %collective-permute-start.4 = (bf16[8,8192]{1,0:T(8,128)(2,1)S(1)}, bf16[8,8192]{1,0:T(8,128)(2,1)S(1)}, u32[]{:S(2)}, u32[]{:S(2)}) collective-permute-start(bf16[8,8192]{1,0:T(8,128)(2,1)S(1)} %slice.121), channel_id=1, source_target_pairs={{0,24},{8,0},{16,8},{24,16},{1,25},{9,1},{17,9},{25,17},{2,26},{10... | collective-permute-start | bytes 393224 | tf_op jit(solution)/shard_map/ppermute | solution.py:128
  26.7 5.8 %collective-permute-start.13 = (bf16[8,8192]{1,0:T(8,128)(2,1)S(1)}, bf16[8,8192]{1,0:T(8,128)(2,1)S(1)}, u32[]{:S(2)}, u32[]{:S(2)}) collective-permute-start(bf16[8,8192]{1,0:T(8,128)(2,1)S(1)} %slice.124), channel_id=1, source_target_pairs={{0,2},{2,4},{4,6},{6,0},{1,3},{3,5},{5,7},{7,1},{8,10},{10,12},{12... | collective-permute-start | bytes 393224 | tf_op jit(solution)/shard_map/ppermute | solution.py:127
  26.8 5.6 %collective-permute-start.14 = (bf16[8,8192]{1,0:T(8,128)(2,1)S(1)}, bf16[8,8192]{1,0:T(8,128)(2,1)S(1)}, u32[]{:S(2)}, u32[]{:S(2)}) collective-permute-start(bf16[8,8192]{1,0:T(8,128)(2,1)S(1)} %slice.125), channel_id=1, source_target_pairs={{0,6},{2,0},{4,2},{6,4},{1,7},{3,1},{5,3},{7,5},{8,14},{10,8},{12,... | collective-permute-start | bytes 393224 | tf_op jit(solution)/shard_map/ppermute | solution.py:128
  29.7 25.3 %collective-permute-start.6 = (bf16[64,8192]{1,0:T(8,128)(2,1)S(1)}, bf16[64,8192]{1,0:T(8,128)(2,1)S(1)}, u32[]{:S(2)}, u32[]{:S(2)}) collective-permute-start(bf16[64,8192]{1,0:T(8,128)(2,1)S(1)} %bitcast.65), channel_id=1, source_target_pairs={{0,2},{2,4},{4,6},{6,0},{1,3},{3,5},{5,7},{7,1},{8,10},{10,12},{12... | collective-permute-start | bytes 3145736 | tf_op jit(solution)/shard_map/ppermute | solution.py:125
  29.8 25.3 %collective-permute-start.5 = (bf16[64,8192]{1,0:T(8,128)(2,1)S(1)}, bf16[64,8192]{1,0:T(8,128)(2,1)S(1)}, u32[]{:S(2)}, u32[]{:S(2)}) collective-permute-start(bf16[64,8192]{1,0:T(8,128)(2,1)S(1)} %bitcast.66), channel_id=1, source_target_pairs={{0,6},{2,0},{4,2},{6,4},{1,7},{3,1},{5,3},{7,5},{8,14},{10,8},{12,... | collective-permute-start | bytes 3145736 | tf_op jit(solution)/shard_map/ppermute | solution.py:126
  32.7 25.6 %collective-permute-start.16 = (bf16[64,8192]{1,0:T(8,128)(2,1)S(1)}, bf16[64,8192]{1,0:T(8,128)(2,1)S(1)}, u32[]{:S(2)}, u32[]{:S(2)}) collective-permute-start(bf16[64,8192]{1,0:T(8,128)(2,1)S(1)} %bitcast.68), channel_id=1, source_target_pairs={{0,8},{8,16},{16,24},{24,0},{1,9},{9,17},{17,25},{25,1},{2,10},{10... | collective-permute-start | bytes 3145736 | tf_op jit(solution)/shard_map/ppermute | solution.py:125
  33.9 25.6 %collective-permute-start.15 = (bf16[64,8192]{1,0:T(8,128)(2,1)S(1)}, bf16[64,8192]{1,0:T(8,128)(2,1)S(1)}, u32[]{:S(2)}, u32[]{:S(2)}) collective-permute-start(bf16[64,8192]{1,0:T(8,128)(2,1)S(1)} %bitcast.69), channel_id=1, source_target_pairs={{0,24},{8,0},{16,8},{24,16},{1,25},{9,1},{17,9},{25,17},{2,26},{10... | collective-permute-start | bytes 3145736 | tf_op jit(solution)/shard_map/ppermute | solution.py:126
  55.0 12.2 %collective-permute-start.7 = (bf16[32,8192]{1,0:T(8,128)(2,1)S(1)}, bf16[32,8192]{1,0:T(8,128)(2,1)S(1)}, u32[]{:S(2)}, u32[]{:S(2)}) collective-permute-start(bf16[32,8192]{1,0:T(8,128)(2,1)S(1)} %slice.122), channel_id=1, source_target_pairs={{0,2},{2,4},{4,6},{6,0},{1,3},{3,5},{5,7},{7,1},{8,10},{10,12},{12... | collective-permute-start | bytes 1572872 | tf_op jit(solution)/shard_map/ppermute | solution.py:127
  55.2 12.1 %collective-permute-start.8 = (bf16[32,8192]{1,0:T(8,128)(2,1)S(1)}, bf16[32,8192]{1,0:T(8,128)(2,1)S(1)}, u32[]{:S(2)}, u32[]{:S(2)}) collective-permute-start(bf16[32,8192]{1,0:T(8,128)(2,1)S(1)} %slice.123), channel_id=1, source_target_pairs={{0,6},{2,0},{4,2},{6,4},{1,7},{3,1},{5,3},{7,5},{8,14},{10,8},{12,... | collective-permute-start | bytes 1572872 | tf_op jit(solution)/shard_map/ppermute | solution.py:128
  58.3 12.0 %collective-permute-start.17 = (bf16[32,8192]{1,0:T(8,128)(2,1)S(1)}, bf16[32,8192]{1,0:T(8,128)(2,1)S(1)}, u32[]{:S(2)}, u32[]{:S(2)}) collective-permute-start(bf16[32,8192]{1,0:T(8,128)(2,1)S(1)} %slice.126), channel_id=1, source_target_pairs={{0,8},{8,16},{16,24},{24,0},{1,9},{9,17},{17,25},{25,1},{2,10},{10... | collective-permute-start | bytes 1572872 | tf_op jit(solution)/shard_map/ppermute | solution.py:127
  59.6 10.7 %collective-permute-start.18 = (bf16[32,8192]{1,0:T(8,128)(2,1)S(1)}, bf16[32,8192]{1,0:T(8,128)(2,1)S(1)}, u32[]{:S(2)}, u32[]{:S(2)}) collective-permute-start(bf16[32,8192]{1,0:T(8,128)(2,1)S(1)} %slice.127), channel_id=1, source_target_pairs={{0,24},{8,0},{16,8},{24,16},{1,25},{9,1},{17,9},{25,17},{2,26},{10... | collective-permute-start | bytes 1572872 | tf_op jit(solution)/shard_map/ppermute | solution.py:128
  80.3 23.3 %collective-permute-start.19 = (bf16[512,8192]{1,0:T(8,128)(2,1)}, bf16[512,8192]{1,0:T(8,128)(2,1)}, u32[]{:S(2)}, u32[]{:S(2)}) collective-permute-start(bf16[512,8192]{1,0:T(8,128)(2,1)} %pad_maximum_fusion), channel_id=1, source_target_pairs={{0,1},{1,0},{2,3},{3,2},{4,5},{5,4},{6,7},{7,6},{8,9},{9,8},{10,11... | collective-permute-start | bytes 25165832 | tf_op jit(solution)/shard_map/ppermute | solution.py:169
  103.6 19.1 %copy-start.1 = (f32[16,512]{1,0:T(8,128)S(1)}, f32[16,512]{1,0:T(8,128)}, u32[]{:S(2)}) copy-start(f32[16,512]{1,0:T(8,128)} %shard_map.46) | copy-start | bytes 98308

commit v12 on v11

--- a/solution.py
+++ b/solution.py
@@ -90,7 +90,7 @@
             ]
             return tuple(merge_sorted(list(kept), bitonic_sort(values)))
 
-        kept = lax.fori_loop(0, steps, insert, (lowest,) * TOP_K, unroll=2)
+        kept = lax.fori_loop(0, steps, insert, (lowest,) * TOP_K, unroll=True)
         kept = list(kept)
         shift = SUBLANES // 2
         while shift >= 1:

time: 149 us -> 149 us (level)
  no operation moved by 1% of the time
where the time goes in v12:
time: 149 us
  starting transfers between devices  33.7 us (23%)
  matrix products  32 us (21%)
  waiting for transfers between devices  30.4 us (20%)
  other arithmetic  22.3 us (15%)
  blocking collectives  16.8 us (11%)
  local copies, waits for them, and re-layouts  7.05 us (5%)
  Pallas kernels  6.02 us (4%)
    ppermute x4, waiting for transfers between devices, ring_gather(): from_minus = lax.ppermute(flat, axis, forward)  21.8 us
    all_to_all x1, blocking collectives, per_device(): lax.all_to_all(outgoing, ('mass', 'x', 'z', 'core'), split_axis=0, concat...  16.8 us
    dot_general x1, matrix products, per_device(): lax.dot_general(library, own_side, (((1,), (1,)), ((), ())), preferred_el...  15.8 us
    dot_general x1, matrix products, per_device(): lax.dot_general(library, other_side, (((1,), (1,)), ((), ())), preferred_...  15.8 us
    ppermute x4, starting transfers between devices, ring_gather(): far_second = lax.ppermute(from_plus[half:], axis, backward)  9.09 us
    ppermute x4, starting transfers between devices, ring_gather(): from_plus = lax.ppermute(flat, axis, backward)  7.9 us
    concatenate x1, other arithmetic, per_device(): jnp.concatenate([part_a.reshape(-1, arrived.shape[1]), part_b.reshape(-1,...  7.67 us
    ppermute x4, waiting for transfers between devices, ring_gather(): far_first = lax.ppermute(from_minus[:half], axis, forward)  6.61 us
  transfers between devices with their start and end apart: 20, of which 7 were waited for; matrix products, arithmetic and copies ran while one was open for 13% of the time, Pallas kernels for 2%

profile of v12, /device:TPU:1, one launch (start us, length us, event | category | flops | bytes accessed | tf_op | source)
XLA Modules:
  0.0 148.6 jit_solution(2143064914140245122)
XLA Ops:
  0.0 0.7 and_compare_fusion.12
  0.7 1.0 pad_maximum_fusion.5
  1.8 1.1 pad_select_fusion.11
  6.2 0.4 multiply_reduce_fusion
  6.7 0.4 fusion
  7.2 2.2 %collective-permute-start = (bf16[8,8192]{1,0:T(8,128)(2,1)S(1)}, bf16[8,8192]{1,0:T(8,128)(2,1)S(1)}, u32[]{:S(2)}, u32[]{:S(2)}) collective-permute-start(bf16[8,8192]{1,0:T(8,128)(2,1)S(1)} %get-tuple-element.26), channel_id=1, source_target_pairs={{0,32},{32,64},{64,96},{96,0},{1,33},{33,65},{65,97},{97,1},{2,34}... | collective-permute-start | bytes 393224 | tf_op jit(solution)/shard_map/ppermute | solution.py:155
  9.4 2.6 %collective-permute-start.9 = (bf16[8,8192]{1,0:T(8,128)(2,1)S(1)}, bf16[8,8192]{1,0:T(8,128)(2,1)S(1)}, u32[]{:S(2)}, u32[]{:S(2)}) collective-permute-start(bf16[8,8192]{1,0:T(8,128)(2,1)S(1)} %get-tuple-element.25), channel_id=1, source_target_pairs={{0,64},{32,96},{64,0},{96,32},{1,65},{33,97},{65,1},{97,33},{2,66}... | collective-permute-start | bytes 393224 | tf_op jit(solution)/shard_map/ppermute | solution.py:155
  12.0 1.1 collective-permute-start.10
  13.1 0.8 collective-permute-done
  13.9 1.2 collective-permute-start.2
  15.1 1.6 %collective-permute-start.1 = (bf16[16,8192]{1,0:T(8,128)(2,1)S(1)}, bf16[16,8192]{1,0:T(8,128)(2,1)S(1)}, u32[]{:S(2)}, u32[]{:S(2)}) collective-permute-start(bf16[16,8192]{1,0:T(8,128)(2,1)S(1)} %get-tuple-element.28), channel_id=1, source_target_pairs={{0,24},{8,0},{16,8},{24,16},{1,25},{9,1},{17,9},{25,17},{2,26},{10... | collective-permute-start | bytes 786440 | tf_op jit(solution)/shard_map/ppermute | solution.py:126
  16.7 1.0 collective-permute-done.9
  17.8 1.7 %collective-permute-start.12 = (bf16[16,8192]{1,0:T(8,128)(2,1)S(1)}, bf16[16,8192]{1,0:T(8,128)(2,1)S(1)}, u32[]{:S(2)}, u32[]{:S(2)}) collective-permute-start(bf16[16,8192]{1,0:T(8,128)(2,1)S(1)} %constant_dynamic-update-slice_fusion), channel_id=1, source_target_pairs={{0,2},{2,4},{4,6},{6,0},{1,3},{3,5},{5,7},{7,1},{8,10},{10,12},{12... | collective-permute-start | bytes 786440 | tf_op jit(solution)/shard_map/ppermute | solution.py:125
  19.5 2.2 %collective-permute-start.11 = (bf16[16,8192]{1,0:T(8,128)(2,1)S(1)}, bf16[16,8192]{1,0:T(8,128)(2,1)S(1)}, u32[]{:S(2)}, u32[]{:S(2)}) collective-permute-start(bf16[16,8192]{1,0:T(8,128)(2,1)S(1)} %constant_dynamic-update-slice_fusion), channel_id=1, source_target_pairs={{0,6},{2,0},{4,2},{6,4},{1,7},{3,1},{5,3},{7,5},{8,14},{10,8},{12,... | collective-permute-start | bytes 786440 | tf_op jit(solution)/shard_map/ppermute | solution.py:126
  21.7 1.2 collective-permute-start.3
  23.0 1.6 %collective-permute-start.4 = (bf16[8,8192]{1,0:T(8,128)(2,1)S(1)}, bf16[8,8192]{1,0:T(8,128)(2,1)S(1)}, u32[]{:S(2)}, u32[]{:S(2)}) collective-permute-start(bf16[8,8192]{1,0:T(8,128)(2,1)S(1)} %slice.121), channel_id=1, source_target_pairs={{0,24},{8,0},{16,8},{24,16},{1,25},{9,1},{17,9},{25,17},{2,26},{10... | collective-permute-start | bytes 393224 | tf_op jit(solution)/shard_map/ppermute | solution.py:128
  24.6 2.1 %collective-permute-done.12 = bf16[16,8192]{1,0:T(8,128)(2,1)S(1)} collective-permute-done((bf16[16,8192]{1,0:T(8,128)(2,1)S(1)}, bf16[16,8192]{1,0:T(8,128)(2,1)S(1)}, u32[]{:S(2)}, u32[]{:S(2)}) %collective-permute-start.12) | collective-permute-done | bytes 262176 | tf_op jit(solution)/shard_map/ppermute | solution.py:125
  26.8 2.7 %collective-permute-start.14 = (bf16[8,8192]{1,0:T(8,128)(2,1)S(1)}, bf16[8,8192]{1,0:T(8,128)(2,1)S(1)}, u32[]{:S(2)}, u32[]{:S(2)}) collective-permute-start(bf16[8,8192]{1,0:T(8,128)(2,1)S(1)} %slice.125), channel_id=1, source_target_pairs={{0,6},{2,0},{4,2},{6,4},{1,7},{3,1},{5,3},{7,5},{8,14},{10,8},{12,... | collective-permute-start | bytes 393224 | tf_op jit(solution)/shard_map/ppermute | solution.py:128
  29.8 2.7 %collective-permute-start.5 = (bf16[64,8192]{1,0:T(8,128)(2,1)S(1)}, bf16[64,8192]{1,0:T(8,128)(2,1)S(1)}, u32[]{:S(2)}, u32[]{:S(2)}) collective-permute-start(bf16[64,8192]{1,0:T(8,128)(2,1)S(1)} %bitcast.66), channel_id=1, source_target_pairs={{0,6},{2,0},{4,2},{6,4},{1,7},{3,1},{5,3},{7,5},{8,14},{10,8},{12,... | collective-permute-start | bytes 3145736 | tf_op jit(solution)/shard_map/ppermute | solution.py:126
  32.7 1.3 collective-permute-start.16
  33.9 1.5 collective-permute-start.15
  35.4 19.6 %collective-permute-done.6 = bf16[64,8192]{1,0:T(8,128)(2,1)S(1)} collective-permute-done((bf16[64,8192]{1,0:T(8,128)(2,1)S(1)}, bf16[64,8192]{1,0:T(8,128)(2,1)S(1)}, u32[]{:S(2)}, u32[]{:S(2)}) %collective-permute-start.6) | collective-permute-done | bytes 1048608 | tf_op jit(solution)/shard_map/ppermute | solution.py:125
  55.2 3.1 %collective-permute-start.8 = (bf16[32,8192]{1,0:T(8,128)(2,1)S(1)}, bf16[32,8192]{1,0:T(8,128)(2,1)S(1)}, u32[]{:S(2)}, u32[]{:S(2)}) collective-permute-start(bf16[32,8192]{1,0:T(8,128)(2,1)S(1)} %slice.123), channel_id=1, source_target_pairs={{0,6},{2,0},{4,2},{6,4},{1,7},{3,1},{5,3},{7,5},{8,14},{10,8},{12,... | collective-permute-start | bytes 1572872 | tf_op jit(solution)/shard_map/ppermute | solution.py:128
  58.3 1.3 collective-permute-start.17
  59.6 1.7 %collective-permute-start.18 = (bf16[32,8192]{1,0:T(8,128)(2,1)S(1)}, bf16[32,8192]{1,0:T(8,128)(2,1)S(1)}, u32[]{:S(2)}, u32[]{:S(2)}) collective-permute-start(bf16[32,8192]{1,0:T(8,128)(2,1)S(1)} %slice.127), channel_id=1, source_target_pairs={{0,24},{8,0},{16,8},{24,16},{1,25},{9,1},{17,9},{25,17},{2,26},{10... | collective-permute-start | bytes 1572872 | tf_op jit(solution)/shard_map/ppermute | solution.py:128
  61.3 5.9 %collective-permute-done.7 = bf16[32,8192]{1,0:T(8,128)(2,1)S(1)} collective-permute-done((bf16[32,8192]{1,0:T(8,128)(2,1)S(1)}, bf16[32,8192]{1,0:T(8,128)(2,1)S(1)}, u32[]{:S(2)}, u32[]{:S(2)}) %collective-permute-start.7) | collective-permute-done | bytes 524320 | tf_op jit(solution)/shard_map/ppermute | solution.py:127
  67.3 2.3 %pad_maximum_fusion.1 = bf16[4,64,8192]{2,1,0:T(8,128)(2,1)} fusion(bf16[1,64,8192]{2,1,0:T(8,128)(2,1)S(1)} %bitcast.71, bf16[1,64,8192]{2,1,0:T(8,128)(2,1)S(1)} %maximum_bitcast_fusion, bf16[1,64,8192]{2,1,0:T(8,128)(2,1)S(1)} %bitcast.72, bf16[1,64,8192]{2,1,0:T(8,128)(2,1)S(1)} %bitcast.67), kind=kLoop, calls=%fused_computation.5 | loop fusion | flops 6291456 | bytes 8388608 | tf_op jit(solution)/shard_map/stack | solution.py:130
  69.6 0.7 collective-permute-done.17
  70.4 2.2 %pad_maximum_fusion.2 = bf16[4,64,8192]{2,1,0:T(8,128)(2,1)} fusion(bf16[1,64,8192]{2,1,0:T(8,128)(2,1)S(1)} %bitcast.73, bf16[1,64,8192]{2,1,0:T(8,128)(2,1)S(1)} %maximum_bitcast_fusion.1, bf16[1,64,8192]{2,1,0:T(8,128)(2,1)S(1)} %bitcast.74, bf16[1,64,8192]{2,1,0:T(8,128)(2,1)S(1)} %bitcast.70), kind=kLoop, calls=%fused_computation.6 | loop fusion | flops 6291456 | bytes 8388608 | tf_op jit(solution)/shard_map/stack | solution.py:130
  72.6 7.7 %pad_maximum_fusion = bf16[512,8192]{1,0:T(8,128)(2,1)} fusion(bf16[256,8192]{1,0:T(8,128)(2,1)} %bitcast.63, bf16[256,8192]{1,0:T(8,128)(2,1)} %bitcast.61), kind=kLoop, calls=%fused_computation.4 | loop fusion | flops 16777216 | bytes 16777216 | tf_op jit(solution)/shard_map/concatenate | solution.py:165
  80.3 3.9 %collective-permute-start.19 = (bf16[512,8192]{1,0:T(8,128)(2,1)}, bf16[512,8192]{1,0:T(8,128)(2,1)}, u32[]{:S(2)}, u32[]{:S(2)}) collective-permute-start(bf16[512,8192]{1,0:T(8,128)(2,1)} %pad_maximum_fusion), channel_id=1, source_target_pairs={{0,1},{1,0},{2,3},{3,2},{4,5},{5,4},{6,7},{7,6},{8,9},{9,8},{10,11... | collective-permute-start | bytes 25165832 | tf_op jit(solution)/shard_map/ppermute | solution.py:169
  84.5 15.8 %convolution_bitcast_fusion.1.scores_ref = f32[1024,512]{1,0:T(8,128)} fusion(bf16[1024,8192]{1,0:T(8,128)(2,1)} %param.7, bf16[256,8192]{1,0:T(8,128)(2,1)} %bitcast.64, bf16[256,8192]{1,0:T(8,128)(2,1)} %bitcast.62), kind=kOutput, calls=%fused_computation.8 | convolution fusion | flops 8606711808 | bytes 27262976 | tf_op jit(solution)/shard_map/dot_general | solution.py:171
  100.3 3.0 %shard_map.46 = f32[16,512]{1,0:T(8,128)} custom-call(f32[1024,512]{1,0:T(8,128)} %convolution_bitcast_fusion.1.scores_ref), custom_call_target="tpu_custom_call" | custom-call | flops 16777216 | bytes 2097152 | tf_op jit(solution)/shard_map/pallas_call | solution.py:107
  103.3 15.8 %convolution_bitcast_fusion.scores_ref = f32[1024,512]{1,0:T(8,128)} fusion(bf16[512,8192]{1,0:T(8,128)(2,1)} %collective-permute-done.19, bf16[1024,8192]{1,0:T(8,128)(2,1)} %param.7), kind=kOutput, calls=%fused_computation.7 | convolution fusion | flops 8589934592 | bytes 27262976 | tf_op jit(solution)/shard_map/dot_general | solution.py:176
  119.1 3.0 %shard_map.47 = f32[16,512]{1,0:T(8,128)} custom-call(f32[1024,512]{1,0:T(8,128)} %convolution_bitcast_fusion.scores_ref), custom_call_target="tpu_custom_call" | custom-call | flops 16777216 | bytes 2097152 | tf_op jit(solution)/shard_map/pallas_call | solution.py:107
  122.1 0.8 maximum_bitcast_fusion.4
  122.9 0.2 copy.30
  123.1 2.8 %gather_fusion = f32[1024,16]{1,0:T(8,128)S(1)} fusion(f32[1024,16]{1,0:T(8,128)S(1)} %copy.30, s32[1024]{0:T(1024)S(1)} %get-tuple-element.43), kind=kCustom, calls=%fused_computation | custom fusion | bytes 135168 | tf_op jit(solution)/shard_map/jit(_take)/gather | solution.py:195
  125.9 0.2 bitcast_select_fusion
  126.1 0.2 reshape.573
  126.4 16.8 %all_to_all.5 = f32[128,1,128]{2,1,0:T(1,128)S(1)} all-to-all(f32[128,1,128]{2,1,0:T(1,128)S(1)} %reshape.573), channel_id=1, replica_groups=mesh['mass'=4,'x'=4,'z'=4,'core'=2] {'mass','x','z','core'}, dimensions={0} | all-to-all | bytes 131072 | tf_op jit(solution)/shard_map/all_to_all | solution.py:196
  143.2 0.5 broadcast.1066
  143.7 0.8 reduce
  144.7 0.2 copy.35
  144.9 0.2 copy.32
  145.2 0.3 reshape.481
  145.4 0.6 gather_fusion.1
  146.1 2.5 %sort_prefixfusion = f32[16,16]{1,0:T(8,128)} fusion(f32[16,512]{1,0:T(8,128)S(1)} %broadcast_select_fusion), kind=kCustom, calls=%top_k.9.sort_prefix | custom fusion | flops 106496 | bytes 33792 | tf_op jit(solution)/shard_map/top_k | solution.py:202
  (76 shorter events, 5.1 us)
Async XLA Ops:
  5.2 1.0 copy-start
  5.3 1.3 copy-start.2
  7.2 6.7 %collective-permute-start = (bf16[8,8192]{1,0:T(8,128)(2,1)S(1)}, bf16[8,8192]{1,0:T(8,128)(2,1)S(1)}, u32[]{:S(2)}, u32[]{:S(2)}) collective-permute-start(bf16[8,8192]{1,0:T(8,128)(2,1)S(1)} %get-tuple-element.26), channel_id=1, source_target_pairs={{0,32},{32,64},{64,96},{96,0},{1,33},{33,65},{65,97},{97,1},{2,34}... | collective-permute-start | bytes 393224 | tf_op jit(solution)/shard_map/ppermute | solution.py:155
  9.4 8.3 %collective-permute-start.9 = (bf16[8,8192]{1,0:T(8,128)(2,1)S(1)}, bf16[8,8192]{1,0:T(8,128)(2,1)S(1)}, u32[]{:S(2)}, u32[]{:S(2)}) collective-permute-start(bf16[8,8192]{1,0:T(8,128)(2,1)S(1)} %get-tuple-element.25), channel_id=1, source_target_pairs={{0,64},{32,96},{64,0},{96,32},{1,65},{33,97},{65,1},{97,33},{2,66}... | collective-permute-start | bytes 393224 | tf_op jit(solution)/shard_map/ppermute | solution.py:155
  12.0 5.7 %collective-permute-start.10 = (bf16[8,8192]{1,0:T(8,128)(2,1)S(1)}, bf16[8,8192]{1,0:T(8,128)(2,1)S(1)}, u32[]{:S(2)}, u32[]{:S(2)}) collective-permute-start(bf16[8,8192]{1,0:T(8,128)(2,1)S(1)} %get-tuple-element.24), channel_id=1, source_target_pairs={{0,96},{32,0},{64,32},{96,64},{1,97},{33,1},{65,33},{97,65},{2,98}... | collective-permute-start | bytes 393224 | tf_op jit(solution)/shard_map/ppermute | solution.py:155
  13.9 7.8 %collective-permute-start.2 = (bf16[16,8192]{1,0:T(8,128)(2,1)S(1)}, bf16[16,8192]{1,0:T(8,128)(2,1)S(1)}, u32[]{:S(2)}, u32[]{:S(2)}) collective-permute-start(bf16[16,8192]{1,0:T(8,128)(2,1)S(1)} %get-tuple-element.28), channel_id=1, source_target_pairs={{0,8},{8,16},{16,24},{24,0},{1,9},{9,17},{17,25},{25,1},{2,10},{10... | collective-permute-start | bytes 786440 | tf_op jit(solution)/shard_map/ppermute | solution.py:125
  15.1 7.9 %collective-permute-start.1 = (bf16[16,8192]{1,0:T(8,128)(2,1)S(1)}, bf16[16,8192]{1,0:T(8,128)(2,1)S(1)}, u32[]{:S(2)}, u32[]{:S(2)}) collective-permute-start(bf16[16,8192]{1,0:T(8,128)(2,1)S(1)} %get-tuple-element.28), channel_id=1, source_target_pairs={{0,24},{8,0},{16,8},{24,16},{1,25},{9,1},{17,9},{25,17},{2,26},{10... | collective-permute-start | bytes 786440 | tf_op jit(solution)/shard_map/ppermute | solution.py:126
  17.8 9.0 %collective-permute-start.12 = (bf16[16,8192]{1,0:T(8,128)(2,1)S(1)}, bf16[16,8192]{1,0:T(8,128)(2,1)S(1)}, u32[]{:S(2)}, u32[]{:S(2)}) collective-permute-start(bf16[16,8192]{1,0:T(8,128)(2,1)S(1)} %constant_dynamic-update-slice_fusion), channel_id=1, source_target_pairs={{0,2},{2,4},{4,6},{6,0},{1,3},{3,5},{5,7},{7,1},{8,10},{10,12},{12... | collective-permute-start | bytes 786440 | tf_op jit(solution)/shard_map/ppermute | solution.py:125
  19.5 7.4 %collective-permute-start.11 = (bf16[16,8192]{1,0:T(8,128)(2,1)S(1)}, bf16[16,8192]{1,0:T(8,128)(2,1)S(1)}, u32[]{:S(2)}, u32[]{:S(2)}) collective-permute-start(bf16[16,8192]{1,0:T(8,128)(2,1)S(1)} %constant_dynamic-update-slice_fusion), channel_id=1, source_target_pairs={{0,6},{2,0},{4,2},{6,4},{1,7},{3,1},{5,3},{7,5},{8,14},{10,8},{12,... | collective-permute-start | bytes 786440 | tf_op jit(solution)/shard_map/ppermute | solution.py:126
  21.7 7.8 %collective-permute-start.3 = (bf16[8,8192]{1,0:T(8,128)(2,1)S(1)}, bf16[8,8192]{1,0:T(8,128)(2,1)S(1)}, u32[]{:S(2)}, u32[]{:S(2)}) collective-permute-start(bf16[8,8192]{1,0:T(8,128)(2,1)S(1)} %slice.120), channel_id=1, source_target_pairs={{0,8},{8,16},{16,24},{24,0},{1,9},{9,17},{17,25},{25,1},{2,10},{10... | collective-permute-start | bytes 393224 | tf_op jit(solution)/shard_map/ppermute | solution.py:127
  23.0 6.6 %collective-permute-start.4 = (bf16[8,8192]{1,0:T(8,128)(2,1)S(1)}, bf16[8,8192]{1,0:T(8,128)(2,1)S(1)}, u32[]{:S(2)}, u32[]{:S(2)}) collective-permute-start(bf16[8,8192]{1,0:T(8,128)(2,1)S(1)} %slice.121), channel_id=1, source_target_pairs={{0,24},{8,0},{16,8},{24,16},{1,25},{9,1},{17,9},{25,17},{2,26},{10... | collective-permute-start | bytes 393224 | tf_op jit(solution)/shard_map/ppermute | solution.py:128
  26.7 5.8 %collective-permute-start.13 = (bf16[8,8192]{1,0:T(8,128)(2,1)S(1)}, bf16[8,8192]{1,0:T(8,128)(2,1)S(1)}, u32[]{:S(2)}, u32[]{:S(2)}) collective-permute-start(bf16[8,8192]{1,0:T(8,128)(2,1)S(1)} %slice.124), channel_id=1, source_target_pairs={{0,2},{2,4},{4,6},{6,0},{1,3},{3,5},{5,7},{7,1},{8,10},{10,12},{12... | collective-permute-start | bytes 393224 | tf_op jit(solution)/shard_map/ppermute | solution.py:127
  26.8 5.6 %collective-permute-start.14 = (bf16[8,8192]{1,0:T(8,128)(2,1)S(1)}, bf16[8,8192]{1,0:T(8,128)(2,1)S(1)}, u32[]{:S(2)}, u32[]{:S(2)}) collective-permute-start(bf16[8,8192]{1,0:T(8,128)(2,1)S(1)} %slice.125), channel_id=1, source_target_pairs={{0,6},{2,0},{4,2},{6,4},{1,7},{3,1},{5,3},{7,5},{8,14},{10,8},{12,... | collective-permute-start | bytes 393224 | tf_op jit(solution)/shard_map/ppermute | solution.py:128
  29.7 25.3 %collective-permute-start.6 = (bf16[64,8192]{1,0:T(8,128)(2,1)S(1)}, bf16[64,8192]{1,0:T(8,128)(2,1)S(1)}, u32[]{:S(2)}, u32[]{:S(2)}) collective-permute-start(bf16[64,8192]{1,0:T(8,128)(2,1)S(1)} %bitcast.65), channel_id=1, source_target_pairs={{0,2},{2,4},{4,6},{6,0},{1,3},{3,5},{5,7},{7,1},{8,10},{10,12},{12... | collective-permute-start | bytes 3145736 | tf_op jit(solution)/shard_map/ppermute | solution.py:125
  29.8 25.3 %collective-permute-start.5 = (bf16[64,8192]{1,0:T(8,128)(2,1)S(1)}, bf16[64,8192]{1,0:T(8,128)(2,1)S(1)}, u32[]{:S(2)}, u32[]{:S(2)}) collective-permute-start(bf16[64,8192]{1,0:T(8,128)(2,1)S(1)} %bitcast.66), channel_id=1, source_target_pairs={{0,6},{2,0},{4,2},{6,4},{1,7},{3,1},{5,3},{7,5},{8,14},{10,8},{12,... | collective-permute-start | bytes 3145736 | tf_op jit(solution)/shard_map/ppermute | solution.py:126
  32.7 25.6 %collective-permute-start.16 = (bf16[64,8192]{1,0:T(8,128)(2,1)S(1)}, bf16[64,8192]{1,0:T(8,128)(2,1)S(1)}, u32[]{:S(2)}, u32[]{:S(2)}) collective-permute-start(bf16[64,8192]{1,0:T(8,128)(2,1)S(1)} %bitcast.68), channel_id=1, source_target_pairs={{0,8},{8,16},{16,24},{24,0},{1,9},{9,17},{17,25},{25,1},{2,10},{10... | collective-permute-start | bytes 3145736 | tf_op jit(solution)/shard_map/ppermute | solution.py:125
  33.9 25.6 %collective-permute-start.15 = (bf16[64,8192]{1,0:T(8,128)(2,1)S(1)}, bf16[64,8192]{1,0:T(8,128)(2,1)S(1)}, u32[]{:S(2)}, u32[]{:S(2)}) collective-permute-start(bf16[64,8192]{1,0:T(8,128)(2,1)S(1)} %bitcast.69), channel_id=1, source_target_pairs={{0,24},{8,0},{16,8},{24,16},{1,25},{9,1},{17,9},{25,17},{2,26},{10... | collective-permute-start | bytes 3145736 | tf_op jit(solution)/shard_map/ppermute | solution.py:126
  55.0 12.2 %collective-permute-start.7 = (bf16[32,8192]{1,0:T(8,128)(2,1)S(1)}, bf16[32,8192]{1,0:T(8,128)(2,1)S(1)}, u32[]{:S(2)}, u32[]{:S(2)}) collective-permute-start(bf16[32,8192]{1,0:T(8,128)(2,1)S(1)} %slice.122), channel_id=1, source_target_pairs={{0,2},{2,4},{4,6},{6,0},{1,3},{3,5},{5,7},{7,1},{8,10},{10,12},{12... | collective-permute-start | bytes 1572872 | tf_op jit(solution)/shard_map/ppermute | solution.py:127
  55.2 12.1 %collective-permute-start.8 = (bf16[32,8192]{1,0:T(8,128)(2,1)S(1)}, bf16[32,8192]{1,0:T(8,128)(2,1)S(1)}, u32[]{:S(2)}, u32[]{:S(2)}) collective-permute-start(bf16[32,8192]{1,0:T(8,128)(2,1)S(1)} %slice.123), channel_id=1, source_target_pairs={{0,6},{2,0},{4,2},{6,4},{1,7},{3,1},{5,3},{7,5},{8,14},{10,8},{12,... | collective-permute-start | bytes 1572872 | tf_op jit(solution)/shard_map/ppermute | solution.py:128
  58.3 12.0 %collective-permute-start.17 = (bf16[32,8192]{1,0:T(8,128)(2,1)S(1)}, bf16[32,8192]{1,0:T(8,128)(2,1)S(1)}, u32[]{:S(2)}, u32[]{:S(2)}) collective-permute-start(bf16[32,8192]{1,0:T(8,128)(2,1)S(1)} %slice.126), channel_id=1, source_target_pairs={{0,8},{8,16},{16,24},{24,0},{1,9},{9,17},{17,25},{25,1},{2,10},{10... | collective-permute-start | bytes 1572872 | tf_op jit(solution)/shard_map/ppermute | solution.py:127
  59.6 10.7 %collective-permute-start.18 = (bf16[32,8192]{1,0:T(8,128)(2,1)S(1)}, bf16[32,8192]{1,0:T(8,128)(2,1)S(1)}, u32[]{:S(2)}, u32[]{:S(2)}) collective-permute-start(bf16[32,8192]{1,0:T(8,128)(2,1)S(1)} %slice.127), channel_id=1, source_target_pairs={{0,24},{8,0},{16,8},{24,16},{1,25},{9,1},{17,9},{25,17},{2,26},{10... | collective-permute-start | bytes 1572872 | tf_op jit(solution)/shard_map/ppermute | solution.py:128
  80.3 23.1 %collective-permute-start.19 = (bf16[512,8192]{1,0:T(8,128)(2,1)}, bf16[512,8192]{1,0:T(8,128)(2,1)}, u32[]{:S(2)}, u32[]{:S(2)}) collective-permute-start(bf16[512,8192]{1,0:T(8,128)(2,1)} %pad_maximum_fusion), channel_id=1, source_target_pairs={{0,1},{1,0},{2,3},{3,2},{4,5},{5,4},{6,7},{7,6},{8,9},{9,8},{10,11... | collective-permute-start | bytes 25165832 | tf_op jit(solution)/shard_map/ppermute | solution.py:169
  103.3 18.8 %copy-start.1 = (f32[16,512]{1,0:T(8,128)S(1)}, f32[16,512]{1,0:T(8,128)}, u32[]{:S(2)}) copy-start(f32[16,512]{1,0:T(8,128)} %shard_map.46) | copy-start | bytes 98308

commit v13 on v12

--- a/solution.py
+++ b/solution.py
@@ -103,7 +103,7 @@
 
 def column_topk(scores):
     rows, columns = scores.shape
-    width = 2 * LANES if columns % (2 * LANES) == 0 else LANES
+    width = 4 * LANES if columns % (4 * LANES) == 0 else LANES
     return pl.pallas_call(
         column_topk_kernel,
         out_shape=jax.ShapeDtypeStruct((TOP_K, columns), jnp.float32),

time: 149 us -> 150 us (level)
  no operation moved by 1% of the time
where the time goes in v13:
time: 150 us; the launch traced here: 149 us
  starting transfers between devices  33.3 us (22%)
  matrix products  32 us (21%)
  waiting for transfers between devices  30.5 us (20%)
  other arithmetic  22.3 us (15%)
  blocking collectives  17 us (11%)
  local copies, waits for them, and re-layouts  7.05 us (5%)
  Pallas kernels  6.73 us (4%)
    ppermute x4, waiting for transfers between devices, ring_gather(): from_minus = lax.ppermute(flat, axis, forward)  21.8 us
    all_to_all x1, blocking collectives, per_device(): lax.all_to_all(outgoing, ('mass', 'x', 'z', 'core'), split_axis=0, concat...  17 us
    dot_general x1, matrix products, per_device(): lax.dot_general(library, own_side, (((1,), (1,)), ((), ())), preferred_el...  15.8 us
    dot_general x1, matrix products, per_device(): lax.dot_general(library, other_side, (((1,), (1,)), ((), ())), preferred_...  15.8 us
    ppermute x4, starting transfers between devices, ring_gather(): far_second = lax.ppermute(from_plus[half:], axis, backward)  8.91 us
    ppermute x4, starting transfers between devices, ring_gather(): from_plus = lax.ppermute(flat, axis, backward)  7.9 us
    concatenate x1, other arithmetic, per_device(): jnp.concatenate([part_a.reshape(-1, arrived.shape[1]), part_b.reshape(-1,...  7.67 us
    ppermute x4, waiting for transfers between devices, ring_gather(): far_first = lax.ppermute(from_minus[:half], axis, forward)  6.8 us
  transfers between devices with their start and end apart: 20, of which 7 were waited for; matrix products, arithmetic and copies ran while one was open for 13% of the time, Pallas kernels for 2%

profile of v13, /device:TPU:1, one launch (start us, length us, event | category | flops | bytes accessed | tf_op | source)
XLA Modules:
  0.0 149.3 jit_solution(5760227754081122500)
XLA Ops:
  0.0 0.7 and_compare_fusion.12
  0.7 1.0 pad_maximum_fusion.5
  1.8 1.1 pad_select_fusion.11
  6.2 0.4 multiply_reduce_fusion
  6.7 0.4 fusion
  7.2 2.2 %collective-permute-start = (bf16[8,8192]{1,0:T(8,128)(2,1)S(1)}, bf16[8,8192]{1,0:T(8,128)(2,1)S(1)}, u32[]{:S(2)}, u32[]{:S(2)}) collective-permute-start(bf16[8,8192]{1,0:T(8,128)(2,1)S(1)} %get-tuple-element.26), channel_id=1, source_target_pairs={{0,32},{32,64},{64,96},{96,0},{1,33},{33,65},{65,97},{97,1},{2,34}... | collective-permute-start | bytes 393224 | tf_op jit(solution)/shard_map/ppermute | solution.py:155
  9.4 2.6 %collective-permute-start.9 = (bf16[8,8192]{1,0:T(8,128)(2,1)S(1)}, bf16[8,8192]{1,0:T(8,128)(2,1)S(1)}, u32[]{:S(2)}, u32[]{:S(2)}) collective-permute-start(bf16[8,8192]{1,0:T(8,128)(2,1)S(1)} %get-tuple-element.25), channel_id=1, source_target_pairs={{0,64},{32,96},{64,0},{96,32},{1,65},{33,97},{65,1},{97,33},{2,66}... | collective-permute-start | bytes 393224 | tf_op jit(solution)/shard_map/ppermute | solution.py:155
  12.0 1.1 collective-permute-start.10
  13.1 0.8 collective-permute-done
  13.9 1.2 collective-permute-start.2
  15.1 1.6 %collective-permute-start.1 = (bf16[16,8192]{1,0:T(8,128)(2,1)S(1)}, bf16[16,8192]{1,0:T(8,128)(2,1)S(1)}, u32[]{:S(2)}, u32[]{:S(2)}) collective-permute-start(bf16[16,8192]{1,0:T(8,128)(2,1)S(1)} %get-tuple-element.28), channel_id=1, source_target_pairs={{0,24},{8,0},{16,8},{24,16},{1,25},{9,1},{17,9},{25,17},{2,26},{10... | collective-permute-start | bytes 786440 | tf_op jit(solution)/shard_map/ppermute | solution.py:126
  16.7 1.0 collective-permute-done.9
  17.8 1.7 %collective-permute-start.12 = (bf16[16,8192]{1,0:T(8,128)(2,1)S(1)}, bf16[16,8192]{1,0:T(8,128)(2,1)S(1)}, u32[]{:S(2)}, u32[]{:S(2)}) collective-permute-start(bf16[16,8192]{1,0:T(8,128)(2,1)S(1)} %constant_dynamic-update-slice_fusion), channel_id=1, source_target_pairs={{0,2},{2,4},{4,6},{6,0},{1,3},{3,5},{5,7},{7,1},{8,10},{10,12},{12... | collective-permute-start | bytes 786440 | tf_op jit(solution)/shard_map/ppermute | solution.py:125
  19.5 2.2 %collective-permute-start.11 = (bf16[16,8192]{1,0:T(8,128)(2,1)S(1)}, bf16[16,8192]{1,0:T(8,128)(2,1)S(1)}, u32[]{:S(2)}, u32[]{:S(2)}) collective-permute-start(bf16[16,8192]{1,0:T(8,128)(2,1)S(1)} %constant_dynamic-update-slice_fusion), channel_id=1, source_target_pairs={{0,6},{2,0},{4,2},{6,4},{1,7},{3,1},{5,3},{7,5},{8,14},{10,8},{12,... | collective-permute-start | bytes 786440 | tf_op jit(solution)/shard_map/ppermute | solution.py:126
  21.7 1.2 collective-permute-start.3
  23.0 1.6 %collective-permute-start.4 = (bf16[8,8192]{1,0:T(8,128)(2,1)S(1)}, bf16[8,8192]{1,0:T(8,128)(2,1)S(1)}, u32[]{:S(2)}, u32[]{:S(2)}) collective-permute-start(bf16[8,8192]{1,0:T(8,128)(2,1)S(1)} %slice.121), channel_id=1, source_target_pairs={{0,24},{8,0},{16,8},{24,16},{1,25},{9,1},{17,9},{25,17},{2,26},{10... | collective-permute-start | bytes 393224 | tf_op jit(solution)/shard_map/ppermute | solution.py:128
  24.6 2.1 %collective-permute-done.12 = bf16[16,8192]{1,0:T(8,128)(2,1)S(1)} collective-permute-done((bf16[16,8192]{1,0:T(8,128)(2,1)S(1)}, bf16[16,8192]{1,0:T(8,128)(2,1)S(1)}, u32[]{:S(2)}, u32[]{:S(2)}) %collective-permute-start.12) | collective-permute-done | bytes 262176 | tf_op jit(solution)/shard_map/ppermute | solution.py:125
  26.8 2.7 %collective-permute-start.14 = (bf16[8,8192]{1,0:T(8,128)(2,1)S(1)}, bf16[8,8192]{1,0:T(8,128)(2,1)S(1)}, u32[]{:S(2)}, u32[]{:S(2)}) collective-permute-start(bf16[8,8192]{1,0:T(8,128)(2,1)S(1)} %slice.125), channel_id=1, source_target_pairs={{0,6},{2,0},{4,2},{6,4},{1,7},{3,1},{5,3},{7,5},{8,14},{10,8},{12,... | collective-permute-start | bytes 393224 | tf_op jit(solution)/shard_map/ppermute | solution.py:128
  29.8 2.7 %collective-permute-start.5 = (bf16[64,8192]{1,0:T(8,128)(2,1)S(1)}, bf16[64,8192]{1,0:T(8,128)(2,1)S(1)}, u32[]{:S(2)}, u32[]{:S(2)}) collective-permute-start(bf16[64,8192]{1,0:T(8,128)(2,1)S(1)} %bitcast.66), channel_id=1, source_target_pairs={{0,6},{2,0},{4,2},{6,4},{1,7},{3,1},{5,3},{7,5},{8,14},{10,8},{12,... | collective-permute-start | bytes 3145736 | tf_op jit(solution)/shard_map/ppermute | solution.py:126
  32.7 1.3 collective-permute-start.16
  33.9 1.5 collective-permute-start.15
  35.4 19.6 %collective-permute-done.6 = bf16[64,8192]{1,0:T(8,128)(2,1)S(1)} collective-permute-done((bf16[64,8192]{1,0:T(8,128)(2,1)S(1)}, bf16[64,8192]{1,0:T(8,128)(2,1)S(1)}, u32[]{:S(2)}, u32[]{:S(2)}) %collective-permute-start.6) | collective-permute-done | bytes 1048608 | tf_op jit(solution)/shard_map/ppermute | solution.py:125
  55.2 3.1 %collective-permute-start.8 = (bf16[32,8192]{1,0:T(8,128)(2,1)S(1)}, bf16[32,8192]{1,0:T(8,128)(2,1)S(1)}, u32[]{:S(2)}, u32[]{:S(2)}) collective-permute-start(bf16[32,8192]{1,0:T(8,128)(2,1)S(1)} %slice.123), channel_id=1, source_target_pairs={{0,6},{2,0},{4,2},{6,4},{1,7},{3,1},{5,3},{7,5},{8,14},{10,8},{12,... | collective-permute-start | bytes 1572872 | tf_op jit(solution)/shard_map/ppermute | solution.py:128
  58.3 1.3 collective-permute-start.17
  59.6 1.5 %collective-permute-start.18 = (bf16[32,8192]{1,0:T(8,128)(2,1)S(1)}, bf16[32,8192]{1,0:T(8,128)(2,1)S(1)}, u32[]{:S(2)}, u32[]{:S(2)}) collective-permute-start(bf16[32,8192]{1,0:T(8,128)(2,1)S(1)} %slice.127), channel_id=1, source_target_pairs={{0,24},{8,0},{16,8},{24,16},{1,25},{9,1},{17,9},{25,17},{2,26},{10... | collective-permute-start | bytes 1572872 | tf_op jit(solution)/shard_map/ppermute | solution.py:128
  61.1 6.1 %collective-permute-done.7 = bf16[32,8192]{1,0:T(8,128)(2,1)S(1)} collective-permute-done((bf16[32,8192]{1,0:T(8,128)(2,1)S(1)}, bf16[32,8192]{1,0:T(8,128)(2,1)S(1)}, u32[]{:S(2)}, u32[]{:S(2)}) %collective-permute-start.7) | collective-permute-done | bytes 524320 | tf_op jit(solution)/shard_map/ppermute | solution.py:127
  67.3 2.3 %pad_maximum_fusion.1 = bf16[4,64,8192]{2,1,0:T(8,128)(2,1)} fusion(bf16[1,64,8192]{2,1,0:T(8,128)(2,1)S(1)} %bitcast.71, bf16[1,64,8192]{2,1,0:T(8,128)(2,1)S(1)} %maximum_bitcast_fusion, bf16[1,64,8192]{2,1,0:T(8,128)(2,1)S(1)} %bitcast.72, bf16[1,64,8192]{2,1,0:T(8,128)(2,1)S(1)} %bitcast.67), kind=kLoop, calls=%fused_computation.5 | loop fusion | flops 6291456 | bytes 8388608 | tf_op jit(solution)/shard_map/stack | solution.py:130
  69.6 0.7 collective-permute-done.17
  70.3 2.2 %pad_maximum_fusion.2 = bf16[4,64,8192]{2,1,0:T(8,128)(2,1)} fusion(bf16[1,64,8192]{2,1,0:T(8,128)(2,1)S(1)} %bitcast.73, bf16[1,64,8192]{2,1,0:T(8,128)(2,1)S(1)} %maximum_bitcast_fusion.1, bf16[1,64,8192]{2,1,0:T(8,128)(2,1)S(1)} %bitcast.74, bf16[1,64,8192]{2,1,0:T(8,128)(2,1)S(1)} %bitcast.70), kind=kLoop, calls=%fused_computation.6 | loop fusion | flops 6291456 | bytes 8388608 | tf_op jit(solution)/shard_map/stack | solution.py:130
  72.6 7.7 %pad_maximum_fusion = bf16[512,8192]{1,0:T(8,128)(2,1)} fusion(bf16[256,8192]{1,0:T(8,128)(2,1)} %bitcast.63, bf16[256,8192]{1,0:T(8,128)(2,1)} %bitcast.61), kind=kLoop, calls=%fused_computation.4 | loop fusion | flops 16777216 | bytes 16777216 | tf_op jit(solution)/shard_map/concatenate | solution.py:165
  80.3 3.7 %collective-permute-start.19 = (bf16[512,8192]{1,0:T(8,128)(2,1)}, bf16[512,8192]{1,0:T(8,128)(2,1)}, u32[]{:S(2)}, u32[]{:S(2)}) collective-permute-start(bf16[512,8192]{1,0:T(8,128)(2,1)} %pad_maximum_fusion), channel_id=1, source_target_pairs={{0,1},{1,0},{2,3},{3,2},{4,5},{5,4},{6,7},{7,6},{8,9},{9,8},{10,11... | collective-permute-start | bytes 25165832 | tf_op jit(solution)/shard_map/ppermute | solution.py:169
  84.3 15.8 %convolution_bitcast_fusion.1.scores_ref = f32[1024,512]{1,0:T(8,128)} fusion(bf16[1024,8192]{1,0:T(8,128)(2,1)} %param.7, bf16[256,8192]{1,0:T(8,128)(2,1)} %bitcast.64, bf16[256,8192]{1,0:T(8,128)(2,1)} %bitcast.62), kind=kOutput, calls=%fused_computation.8 | convolution fusion | flops 8606711808 | bytes 27262976 | tf_op jit(solution)/shard_map/dot_general | solution.py:171
  100.1 3.4 %shard_map.46 = f32[16,512]{1,0:T(8,128)} custom-call(f32[1024,512]{1,0:T(8,128)} %convolution_bitcast_fusion.1.scores_ref), custom_call_target="tpu_custom_call" | custom-call | flops 16777216 | bytes 2097152 | tf_op jit(solution)/shard_map/pallas_call | solution.py:107
  103.5 15.8 %convolution_bitcast_fusion.scores_ref = f32[1024,512]{1,0:T(8,128)} fusion(bf16[512,8192]{1,0:T(8,128)(2,1)} %collective-permute-done.19, bf16[1024,8192]{1,0:T(8,128)(2,1)} %param.7), kind=kOutput, calls=%fused_computation.7 | convolution fusion | flops 8589934592 | bytes 27262976 | tf_op jit(solution)/shard_map/dot_general | solution.py:176
  119.3 3.4 %shard_map.47 = f32[16,512]{1,0:T(8,128)} custom-call(f32[1024,512]{1,0:T(8,128)} %convolution_bitcast_fusion.scores_ref), custom_call_target="tpu_custom_call" | custom-call | flops 16777216 | bytes 2097152 | tf_op jit(solution)/shard_map/pallas_call | solution.py:107
  122.7 0.8 maximum_bitcast_fusion.4
  123.4 0.2 copy.30
  123.6 2.8 %gather_fusion = f32[1024,16]{1,0:T(8,128)S(1)} fusion(f32[1024,16]{1,0:T(8,128)S(1)} %copy.30, s32[1024]{0:T(1024)S(1)} %get-tuple-element.43), kind=kCustom, calls=%fused_computation | custom fusion | bytes 135168 | tf_op jit(solution)/shard_map/jit(_take)/gather | solution.py:195
  126.4 0.2 bitcast_select_fusion
  126.7 0.2 reshape.573
  126.9 17.0 %all_to_all.5 = f32[128,1,128]{2,1,0:T(1,128)S(1)} all-to-all(f32[128,1,128]{2,1,0:T(1,128)S(1)} %reshape.573), channel_id=1, replica_groups=mesh['mass'=4,'x'=4,'z'=4,'core'=2] {'mass','x','z','core'}, dimensions={0} | all-to-all | bytes 131072 | tf_op jit(solution)/shard_map/all_to_all | solution.py:196
  143.9 0.5 broadcast.1066
  144.4 0.8 reduce
  145.4 0.2 copy.35
  145.6 0.2 copy.32
  145.9 0.3 reshape.481
  146.2 0.6 gather_fusion.1
  146.8 2.5 %sort_prefixfusion = f32[16,16]{1,0:T(8,128)} fusion(f32[16,512]{1,0:T(8,128)S(1)} %broadcast_select_fusion), kind=kCustom, calls=%top_k.9.sort_prefix | custom fusion | flops 106496 | bytes 33792 | tf_op jit(solution)/shard_map/top_k | solution.py:202
  (76 shorter events, 5.1 us)
Async XLA Ops:
  5.2 1.0 copy-start
  5.3 1.3 copy-start.2
  7.2 6.7 %collective-permute-start = (bf16[8,8192]{1,0:T(8,128)(2,1)S(1)}, bf16[8,8192]{1,0:T(8,128)(2,1)S(1)}, u32[]{:S(2)}, u32[]{:S(2)}) collective-permute-start(bf16[8,8192]{1,0:T(8,128)(2,1)S(1)} %get-tuple-element.26), channel_id=1, source_target_pairs={{0,32},{32,64},{64,96},{96,0},{1,33},{33,65},{65,97},{97,1},{2,34}... | collective-permute-start | bytes 393224 | tf_op jit(solution)/shard_map/ppermute | solution.py:155
  9.4 8.3 %collective-permute-start.9 = (bf16[8,8192]{1,0:T(8,128)(2,1)S(1)}, bf16[8,8192]{1,0:T(8,128)(2,1)S(1)}, u32[]{:S(2)}, u32[]{:S(2)}) collective-permute-start(bf16[8,8192]{1,0:T(8,128)(2,1)S(1)} %get-tuple-element.25), channel_id=1, source_target_pairs={{0,64},{32,96},{64,0},{96,32},{1,65},{33,97},{65,1},{97,33},{2,66}... | collective-permute-start | bytes 393224 | tf_op jit(solution)/shard_map/ppermute | solution.py:155
  12.0 5.7 %collective-permute-start.10 = (bf16[8,8192]{1,0:T(8,128)(2,1)S(1)}, bf16[8,8192]{1,0:T(8,128)(2,1)S(1)}, u32[]{:S(2)}, u32[]{:S(2)}) collective-permute-start(bf16[8,8192]{1,0:T(8,128)(2,1)S(1)} %get-tuple-element.24), channel_id=1, source_target_pairs={{0,96},{32,0},{64,32},{96,64},{1,97},{33,1},{65,33},{97,65},{2,98}... | collective-permute-start | bytes 393224 | tf_op jit(solution)/shard_map/ppermute | solution.py:155
  13.9 7.8 %collective-permute-start.2 = (bf16[16,8192]{1,0:T(8,128)(2,1)S(1)}, bf16[16,8192]{1,0:T(8,128)(2,1)S(1)}, u32[]{:S(2)}, u32[]{:S(2)}) collective-permute-start(bf16[16,8192]{1,0:T(8,128)(2,1)S(1)} %get-tuple-element.28), channel_id=1, source_target_pairs={{0,8},{8,16},{16,24},{24,0},{1,9},{9,17},{17,25},{25,1},{2,10},{10... | collective-permute-start | bytes 786440 | tf_op jit(solution)/shard_map/ppermute | solution.py:125
  15.1 7.9 %collective-permute-start.1 = (bf16[16,8192]{1,0:T(8,128)(2,1)S(1)}, bf16[16,8192]{1,0:T(8,128)(2,1)S(1)}, u32[]{:S(2)}, u32[]{:S(2)}) collective-permute-start(bf16[16,8192]{1,0:T(8,128)(2,1)S(1)} %get-tuple-element.28), channel_id=1, source_target_pairs={{0,24},{8,0},{16,8},{24,16},{1,25},{9,1},{17,9},{25,17},{2,26},{10... | collective-permute-start | bytes 786440 | tf_op jit(solution)/shard_map/ppermute | solution.py:126
  17.8 9.0 %collective-permute-start.12 = (bf16[16,8192]{1,0:T(8,128)(2,1)S(1)}, bf16[16,8192]{1,0:T(8,128)(2,1)S(1)}, u32[]{:S(2)}, u32[]{:S(2)}) collective-permute-start(bf16[16,8192]{1,0:T(8,128)(2,1)S(1)} %constant_dynamic-update-slice_fusion), channel_id=1, source_target_pairs={{0,2},{2,4},{4,6},{6,0},{1,3},{3,5},{5,7},{7,1},{8,10},{10,12},{12... | collective-permute-start | bytes 786440 | tf_op jit(solution)/shard_map/ppermute | solution.py:125
  19.5 7.4 %collective-permute-start.11 = (bf16[16,8192]{1,0:T(8,128)(2,1)S(1)}, bf16[16,8192]{1,0:T(8,128)(2,1)S(1)}, u32[]{:S(2)}, u32[]{:S(2)}) collective-permute-start(bf16[16,8192]{1,0:T(8,128)(2,1)S(1)} %constant_dynamic-update-slice_fusion), channel_id=1, source_target_pairs={{0,6},{2,0},{4,2},{6,4},{1,7},{3,1},{5,3},{7,5},{8,14},{10,8},{12,... | collective-permute-start | bytes 786440 | tf_op jit(solution)/shard_map/ppermute | solution.py:126
  21.7 7.8 %collective-permute-start.3 = (bf16[8,8192]{1,0:T(8,128)(2,1)S(1)}, bf16[8,8192]{1,0:T(8,128)(2,1)S(1)}, u32[]{:S(2)}, u32[]{:S(2)}) collective-permute-start(bf16[8,8192]{1,0:T(8,128)(2,1)S(1)} %slice.120), channel_id=1, source_target_pairs={{0,8},{8,16},{16,24},{24,0},{1,9},{9,17},{17,25},{25,1},{2,10},{10... | collective-permute-start | bytes 393224 | tf_op jit(solution)/shard_map/ppermute | solution.py:127
  23.0 6.6 %collective-permute-start.4 = (bf16[8,8192]{1,0:T(8,128)(2,1)S(1)}, bf16[8,8192]{1,0:T(8,128)(2,1)S(1)}, u32[]{:S(2)}, u32[]{:S(2)}) collective-permute-start(bf16[8,8192]{1,0:T(8,128)(2,1)S(1)} %slice.121), channel_id=1, source_target_pairs={{0,24},{8,0},{16,8},{24,16},{1,25},{9,1},{17,9},{25,17},{2,26},{10... | collective-permute-start | bytes 393224 | tf_op jit(solution)/shard_map/ppermute | solution.py:128
  26.7 5.8 %collective-permute-start.13 = (bf16[8,8192]{1,0:T(8,128)(2,1)S(1)}, bf16[8,8192]{1,0:T(8,128)(2,1)S(1)}, u32[]{:S(2)}, u32[]{:S(2)}) collective-permute-start(bf16[8,8192]{1,0:T(8,128)(2,1)S(1)} %slice.124), channel_id=1, source_target_pairs={{0,2},{2,4},{4,6},{6,0},{1,3},{3,5},{5,7},{7,1},{8,10},{10,12},{12... | collective-permute-start | bytes 393224 | tf_op jit(solution)/shard_map/ppermute | solution.py:127
  26.8 5.6 %collective-permute-start.14 = (bf16[8,8192]{1,0:T(8,128)(2,1)S(1)}, bf16[8,8192]{1,0:T(8,128)(2,1)S(1)}, u32[]{:S(2)}, u32[]{:S(2)}) collective-permute-start(bf16[8,8192]{1,0:T(8,128)(2,1)S(1)} %slice.125), channel_id=1, source_target_pairs={{0,6},{2,0},{4,2},{6,4},{1,7},{3,1},{5,3},{7,5},{8,14},{10,8},{12,... | collective-permute-start | bytes 393224 | tf_op jit(solution)/shard_map/ppermute | solution.py:128
  29.7 25.3 %collective-permute-start.6 = (bf16[64,8192]{1,0:T(8,128)(2,1)S(1)}, bf16[64,8192]{1,0:T(8,128)(2,1)S(1)}, u32[]{:S(2)}, u32[]{:S(2)}) collective-permute-start(bf16[64,8192]{1,0:T(8,128)(2,1)S(1)} %bitcast.65), channel_id=1, source_target_pairs={{0,2},{2,4},{4,6},{6,0},{1,3},{3,5},{5,7},{7,1},{8,10},{10,12},{12... | collective-permute-start | bytes 3145736 | tf_op jit(solution)/shard_map/ppermute | solution.py:125
  29.8 25.3 %collective-permute-start.5 = (bf16[64,8192]{1,0:T(8,128)(2,1)S(1)}, bf16[64,8192]{1,0:T(8,128)(2,1)S(1)}, u32[]{:S(2)}, u32[]{:S(2)}) collective-permute-start(bf16[64,8192]{1,0:T(8,128)(2,1)S(1)} %bitcast.66), channel_id=1, source_target_pairs={{0,6},{2,0},{4,2},{6,4},{1,7},{3,1},{5,3},{7,5},{8,14},{10,8},{12,... | collective-permute-start | bytes 3145736 | tf_op jit(solution)/shard_map/ppermute | solution.py:126
  32.7 25.6 %collective-permute-start.16 = (bf16[64,8192]{1,0:T(8,128)(2,1)S(1)}, bf16[64,8192]{1,0:T(8,128)(2,1)S(1)}, u32[]{:S(2)}, u32[]{:S(2)}) collective-permute-start(bf16[64,8192]{1,0:T(8,128)(2,1)S(1)} %bitcast.68), channel_id=1, source_target_pairs={{0,8},{8,16},{16,24},{24,0},{1,9},{9,17},{17,25},{25,1},{2,10},{10... | collective-permute-start | bytes 3145736 | tf_op jit(solution)/shard_map/ppermute | solution.py:125
  33.9 25.6 %collective-permute-start.15 = (bf16[64,8192]{1,0:T(8,128)(2,1)S(1)}, bf16[64,8192]{1,0:T(8,128)(2,1)S(1)}, u32[]{:S(2)}, u32[]{:S(2)}) collective-permute-start(bf16[64,8192]{1,0:T(8,128)(2,1)S(1)} %bitcast.69), channel_id=1, source_target_pairs={{0,24},{8,0},{16,8},{24,16},{1,25},{9,1},{17,9},{25,17},{2,26},{10... | collective-permute-start | bytes 3145736 | tf_op jit(solution)/shard_map/ppermute | solution.py:126
  55.0 12.2 %collective-permute-start.7 = (bf16[32,8192]{1,0:T(8,128)(2,1)S(1)}, bf16[32,8192]{1,0:T(8,128)(2,1)S(1)}, u32[]{:S(2)}, u32[]{:S(2)}) collective-permute-start(bf16[32,8192]{1,0:T(8,128)(2,1)S(1)} %slice.122), channel_id=1, source_target_pairs={{0,2},{2,4},{4,6},{6,0},{1,3},{3,5},{5,7},{7,1},{8,10},{10,12},{12... | collective-permute-start | bytes 1572872 | tf_op jit(solution)/shard_map/ppermute | solution.py:127
  55.2 12.1 %collective-permute-start.8 = (bf16[32,8192]{1,0:T(8,128)(2,1)S(1)}, bf16[32,8192]{1,0:T(8,128)(2,1)S(1)}, u32[]{:S(2)}, u32[]{:S(2)}) collective-permute-start(bf16[32,8192]{1,0:T(8,128)(2,1)S(1)} %slice.123), channel_id=1, source_target_pairs={{0,6},{2,0},{4,2},{6,4},{1,7},{3,1},{5,3},{7,5},{8,14},{10,8},{12,... | collective-permute-start | bytes 1572872 | tf_op jit(solution)/shard_map/ppermute | solution.py:128
  58.3 12.0 %collective-permute-start.17 = (bf16[32,8192]{1,0:T(8,128)(2,1)S(1)}, bf16[32,8192]{1,0:T(8,128)(2,1)S(1)}, u32[]{:S(2)}, u32[]{:S(2)}) collective-permute-start(bf16[32,8192]{1,0:T(8,128)(2,1)S(1)} %slice.126), channel_id=1, source_target_pairs={{0,8},{8,16},{16,24},{24,0},{1,9},{9,17},{17,25},{25,1},{2,10},{10... | collective-permute-start | bytes 1572872 | tf_op jit(solution)/shard_map/ppermute | solution.py:127
  59.6 10.7 %collective-permute-start.18 = (bf16[32,8192]{1,0:T(8,128)(2,1)S(1)}, bf16[32,8192]{1,0:T(8,128)(2,1)S(1)}, u32[]{:S(2)}, u32[]{:S(2)}) collective-permute-start(bf16[32,8192]{1,0:T(8,128)(2,1)S(1)} %slice.127), channel_id=1, source_target_pairs={{0,24},{8,0},{16,8},{24,16},{1,25},{9,1},{17,9},{25,17},{2,26},{10... | collective-permute-start | bytes 1572872 | tf_op jit(solution)/shard_map/ppermute | solution.py:128
  80.3 23.2 %collective-permute-start.19 = (bf16[512,8192]{1,0:T(8,128)(2,1)}, bf16[512,8192]{1,0:T(8,128)(2,1)}, u32[]{:S(2)}, u32[]{:S(2)}) collective-permute-start(bf16[512,8192]{1,0:T(8,128)(2,1)} %pad_maximum_fusion), channel_id=1, source_target_pairs={{0,1},{1,0},{2,3},{3,2},{4,5},{5,4},{6,7},{7,6},{8,9},{9,8},{10,11... | collective-permute-start | bytes 25165832 | tf_op jit(solution)/shard_map/ppermute | solution.py:169
  103.5 19.2 %copy-start.1 = (f32[16,512]{1,0:T(8,128)S(1)}, f32[16,512]{1,0:T(8,128)}, u32[]{:S(2)}) copy-start(f32[16,512]{1,0:T(8,128)} %shard_map.46) | copy-start | bytes 98308
